TPU v7x, 32 devices: a whole 2x2x4 slice. The times are simulated.
32 devices in a mesh: task: 2 (over y), row: 4 (over z), col: 4 (over x, core).
Axes of the slice: x: 2, y: 2, z: 4, core: 2. Of those that a mesh axis runs over, the one named last changes fastest.
Arguments:
- features: bfloat16 [164, 4096], P(None, ('task', 'row', 'col')), parts along dimension 1, may hold values from -6 to 6
- rung_index: int32 [4096], P(('task', 'row', 'col')), parts along dimension 0, may hold values from 0 to 3
- w_first: bfloat16 [164, 512], replicated, may hold values from -0.5 to 0.5
- b_first: float32 [512], replicated, may hold values from -4 to 4
- w_second: bfloat16 [512, 512], replicated, may hold values from -0.25 to 0.25
- b_second: float32 [512], replicated, may hold values from -4 to 4
- w_third: bfloat16 [512, 64], replicated, may hold values from -0.25 to 0.25
- targets: float32 [16, 4096], P(None, ('task', 'row', 'col')), parts along dimension 1, may hold values from -80 to 80
- fidelity_factor: float32 [8, 4], P('task'), parts along dimension 0, may hold values from -4 to 4
- inverse_scale: float32 [2], P('task'), parts along dimension 0, may hold values from 0.02 to 0.1
- noise_var: float32 [2], P('task'), parts along dimension 0, may hold values from 0.3 to 1
Outputs:
- solution: float32 [16, 4096], P(None, ('task', 'row', 'col')), parts along dimension 1
- residual: float32 [16, 4096], P(None, ('task', 'row', 'col')), parts along dimension 1
There are 2 independent parts, one for each index of `task`. A program takes and returns all parts, laid end to end along the dimension named above; an argument that names none is the same for every part. Nothing has to cross between parts.
All inputs are finite; a program needn't handle non-finite values.
Results may differ from a plain program's by a relative error of at most 0.012.
The roundings to bfloat16 on the way count: a program that leaves them out, or rounds other values in their place, can miss the bound.
Values may be sent and summed in bfloat16 or wider, within the bound.
No kernel may reach another device: no remote copies, remote signals or barrier semaphores. Data moves between devices by JAX's collectives and lax.ppermute only.
A program may use at most 64 MiB of HBM per device.

v0:
```python
import jax
import jax.numpy as jnp
from jax import lax
from jax.sharding import PartitionSpec as P

ITERS = 2


def fidelity_matrix(fidelity_factor):
    lower = jnp.tril(fidelity_factor)
    return jnp.dot(lower, lower.T, precision=lax.Precision.HIGHEST) + 0.5 * jnp.eye(
        fidelity_factor.shape[0], dtype=jnp.float32
    )


def left_product(weights, values):
    return lax.dot_general(
        weights, values, (((0,), (0,)), ((), ())), preferred_element_type=jnp.float32
    )


def outer_gram(left_side, right_side):
    return lax.dot_general(
        left_side, right_side, (((1,), (1,)), ((), ())), precision=lax.Precision.HIGHEST
    )


def solve_spd(matrix, right_side):
    return jax.scipy.linalg.cho_solve((jnp.linalg.cholesky(matrix), True), right_side)


def block_size(total_count, largest):
    chosen = min(total_count, largest)
    while total_count % chosen != 0:
        chosen = chosen - 1
    return chosen


def one_hot_rows(rung_value, count_rungs):
    levels = jnp.arange(count_rungs, dtype=jnp.float32)
    return (rung_value.astype(jnp.float32)[:, None] == levels[None, :]).astype(jnp.float32)


def kernel_rows(
    row_embedding,
    row_squares,
    row_onehot,
    col_embedding,
    col_rung,
    direction,
    fidelity,
    inverse_scale,
):
    count_rows = row_embedding.shape[1]
    count_cols = col_embedding.shape[1]
    row_block = block_size(count_rows, 512)
    col_block = block_size(count_cols, 2048)
    col_squares = jnp.sum(jnp.square(col_embedding.astype(jnp.float32)), axis=0)
    col_fidelity = jnp.dot(
        fidelity, one_hot_rows(col_rung, fidelity.shape[0]).T, precision=lax.Precision.HIGHEST
    )

    def one_row_block(block_number):
        first_row = block_number * row_block
        rows_embedding = lax.dynamic_slice_in_dim(row_embedding, first_row, row_block, 1)
        rows_squares = lax.dynamic_slice_in_dim(row_squares, first_row, row_block, 0)
        rows_onehot = lax.dynamic_slice_in_dim(row_onehot, first_row, row_block, 0)

        def one_col_block(running, column_number):
            first_col = column_number * col_block
            cols_embedding = lax.dynamic_slice_in_dim(col_embedding, first_col, col_block, 1)
            cols_squares = lax.dynamic_slice_in_dim(col_squares, first_col, col_block, 0)
            cols_fidelity = lax.dynamic_slice_in_dim(col_fidelity, first_col, col_block, 1)
            cols_direction = lax.dynamic_slice_in_dim(direction, first_col, col_block, 1)
            inner = left_product(rows_embedding, cols_embedding)
            distance = rows_squares[:, None] + cols_squares[None, :] - 2.0 * inner
            tile_fidelity = jnp.dot(rows_onehot, cols_fidelity, precision=lax.Precision.HIGHEST)
            kernel = jnp.exp(-inverse_scale[0] * distance) * tile_fidelity
            contribution = lax.dot_general(
                cols_direction, kernel, (((1,), (1,)), ((), ())), precision=lax.Precision.HIGHEST
            )
            return (running + contribution, None)

        start_value = jnp.zeros((direction.shape[0], row_block), jnp.float32)
        result, unused = lax.scan(
            one_col_block, start_value, jnp.arange(count_cols // col_block, dtype=jnp.int32)
        )
        return result

    stacked = lax.map(one_row_block, jnp.arange(count_rows // row_block, dtype=jnp.int32))
    return jnp.transpose(stacked, (1, 0, 2)).reshape(direction.shape[0], count_rows)


def on_device(
    features,
    rung_index,
    w_first,
    b_first,
    w_second,
    b_second,
    w_third,
    targets,
    fidelity_factor,
    inverse_scale,
    noise_var,
):
    fidelity = fidelity_matrix(fidelity_factor)
    hidden_one = jax.nn.silu(left_product(w_first, features) + b_first[:, None]).astype(
        jnp.bfloat16
    )
    hidden_two = jax.nn.silu(left_product(w_second, hidden_one) + b_second[:, None]).astype(
        jnp.bfloat16
    )
    embedding = left_product(w_third, hidden_two).astype(jnp.bfloat16)
    rung_value = rung_index.astype(jnp.float32).astype(jnp.bfloat16)
    row_embedding, row_rung = (
        lax.all_gather(embedding, "col", axis=1, tiled=True),
        lax.all_gather(rung_value, "col", axis=0, tiled=True),
    )
    col_embedding, col_rung = (
        lax.all_gather(embedding, "row", axis=1, tiled=True),
        lax.all_gather(rung_value, "row", axis=0, tiled=True),
    )
    row_squares = jnp.sum(jnp.square(row_embedding.astype(jnp.float32)), axis=0)
    row_onehot = one_hot_rows(row_rung, fidelity.shape[0])
    solution = jnp.zeros_like(targets)
    residual = targets
    direction = targets
    gram = lax.psum(outer_gram(residual, residual), ("row", "col"))
    for iteration in range(ITERS):
        partial_value = kernel_rows(
            row_embedding,
            row_squares,
            row_onehot,
            col_embedding,
            col_rung,
            lax.all_gather(direction, "row", axis=1, tiled=True),
            fidelity,
            inverse_scale,
        )
        image = (
            lax.psum_scatter(partial_value, "col", scatter_dimension=1, tiled=True)
            + noise_var[0] * direction
        )
        curvature = lax.psum(outer_gram(direction, image), ("row", "col"))
        step_matrix = solve_spd(curvature, gram)
        solution = solution + jnp.dot(step_matrix.T, direction, precision=lax.Precision.HIGHEST)
        residual = residual - jnp.dot(step_matrix.T, image, precision=lax.Precision.HIGHEST)
        if iteration + 1 < ITERS:
            new_gram = lax.psum(outer_gram(residual, residual), ("row", "col"))
        if iteration + 1 < ITERS:
            update_matrix = solve_spd(gram, new_gram)
            direction = residual + jnp.dot(
                update_matrix.T, direction, precision=lax.Precision.HIGHEST
            )
            gram = new_gram
    return (solution, residual)


def solution(mesh):
    placed = (
        P(None, ("task", "row", "col")),
        P(("task", "row", "col")),
        P(),
        P(),
        P(),
        P(),
        P(),
        P(None, ("task", "row", "col")),
        P("task", None),
        P("task"),
        P("task"),
    )
    return jax.shard_map(
        on_device,
        mesh=mesh,
        in_specs=placed,
        out_specs=(P(None, ("task", "row", "col")), P(None, ("task", "row", "col"))),
        check_vma=False,
    )
```

profile of v0, /device:TPU:0, one launch (start us, length us, event | category | flops | bytes accessed | tf_op | source)
XLA Modules:
  0.0 256.6 jit_solution(4763473048253713967)
XLA Ops:
  7.2 1.3 multiply_convert_fusion.1
  9.1 13.7 %all_gather.19 = bf16[64,512]{1,0:T(8,128)(2,1)S(1)} all-gather(bf16[64,128]{1,0:T(8,128)(2,1)S(1)} %fusion.4), channel_id=1, replica_groups=mesh['task'=2,'row'=4,'col'=4] {'row'}, dimensions={1}, use_global_device_ids=true | all-gather | bytes 81920 | tf_op jit(solution)/shard_map/all_gather | solution.py:121
  22.8 5.4 %all_gather.18 = bf16[64,512]{1,0:T(8,128)(2,1)S(1)} all-gather(bf16[64,128]{1,0:T(8,128)(2,1)S(1)} %fusion.4), channel_id=1, replica_groups=mesh['task'=2,'row'=4,'col'=4] {'col'}, dimensions={1}, use_global_device_ids=true | all-gather | bytes 81920 | tf_op jit(solution)/shard_map/all_gather | solution.py:117
  28.2 9.8 %all-gather.1 = bf16[4,1,128]{2,1,0:T(2,128)(2,1)S(1)} all-gather(bf16[1,1,128]{2,1,0:T(2,128)(2,1)S(1)} %convert_bitcast_fusion), channel_id=1, replica_groups=mesh['task'=2,'row'=4,'col'=4] {'row'}, dimensions={0}, use_global_device_ids=true | all-gather | bytes 1280 | tf_op jit(solution)/shard_map/all_gather | solution.py:122
  38.0 5.0 %all-gather = bf16[4,1,128]{2,1,0:T(2,128)(2,1)S(1)} all-gather(bf16[1,1,128]{2,1,0:T(2,128)(2,1)S(1)} %convert_bitcast_fusion), channel_id=1, replica_groups=mesh['task'=2,'row'=4,'col'=4] {'col'}, dimensions={0}, use_global_device_ids=true | all-gather | bytes 1280 | tf_op jit(solution)/shard_map/all_gather | solution.py:118
  44.5 13.1 %all_gather.22 = f32[16,512]{1,0:T(8,128)S(1)} all-gather(f32[16,128]{1,0:T(8,128)S(1)} %copy-done.1), channel_id=1, replica_groups=mesh['task'=2,'row'=4,'col'=4] {'row'}, dimensions={1}, use_global_device_ids=true | all-gather | bytes 40960 | tf_op jit(solution)/shard_map/all_gather | solution.py:137
  59.0 1.6 convolution_bitcast_fusion
  61.5 17.0 %reduce-scatter.3.cloned.1.call-done = f32[16,128]{1,0:T(8,128)} async-done(((f32[16,512]{1,0:T(8,128)}), f32[16,128]{1,0:T(8,128)}) %reduce-scatter.3.cloned.1.call-update) | async-done | bytes 8208 | tf_op jit(solution)/shard_map/reduce_scatter | solution.py:142
  78.5 0.8 convolution_bitcast_fusion.1
  79.3 59.7 %all-reduce = (f32[16,16]{0,1:T(8,128)S(1)}, f32[16,16]{0,1:T(8,128)S(1)}) all-reduce(f32[16,16]{0,1:T(8,128)S(1)} %fusion.37, f32[16,16]{0,1:T(8,128)S(1)} %convolution_bitcast_fusion.1), channel_id=1, replica_groups=mesh['task'=2,'row'=4,'col'=4] {'row','col'}, use_global_device_ids=true, to_apply=%region_6.8 | all-reduce | flops 512 | bytes 4096 | tf_op jit(solution)/shard_map/psum | solution.py:129
  139.2 1.5 cholesky.70
  142.0 1.2 custom-call.10
  143.2 1.5 cholesky.59
  146.0 1.2 custom-call.9
  148.5 30.0 %psum.30 = f32[16,16]{1,0:T(8,128)S(1)} all-reduce(f32[16,16]{1,0:T(8,128)S(1)} %fusion.39), channel_id=1, replica_groups=mesh['task'=2,'row'=4,'col'=4] {'row','col'}, use_global_device_ids=true, to_apply=%region_7.10 | all-reduce | flops 256 | bytes 2048 | tf_op jit(solution)/shard_map/psum | solution.py:150
  179.0 13.1 %all_gather.23 = f32[16,512]{1,0:T(8,128)S(1)} all-gather(f32[16,128]{1,0:T(8,128)S(1)} %convolution_add_fusion.3), channel_id=1, replica_groups=mesh['task'=2,'row'=4,'col'=4] {'row'}, dimensions={1}, use_global_device_ids=true | all-gather | bytes 40960 | tf_op jit(solution)/shard_map/all_gather | solution.py:137
  192.1 1.6 fusion.40
  193.9 16.7 %reduce-scatter.5.cloned.1.call-done = f32[16,128]{1,0:T(8,128)} async-done(((f32[16,512]{1,0:T(8,128)}), f32[16,128]{1,0:T(8,128)}) %reduce-scatter.5.cloned.1.call-update) | async-done | bytes 8208 | tf_op jit(solution)/shard_map/reduce_scatter | solution.py:142
  210.7 0.8 fusion.28
  211.5 32.2 %psum.31 = f32[16,16]{0,1:T(8,128)S(1)} all-reduce(f32[16,16]{0,1:T(8,128)S(1)} %fusion.28), channel_id=1, replica_groups=mesh['task'=2,'row'=4,'col'=4] {'row','col'}, use_global_device_ids=true, to_apply=%region_9.12 | all-reduce | flops 256 | bytes 2048 | tf_op jit(solution)/shard_map/psum | solution.py:145
  243.8 1.5 cholesky.81
  246.6 1.2 custom-call.11
  248.1 0.8 convolution_add_fusion.2
  249.0 0.8 convolution_subtract_fusion
  (55 shorter events, 9.4 us)
Async XLA Ops:
  7.2 1.4 copy-start
  7.2 1.4 copy-start.5
  7.2 1.4 copy-start.4
  7.2 71.3 %reduce-scatter.3.cloned.1.call-start = ((), (), s32[]{:S(2)}) async-start(), calls=%async_computation.2 | async-start | bytes 40960 | tf_op jit(solution)/shard_map/reduce_scatter | solution.py:142
  22.8 5.4 %copy-start.7 = (s32[128]{0:T(128)S(1)}, s32[128]{0:T(128)}, u32[]{:S(2)}) copy-start(s32[128]{0:T(128)} %param.15) | copy-start | bytes 1540
  43.1 0.7 copy-start.6
  43.8 0.7 copy-start.1
  60.6 150.1 %reduce-scatter.5.cloned.1.call-start = ((), (), s32[]{:S(2)}) async-start(), calls=%async_computation.3 | async-start | bytes 40960 | tf_op jit(solution)/shard_map/reduce_scatter | solution.py:142
  147.4 0.7 copy-start.2
  248.1 0.8 copy-start.3
Sparse Core Ops, SparseCore 0:
  60.7 17.7 reduce-scatter.2
  193.9 16.7 reduce-scatter.4
where the time goes:
time: 257 us
  blocking collectives  182 us (71%)
  waiting for transfers between devices  33.8 us (13%)
  between operations  15.5 us (6%)
  other arithmetic  12.1 us (5%)
  matrix products  11.6 us (5%)
    psum x1, blocking collectives, on_device(): gram = lax.psum(outer_gram(residual, residual), ('row', 'col'))  59.7 us
    reduce_scatter x2, waiting for transfers between devices, on_device(): lax.psum_scatter(partial_value, 'col', scatter_dimension=1, tiled=True)  33.8 us
    psum x1, blocking collectives, on_device(): curvature = lax.psum(outer_gram(direction, image), ('row', 'col'))  32.2 us
    psum x1, blocking collectives, on_device(): new_gram = lax.psum(outer_gram(residual, residual), ('row', 'col'))  30 us
    all_gather x2, blocking collectives, on_device(): lax.all_gather(direction, 'row', axis=1, tiled=True)  26.2 us
    all_gather x1, blocking collectives, on_device(): lax.all_gather(embedding, 'row', axis=1, tiled=True)  13.7 us
    all_gather x1, blocking collectives, on_device(): lax.all_gather(rung_value, 'row', axis=0, tiled=True)  9.84 us
    another operation x9, other arithmetic, solve_spd(): jnp.linalg.cholesky(matrix)  6.39 us
  transfers between devices with their start and end apart: 2, of which 2 were waited for; matrix products, arithmetic and copies ran while one was open for 0% of the time, Pallas kernels for 0%

commit v1 on v0

v1 whole, which is shorter than its diff:
```python
import jax
import jax.numpy as jnp
from jax import lax
from jax.sharding import PartitionSpec as P

ITERS = 2


def fidelity_matrix(fidelity_factor):
    lower = jnp.tril(fidelity_factor)
    return jnp.dot(lower, lower.T, precision=lax.Precision.HIGHEST) + 0.5 * jnp.eye(
        fidelity_factor.shape[0], dtype=jnp.float32
    )


def left_product(weights, values):
    return lax.dot_general(
        weights, values, (((0,), (0,)), ((), ())), preferred_element_type=jnp.float32
    )


def outer_gram(left_side, right_side):
    return lax.dot_general(
        left_side, right_side, (((1,), (1,)), ((), ())), precision=lax.Precision.HIGHEST
    )


def solve_spd(matrix, right_side):
    return jax.scipy.linalg.cho_solve((jnp.linalg.cholesky(matrix), True), right_side)


def block_size(total_count, largest):
    chosen = min(total_count, largest)
    while total_count % chosen != 0:
        chosen = chosen - 1
    return chosen


def rung_fidelity(fidelity, rung_value):
    levels = jnp.arange(fidelity.shape[0], dtype=jnp.float32)
    onehot = (rung_value.astype(jnp.float32)[None, :] == levels[:, None]).astype(jnp.float32)
    return jnp.dot(fidelity, onehot, precision=lax.Precision.HIGHEST)


def kernel_image(embedding, squares, rung_value, col_fidelity, inverse_scale, direction):
    count = embedding.shape[1]
    row_block = block_size(count, 2048)
    col_block = block_size(count, 2048)
    levels = jnp.arange(col_fidelity.shape[0], dtype=jnp.float32)

    def one_row_block(block_number):
        first_row = block_number * row_block
        rows_embedding = lax.dynamic_slice_in_dim(embedding, first_row, row_block, 1)
        rows_squares = lax.dynamic_slice_in_dim(squares, first_row, row_block, 0)
        rows_rung = lax.dynamic_slice_in_dim(rung_value, first_row, row_block, 0)
        rows_match = rows_rung.astype(jnp.float32)[:, None] == levels[None, :]

        def one_col_block(running, column_number):
            first_col = column_number * col_block
            cols_embedding = lax.dynamic_slice_in_dim(embedding, first_col, col_block, 1)
            cols_squares = lax.dynamic_slice_in_dim(squares, first_col, col_block, 0)
            cols_fidelity = lax.dynamic_slice_in_dim(col_fidelity, first_col, col_block, 1)
            cols_direction = lax.dynamic_slice_in_dim(direction, first_col, col_block, 1)
            inner = left_product(rows_embedding, cols_embedding)
            distance = rows_squares[:, None] + cols_squares[None, :] - 2.0 * inner
            tile_fidelity = cols_fidelity[0][None, :]
            for level in range(1, col_fidelity.shape[0]):
                tile_fidelity = jnp.where(
                    rows_match[:, level : level + 1], cols_fidelity[level][None, :], tile_fidelity
                )
            kernel = jnp.exp(-inverse_scale[0] * distance) * tile_fidelity
            contribution = lax.dot_general(
                cols_direction, kernel, (((1,), (1,)), ((), ())), precision=lax.Precision.HIGHEST
            )
            return (running + contribution, None)

        start_value = jnp.zeros((direction.shape[0], row_block), jnp.float32)
        result, unused = lax.scan(
            one_col_block, start_value, jnp.arange(count // col_block, dtype=jnp.int32)
        )
        return result

    stacked = lax.map(one_row_block, jnp.arange(count // row_block, dtype=jnp.int32))
    return jnp.transpose(stacked, (1, 0, 2)).reshape(direction.shape[0], count)


def on_device(
    features,
    rung_index,
    w_first,
    b_first,
    w_second,
    b_second,
    w_third,
    targets,
    fidelity_factor,
    inverse_scale,
    noise_var,
):
    fidelity = fidelity_matrix(fidelity_factor)
    hidden_one = jax.nn.silu(left_product(w_first, features) + b_first[:, None]).astype(
        jnp.bfloat16
    )
    hidden_two = jax.nn.silu(left_product(w_second, hidden_one) + b_second[:, None]).astype(
        jnp.bfloat16
    )
    embedding = left_product(w_third, hidden_two).astype(jnp.bfloat16)
    rung_value = rung_index.astype(jnp.float32).astype(jnp.bfloat16)
    own_count = targets.shape[1]
    own_first = (lax.axis_index("row") * lax.axis_size("col") + lax.axis_index("col")) * own_count

    all_embedding = lax.all_gather(embedding, ("row", "col"), axis=1, tiled=True)
    all_rung = lax.all_gather(rung_value, ("row", "col"), axis=0, tiled=True)
    all_targets = lax.all_gather(targets, ("row", "col"), axis=1, tiled=True)

    squares = jnp.sum(jnp.square(all_embedding.astype(jnp.float32)), axis=0)
    col_fidelity = rung_fidelity(fidelity, all_rung)

    solution = jnp.zeros_like(all_targets)
    residual = all_targets
    direction = all_targets
    gram = outer_gram(residual, residual)
    for iteration in range(ITERS):
        image = (
            kernel_image(all_embedding, squares, all_rung, col_fidelity, inverse_scale, direction)
            + noise_var[0] * direction
        )
        curvature = outer_gram(direction, image)
        step_matrix = solve_spd(curvature, gram)
        solution = solution + jnp.dot(step_matrix.T, direction, precision=lax.Precision.HIGHEST)
        residual = residual - jnp.dot(step_matrix.T, image, precision=lax.Precision.HIGHEST)
        if iteration + 1 < ITERS:
            new_gram = outer_gram(residual, residual)
            update_matrix = solve_spd(gram, new_gram)
            direction = residual + jnp.dot(
                update_matrix.T, direction, precision=lax.Precision.HIGHEST
            )
            gram = new_gram
    own_solution = lax.dynamic_slice_in_dim(solution, own_first, own_count, 1)
    own_residual = lax.dynamic_slice_in_dim(residual, own_first, own_count, 1)
    return (own_solution, own_residual)


def solution(mesh):
    placed = (
        P(None, ("task", "row", "col")),
        P(("task", "row", "col")),
        P(),
        P(),
        P(),
        P(),
        P(),
        P(None, ("task", "row", "col")),
        P("task", None),
        P("task"),
        P("task"),
    )
    return jax.shard_map(
        on_device,
        mesh=mesh,
        in_specs=placed,
        out_specs=(P(None, ("task", "row", "col")), P(None, ("task", "row", "col"))),
        check_vma=False,
    )
```

time: 257 us -> 122 us (0.47)
  blocking collectives: 182 us -> 60.5 us
  waiting for transfers between devices: 33.8 us -> 0 us
  matrix products: 11.6 us -> 45.3 us
  between operations: 15.5 us -> 2.14 us
    psum x3 -> x0, blocking collectives: 122 us -> none  [the longest x1 59.7 us: on_device(): gram = lax.psum(outer_gram(residual, residual), ('row', 'col'))]
    reduce_scatter x2 -> x0, waiting for transfers between devices: 33.8 us -> none  [on_device(): lax.psum_scatter(partial_value, 'col', scatter_dimension=1, tiled=True)]
    dot_general x2, matrix products: 3.18 us -> 31.2 us  [one_col_block(): lax.dot_general(cols_direction, kernel, (((1,), (1,)), ((), ())), precisi...]
    dot_general x3, matrix products: 2.22 us -> 9.19 us  [left_product(): lax.dot_general(weights, values, (((0,), (0,)), ((), ())), preferred_elem...]
    all_gather x6 -> x3, blocking collectives: 60.2 us -> 60.5 us  [the longest x1 23.1 us: on_device(): all_rung = lax.all_gather(rung_value, ('row', 'col'), axis=0, tiled=True)]
  transfers between devices with their start and end apart: 2 -> 0, of which waited for: 2 -> 0; matrix products, arithmetic and copies ran while one was open for 0% -> 0% of each run, Pallas kernels for 0% -> 0%
where the time goes in v1:
time: 122 us
  blocking collectives  60.5 us (50%)
  matrix products  45.3 us (37%)
  other arithmetic  13.7 us (11%)
  between operations  2.14 us (2%)
    dot_general x2, matrix products, one_col_block(): lax.dot_general(cols_direction, kernel, (((1,), (1,)), ((), ())), precisi...  31.2 us
    all_gather x1, blocking collectives, on_device(): all_rung = lax.all_gather(rung_value, ('row', 'col'), axis=0, tiled=True)  23.1 us
    all_gather x1, blocking collectives, on_device(): all_targets = lax.all_gather(targets, ('row', 'col'), axis=1, tiled=True)  19.3 us
    all_gather x1, blocking collectives, on_device(): lax.all_gather(embedding, ('row', 'col'), axis=1, tiled=True)  18.2 us
    dot_general x3, matrix products, left_product(): lax.dot_general(weights, values, (((0,), (0,)), ((), ())), preferred_elem...  9.19 us
    another operation x9, other arithmetic, solve_spd(): jnp.linalg.cholesky(matrix)  6.57 us
    another operation x6, other arithmetic, solve_spd(): jax.scipy.linalg.cho_solve((jnp.linalg.cholesky(matrix), True), right_side)  5.63 us

profile of v1, /device:TPU:0, one launch (start us, length us, event | category | flops | bytes accessed | tf_op | source)
XLA Modules:
  0.0 122.0 jit_solution(9418712131245514869)
XLA Ops:
  0.6 0.7 convert_bitcast_fusion
  1.4 23.1 %all-gather = bf16[16,1,128]{2,1,0:T(2,128)(2,1)S(1)} all-gather(bf16[1,1,128]{2,1,0:T(2,128)(2,1)S(1)} %convert_bitcast_fusion), channel_id=1, replica_groups=mesh['task'=2,'row'=4,'col'=4] {'row','col'}, dimensions={0}, use_global_device_ids=true | all-gather | bytes 4352 | tf_op jit(solution)/shard_map/all_gather | solution.py:113
  24.5 0.9 convolution_add_fusion.4
  25.7 1.3 %multiply_convert_fusion.1 = bf16[512,128]{1,0:T(8,128)(2,1)S(1)} fusion(bf16[164,512]{1,0:T(8,128)(2,1)} %param.16, bf16[164,128]{1,0:T(8,128)(2,1)} %param.14, f32[512]{0:T(512)} %param.17), kind=kOutput, calls=%fused_computation.14 | convolution fusion | flops 21889024 | bytes 343040 | tf_op jit(solution)/shard_map/dot_general | solution.py:17
  26.9 1.4 %fusion.2 = bf16[64,128]{1,0:T(8,128)(2,1)S(1)} fusion(bf16[512,64]{0,1:T(8,128)(2,1)} %param.20, bf16[512,128]{1,0:T(8,128)(2,1)S(1)} %multiply_convert_fusion.1, bf16[512,512]{1,0:T(8,128)(2,1)S(1)} %copy-done, f32[512]{0:T(512)} %param.19), kind=kOutput, calls=%fused_computation.10 | convolution fusion | flops 75898880 | bytes 739328 | tf_op jit(solution)/shard_map/dot_general | solution.py:17
  28.3 18.2 %all_gather.9 = bf16[64,2048]{1,0:T(8,128)(2,1)S(1)} all-gather(bf16[64,128]{1,0:T(8,128)(2,1)S(1)} %fusion.2), channel_id=1, replica_groups=mesh['task'=2,'row'=4,'col'=4] {'row','col'}, dimensions={1}, use_global_device_ids=true | all-gather | bytes 278528 | tf_op jit(solution)/shard_map/all_gather | solution.py:112
  47.2 6.6 %select_multiply_fusion = f32[2048,2048]{1,0:T(8,128)S(1)} fusion(bf16[64,2048]{1,0:T(8,128)(2,1)S(1)} %all_gather.9, f32[2048]{0:T(1024)S(1)} %bitcast.95, f32[2048]{0:T(1024)S(1)} %bitcast.96, f32[2048]{0:T(1024)S(1)} %bitcast.97, f32[2048]{0:T(1024)S(1)} %bitcast.94, f32[2048]{0:T(1024)S(1)} %multiply_reduce_fusion, f32[]{:T(128)} %bitcast, ...), kind=kOutput, calls=%fused_computation | convolution fusion | flops 570425344 | bytes 17086468 | tf_op jit(solution)/shard_map/while/body/eval_jaxpr/while/body/eval_jaxpr/dot_general | solution.py:17
  53.8 19.3 %all_gather.11 = f32[16,2048]{1,0:T(8,128)S(1)} all-gather(f32[16,128]{1,0:T(8,128)S(1)} %copy-done.2), channel_id=1, replica_groups=mesh['task'=2,'row'=4,'col'=4] {'row','col'}, dimensions={1}, use_global_device_ids=true | all-gather | bytes 139264 | tf_op jit(solution)/shard_map/all_gather | solution.py:114
  73.8 14.1 %fusion = f32[16,2048]{1,0:T(8,128)S(1)} fusion(f32[2048,2048]{1,0:T(8,128)S(1)} %select_multiply_fusion, f32[16,2048]{1,0:T(8,128)S(1)} %all_gather.11, f32[]{:T(128)} %bitcast.89), kind=kOutput, calls=%fused_computation.5 | convolution fusion | flops 805371904 | bytes 17039364 | tf_op jit(solution)/shard_map/while/body/eval_jaxpr/while/body/eval_jaxpr/dot_general | solution.py:72
  88.2 1.5 %cholesky.59 = f32[16,16]{1,0:T(8,128)S(1)} custom-call(f32[16,16]{1,0:T(8,128)S(1)} %add_multiply_fusion), custom_call_target="Cholesky" | custom-call | tf_op jit(solution)/shard_map/jit(cholesky)/cholesky | solution.py:29
  89.8 0.6 compare_reduce_fusion.2
  90.4 0.6 fusion.7
  91.1 1.2 %custom-call.9 = f32[1,16,16]{1,2,0:T(8,128)S(1)} custom-call(f32[1,16,16]{2,1,0:T(8,128)S(1)} %fusion.7), custom_call_target="InvertDiagBlocksLowerTriangular" | custom-call | tf_op jit(solution)/shard_map/jit(_cho_solve)/triangular_solve | solution.py:29
  93.3 0.4 fusion.32
  93.8 1.5 %cholesky.70 = f32[16,16]{1,0:T(8,128)S(1)} custom-call(f32[16,16]{1,0:T(8,128)S(1)} %fusion.19), custom_call_target="Cholesky" | custom-call | tf_op jit(solution)/shard_map/jit(cholesky)/cholesky | solution.py:29
  95.4 0.6 compare_reduce_fusion.1
  96.0 0.6 fusion.8
  96.7 1.2 %custom-call.10 = f32[1,16,16]{1,2,0:T(8,128)S(1)} custom-call(f32[1,16,16]{2,1,0:T(8,128)S(1)} %fusion.8), custom_call_target="InvertDiagBlocksLowerTriangular" | custom-call | tf_op jit(solution)/shard_map/jit(_cho_solve)/triangular_solve | solution.py:29
  98.6 17.1 %convolution_add_fusion.1 = f32[16,2048]{1,0:T(8,128)S(1)} fusion(f32[16,2048]{1,0:T(8,128)S(1)} %convolution_add_fusion, f32[2048,2048]{1,0:T(8,128)} %copy-done.1, f32[]{:T(128)} %bitcast.90), kind=kOutput, calls=%fused_computation.3 | convolution fusion | flops 805371904 | bytes 17039364 | tf_op jit(solution)/shard_map/while/body/eval_jaxpr/while/body/eval_jaxpr/dot_general | solution.py:72
  116.0 1.5 %cholesky.81 = f32[16,16]{1,0:T(8,128)S(1)} custom-call(f32[16,16]{1,0:T(8,128)S(1)} %fusion.14), custom_call_target="Cholesky" | custom-call | tf_op jit(solution)/shard_map/jit(cholesky)/cholesky | solution.py:29
  117.5 0.6 compare_reduce_fusion
  118.2 0.6 fusion.9
  118.9 1.2 %custom-call.11 = f32[1,16,16]{1,2,0:T(8,128)S(1)} custom-call(f32[1,16,16]{2,1,0:T(8,128)S(1)} %fusion.9), custom_call_target="InvertDiagBlocksLowerTriangular" | custom-call | tf_op jit(solution)/shard_map/jit(_cho_solve)/triangular_solve | solution.py:29
  121.4 0.6 dynamic-slice_subtract_fusion
  (35 shorter events, 4.2 us)
Async XLA Ops:
  0.6 26.3 %copy-start = (bf16[512,512]{1,0:T(8,128)(2,1)S(1)}, bf16[512,512]{1,0:T(8,128)(2,1)}, u32[]{:S(2)}) copy-start(bf16[512,512]{1,0:T(8,128)(2,1)} %param.18) | copy-start | bytes 1572868
  47.2 6.6 %copy-start.2 = (f32[16,128]{1,0:T(8,128)S(1)}, f32[16,128]{1,0:T(8,128)}, u32[]{:S(2)}) copy-start(f32[16,128]{1,0:T(8,128)} %param.21) | copy-start | bytes 24580
  53.8 20.0 %copy-start.1 = (f32[2048,2048]{1,0:T(8,128)}, f32[2048,2048]{1,0:T(8,128)S(1)}, u32[]{:S(2)}) copy-start(f32[2048,2048]{1,0:T(8,128)S(1)} %select_multiply_fusion) | copy-start | bytes 50331652

commit v2 on v1

--- a/solution.py
+++ b/solution.py
@@ -70,7 +70,7 @@
                 )
             kernel = jnp.exp(-inverse_scale[0] * distance) * tile_fidelity
             contribution = lax.dot_general(
-                cols_direction, kernel, (((1,), (1,)), ((), ())), precision=lax.Precision.HIGHEST
+                cols_direction, kernel, (((1,), (1,)), ((), ())), precision=lax.Precision.HIGH
             )
             return (running + contribution, None)
 
@@ -109,9 +109,14 @@
     own_count = targets.shape[1]
     own_first = (lax.axis_index("row") * lax.axis_size("col") + lax.axis_index("col")) * own_count
 
-    all_embedding = lax.all_gather(embedding, ("row", "col"), axis=1, tiled=True)
-    all_rung = lax.all_gather(rung_value, ("row", "col"), axis=0, tiled=True)
-    all_targets = lax.all_gather(targets, ("row", "col"), axis=1, tiled=True)
+    emb_rows = embedding.shape[0]
+    packed = jnp.concatenate(
+        [embedding.astype(jnp.float32), targets, rung_value.astype(jnp.float32)[None, :]], axis=0
+    )
+    gathered = lax.all_gather(packed, ("row", "col"), axis=1, tiled=True)
+    all_embedding = gathered[:emb_rows].astype(jnp.bfloat16)
+    all_targets = gathered[emb_rows : emb_rows + targets.shape[0]]
+    all_rung = gathered[emb_rows + targets.shape[0]]
 
     squares = jnp.sum(jnp.square(all_embedding.astype(jnp.float32)), axis=0)
     col_fidelity = rung_fidelity(fidelity, all_rung)

time: 122 us -> 79 us (0.65)
  blocking collectives: 60.5 us -> 25.3 us
  matrix products: 45.3 us -> 31.6 us
  local copies, waits for them, and re-layouts: 0.37 us -> 5.42 us
    all_gather x3 -> x1, blocking collectives: 60.5 us -> 25.3 us  [on_device(): gathered = lax.all_gather(packed, ('row', 'col'), axis=1, tiled=True)]
    dot_general x2, matrix products: 31.2 us -> 17.5 us  [one_col_block(): lax.dot_general(cols_direction, kernel, (((1,), (1,)), ((), ())), precisi...]
    unnamed x6 -> x4, local copies, waits for them, and re-layouts: 0.02 us -> 5.07 us
where the time goes in v2:
time: 79 us; the launch traced here: 78.7 us
  matrix products  31.6 us (40%)
  blocking collectives  25.3 us (32%)
  other arithmetic  14.3 us (18%)
  local copies, waits for them, and re-layouts  5.42 us (7%)
  between operations  2.1 us (3%)
    all_gather x1, blocking collectives, on_device(): gathered = lax.all_gather(packed, ('row', 'col'), axis=1, tiled=True)  25.3 us
    dot_general x2, matrix products, one_col_block(): lax.dot_general(cols_direction, kernel, (((1,), (1,)), ((), ())), precisi...  17.5 us
    dot_general x3, matrix products, left_product(): lax.dot_general(weights, values, (((0,), (0,)), ((), ())), preferred_elem...  9.48 us
    another operation x9, other arithmetic, solve_spd(): jnp.linalg.cholesky(matrix)  6.57 us
    another operation x6, other arithmetic, solve_spd(): jax.scipy.linalg.cho_solve((jnp.linalg.cholesky(matrix), True), right_side)  5.63 us
    unnamed x4, local copies, waits for them, and re-layouts  5.07 us

profile of v2, /device:TPU:0, one launch (start us, length us, event | category | flops | bytes accessed | tf_op | source)
XLA Modules:
  0.0 78.7 jit_solution(6913795889890176275)
XLA Ops:
  0.6 1.3 %multiply_convert_fusion.1 = bf16[512,128]{1,0:T(8,128)(2,1)S(1)} fusion(bf16[164,512]{1,0:T(8,128)(2,1)} %param.16, bf16[164,128]{1,0:T(8,128)(2,1)} %param.14, f32[512]{0:T(512)} %param.17), kind=kOutput, calls=%fused_computation.15 | convolution fusion | flops 21889024 | bytes 343040 | tf_op jit(solution)/shard_map/dot_general | solution.py:17
  2.0 1.3 %fusion.2 = f32[64,128]{1,0:T(8,128)S(1)} fusion(bf16[512,64]{0,1:T(8,128)(2,1)} %param.20, bf16[512,128]{1,0:T(8,128)(2,1)S(1)} %multiply_convert_fusion.1, bf16[512,512]{1,0:T(8,128)(2,1)S(1)} %copy-done, f32[512]{0:T(512)} %param.19), kind=kOutput, calls=%fused_computation.10 | convolution fusion | flops 75907072 | bytes 755712 | tf_op jit(solution)/shard_map/dot_general | solution.py:17
  3.3 0.7 bitcast_convert_fusion
  4.0 0.7 pad_maximum_fusion
  4.7 25.3 %all_gather.3 = f32[81,2048]{1,0:T(8,128)S(1)} all-gather(f32[81,128]{1,0:T(8,128)S(1)} %pad_maximum_fusion), channel_id=1, replica_groups=mesh['task'=2,'row'=4,'col'=4] {'row','col'}, dimensions={1}, use_global_device_ids=true | all-gather | bytes 705024 | tf_op jit(solution)/shard_map/all_gather | solution.py:116
  29.9 0.9 %convolution_add_fusion.5 = f32[4,4]{1,0:T(4,128)S(1)} fusion(f32[4,4]{1,0:T(4,128)} %param.22), kind=kOutput, calls=%fused_computation.11 | convolution fusion | flops 848 | bytes 128 | tf_op jit(solution)/shard_map/dot_general | solution.py:11
  31.9 6.8 %select_multiply_fusion = f32[2048,2048]{1,0:T(8,128)S(1)} fusion(f32[2048]{0:T(1024)S(1)} %bitcast.84, f32[2048]{0:T(1024)S(1)} %bitcast.85, f32[2048]{0:T(1024)S(1)} %bitcast.86, f32[2048]{0:T(1024)S(1)} %bitcast.83, f32[2048]{0:T(1024)S(1)} %multiply_reduce_fusion, f32[]{:T(128)} %bitcast.3, pred[2048]{0:T(1024)(128)(4,1)S(1)} %get-tuple-element.111, ...), kind=kOutput, calls=%fused_computation | convolution fusion | flops 570425344 | bytes 17094660 | tf_op jit(solution)/shard_map/while/body/eval_jaxpr/while/body/eval_jaxpr/dot_general | solution.py:17
  39.3 5.1 %copy-done.1 = f32[2048,2048]{1,0:T(8,128)} copy-done((f32[2048,2048]{1,0:T(8,128)}, f32[2048,2048]{1,0:T(8,128)S(1)}, u32[]{:S(2)}) %copy-start.1) | copy-done | bytes 16777240
  44.4 7.3 %convolution_add_fusion.2 = f32[16,2048]{1,0:T(8,128)S(1)} fusion(f32[2048,2048]{1,0:T(8,128)S(1)} %select_multiply_fusion, f32[81,2048]{1,0:T(8,128)S(1)} %all_gather.3, f32[]{:T(128)} %bitcast.79), kind=kOutput, calls=%fused_computation.4 | convolution fusion | flops 402718720 | bytes 17170436 | tf_op jit(solution)/shard_map/while/body/eval_jaxpr/while/body/eval_jaxpr/dot_general | solution.py:72
  52.1 1.5 %cholesky.59 = f32[16,16]{1,0:T(8,128)S(1)} custom-call(f32[16,16]{1,0:T(8,128)S(1)} %fusion.32), custom_call_target="Cholesky" | custom-call | tf_op jit(solution)/shard_map/jit(cholesky)/cholesky | solution.py:29
  53.6 0.6 compare_reduce_fusion.2
  54.3 0.6 fusion.15
  54.9 1.2 %custom-call.9 = f32[1,16,16]{1,2,0:T(8,128)S(1)} custom-call(f32[1,16,16]{2,1,0:T(8,128)S(1)} %fusion.15), custom_call_target="InvertDiagBlocksLowerTriangular" | custom-call | tf_op jit(solution)/shard_map/jit(_cho_solve)/triangular_solve | solution.py:29
  57.8 1.5 %cholesky.70 = f32[16,16]{1,0:T(8,128)S(1)} custom-call(f32[16,16]{1,0:T(8,128)S(1)} %fusion.27), custom_call_target="Cholesky" | custom-call | tf_op jit(solution)/shard_map/jit(cholesky)/cholesky | solution.py:29
  59.3 0.6 compare_reduce_fusion.1
  60.0 0.6 fusion.16
  60.6 1.2 %custom-call.10 = f32[1,16,16]{1,2,0:T(8,128)S(1)} custom-call(f32[1,16,16]{2,1,0:T(8,128)S(1)} %fusion.16), custom_call_target="InvertDiagBlocksLowerTriangular" | custom-call | tf_op jit(solution)/shard_map/jit(_cho_solve)/triangular_solve | solution.py:29
  62.2 0.3 convolution_add_fusion
  62.5 10.1 %convolution_add_fusion.1 = f32[16,2048]{1,0:T(8,128)S(1)} fusion(f32[16,2048]{1,0:T(8,128)S(1)} %convolution_add_fusion, f32[2048,2048]{1,0:T(8,128)} %copy-done.1, f32[]{:T(128)} %bitcast.80), kind=kOutput, calls=%fused_computation.3 | convolution fusion | flops 402718720 | bytes 17039364 | tf_op jit(solution)/shard_map/while/body/eval_jaxpr/while/body/eval_jaxpr/dot_general | solution.py:72
  73.0 1.5 %cholesky.81 = f32[16,16]{1,0:T(8,128)S(1)} custom-call(f32[16,16]{1,0:T(8,128)S(1)} %fusion.22), custom_call_target="Cholesky" | custom-call | tf_op jit(solution)/shard_map/jit(cholesky)/cholesky | solution.py:29
  74.5 0.6 compare_reduce_fusion
  75.2 0.6 fusion.17
  75.8 1.2 %custom-call.11 = f32[1,16,16]{1,2,0:T(8,128)S(1)} custom-call(f32[1,16,16]{2,1,0:T(8,128)S(1)} %fusion.17), custom_call_target="InvertDiagBlocksLowerTriangular" | custom-call | tf_op jit(solution)/shard_map/jit(_cho_solve)/triangular_solve | solution.py:29
  78.0 0.6 dynamic-slice_subtract_fusion
  (32 shorter events, 4.0 us)
Async XLA Ops:
  0.6 1.3 %copy-start = (bf16[512,512]{1,0:T(8,128)(2,1)S(1)}, bf16[512,512]{1,0:T(8,128)(2,1)}, u32[]{:S(2)}) copy-start(bf16[512,512]{1,0:T(8,128)(2,1)} %param.18) | copy-start | bytes 1572868
  38.7 5.7 %copy-start.1 = (f32[2048,2048]{1,0:T(8,128)}, f32[2048,2048]{1,0:T(8,128)S(1)}, u32[]{:S(2)}) copy-start(f32[2048,2048]{1,0:T(8,128)S(1)} %select_multiply_fusion) | copy-start | bytes 50331652

commit v3 on v2

--- a/solution.py
+++ b/solution.py
@@ -40,6 +40,41 @@
     levels = jnp.arange(fidelity.shape[0], dtype=jnp.float32)
     onehot = (rung_value.astype(jnp.float32)[None, :] == levels[:, None]).astype(jnp.float32)
     return jnp.dot(fidelity, onehot, precision=lax.Precision.HIGHEST)
+
+
+def split_three(values):
+    first = lax.reduce_precision(values, exponent_bits=8, mantissa_bits=7)
+    rest = values - first
+    second = lax.reduce_precision(rest, exponent_bits=8, mantissa_bits=7)
+    third = lax.reduce_precision(rest - second, exponent_bits=8, mantissa_bits=7)
+    return (
+        first.astype(jnp.bfloat16),
+        second.astype(jnp.bfloat16),
+        third.astype(jnp.bfloat16),
+    )
+
+
+def split_product(direction, kernel):
+    count = direction.shape[0]
+    d_one, d_two, d_three = split_three(direction)
+    k_one, k_two, k_three = split_three(kernel)
+    dims = (((1,), (1,)), ((), ()))
+    by_first = lax.dot_general(
+        jnp.concatenate([d_one, d_two, d_three], axis=0), k_one, dims,
+        preferred_element_type=jnp.float32,
+    )
+    by_second = lax.dot_general(
+        jnp.concatenate([d_one, d_two], axis=0), k_two, dims, preferred_element_type=jnp.float32
+    )
+    by_third = lax.dot_general(d_one, k_three, dims, preferred_element_type=jnp.float32)
+    return (
+        by_first[:count]
+        + by_first[count : 2 * count]
+        + by_first[2 * count :]
+        + by_second[:count]
+        + by_second[count:]
+        + by_third
+    )
 
 
 def kernel_image(embedding, squares, rung_value, col_fidelity, inverse_scale, direction):
@@ -69,9 +104,7 @@
                     rows_match[:, level : level + 1], cols_fidelity[level][None, :], tile_fidelity
                 )
             kernel = jnp.exp(-inverse_scale[0] * distance) * tile_fidelity
-            contribution = lax.dot_general(
-                cols_direction, kernel, (((1,), (1,)), ((), ())), precision=lax.Precision.HIGH
-            )
+            contribution = split_product(cols_direction, kernel)
             return (running + contribution, None)
 
         start_value = jnp.zeros((direction.shape[0], row_block), jnp.float32)

time: 79 us -> 89.9 us (1.14)
  matrix products: 31.6 us -> 46.8 us
  local copies, waits for them, and re-layouts: 5.42 us -> 0.84 us
    dot_general x2 -> x6, matrix products: 17.5 us -> 28.3 us  [the longest x2 11.7 us: split_product(): lax.dot_general(jnp.concatenate([d_one, d_two], axis=0), k_two, dims, pre...]
    unnamed x4 -> x6, local copies, waits for them, and re-layouts: 5.07 us -> 0.49 us
    dot_general x3, matrix products: 9.48 us -> 13.9 us  [left_product(): lax.dot_general(weights, values, (((0,), (0,)), ((), ())), preferred_elem...]
where the time goes in v3:
time: 89.9 us; the launch traced here: 89.6 us
  matrix products  46.8 us (52%)
  blocking collectives  25.3 us (28%)
  other arithmetic  14.4 us (16%)
  between operations  2.17 us (2%)
    all_gather x1, blocking collectives, on_device(): gathered = lax.all_gather(packed, ('row', 'col'), axis=1, tiled=True)  25.3 us
    dot_general x3, matrix products, left_product(): lax.dot_general(weights, values, (((0,), (0,)), ((), ())), preferred_elem...  13.9 us
    dot_general x2, matrix products, split_product(): lax.dot_general(jnp.concatenate([d_one, d_two], axis=0), k_two, dims, pre...  11.7 us
    dot_general x2, matrix products, split_product(): lax.dot_general(d_one, k_three, dims, preferred_element_type=jnp.float32)  11.3 us
    another operation x9, other arithmetic, solve_spd(): jnp.linalg.cholesky(matrix)  6.65 us
    another operation x6, other arithmetic, solve_spd(): jax.scipy.linalg.cho_solve((jnp.linalg.cholesky(matrix), True), right_side)  5.67 us
    dot_general x2, matrix products, split_product(): lax.dot_general(jnp.concatenate([d_one, d_two, d_three], axis=0), k_one,...  5.26 us

profile of v3, /device:TPU:0, one launch (start us, length us, event | category | flops | bytes accessed | tf_op | source)
XLA Modules:
  0.0 89.6 jit_solution(3814902832019437512)
XLA Ops:
  2.0 0.7 bitcast_convert_fusion
  2.7 0.9 convolution_add_fusion.5
  3.5 1.3 %multiply_convert_fusion.1 = bf16[512,128]{1,0:T(8,128)(2,1)S(1)} fusion(bf16[164,512]{1,0:T(8,128)(2,1)} %param.16, bf16[164,128]{1,0:T(8,128)(2,1)} %param.14, f32[512]{0:T(512)} %param.17), kind=kOutput, calls=%fused_computation.27 | convolution fusion | flops 21889024 | bytes 343040 | tf_op jit(solution)/shard_map/dot_general | solution.py:17
  4.8 1.4 %fusion.10 = f32[64,128]{1,0:T(8,128)S(1)} fusion(bf16[512,64]{0,1:T(8,128)(2,1)} %param.20, bf16[512,128]{1,0:T(8,128)(2,1)S(1)} %multiply_convert_fusion.1, bf16[512,512]{1,0:T(8,128)(2,1)S(1)} %copy-done, f32[512]{0:T(512)} %param.19), kind=kOutput, calls=%fused_computation.22 | convolution fusion | flops 75907072 | bytes 755712 | tf_op jit(solution)/shard_map/dot_general | solution.py:17
  6.2 0.7 pad_maximum_fusion
  6.9 25.3 %all_gather.3 = f32[81,2048]{1,0:T(8,128)S(1)} all-gather(f32[81,128]{1,0:T(8,128)S(1)} %pad_maximum_fusion), channel_id=1, replica_groups=mesh['task'=2,'row'=4,'col'=4] {'row','col'}, dimensions={1}, use_global_device_ids=true | all-gather | bytes 705024 | tf_op jit(solution)/shard_map/all_gather | solution.py:149
  32.4 1.5 %cholesky.70 = f32[16,16]{1,0:T(8,128)S(1)} custom-call(f32[16,16]{1,0:T(8,128)S(1)} %fusion.54), custom_call_target="Cholesky" | custom-call | tf_op jit(solution)/shard_map/jit(cholesky)/cholesky | solution.py:29
  34.0 0.7 compare_reduce_fusion.1
  34.7 0.7 fusion.43
  35.4 1.2 %custom-call.10 = f32[1,16,16]{1,2,0:T(8,128)S(1)} custom-call(f32[1,16,16]{2,1,0:T(8,128)S(1)} %fusion.43), custom_call_target="InvertDiagBlocksLowerTriangular" | custom-call | tf_op jit(solution)/shard_map/jit(_cho_solve)/triangular_solve | solution.py:29
  37.1 11.3 %fusion.1 = (bf16[2048,2048]{1,0:T(8,128)(2,1)}, f32[2048,2048]{1,0:T(8,128)S(1)}) fusion(f32[2048]{0:T(1024)S(1)} %bitcast.85, f32[2048]{0:T(1024)S(1)} %bitcast.86, pred[2048]{0:T(1024)(128)(4,1)S(1)} %get-tuple-element.111, f32[2048]{0:T(1024)S(1)} %bitcast.87, pred[2048]{0:T(1024)(128)(4,1)S(1)} %get-tuple-element.112, f32[2048]{0:T(1024)S(1)} %bitcast.84, ...), kind=kOutput, calls=%fused_computation.5 | convolution fusion | flops 595591168 | bytes 25483268 | tf_op jit(solution)/shard_map/while/body/eval_jaxpr/while/body/eval_jaxpr/dot_general | solution.py:17
  48.3 2.6 %fusion.7 = f32[32,2048]{1,0:T(8,128)S(1)} fusion(f32[2048,2048]{1,0:T(8,128)S(1)} %get-tuple-element.152, bf16[16,2048]{1,0:T(8,128)(2,1)S(1)} %get-tuple-element.114, bf16[16,2048]{1,0:T(8,128)(2,1)S(1)} %get-tuple-element.134), kind=kOutput, calls=%fused_computation.16 | convolution fusion | flops 285474816 | bytes 17170432 | tf_op jit(solution)/shard_map/while/body/eval_jaxpr/while/body/eval_jaxpr/dot_general | solution.py:66
  50.9 2.6 %fusion.3 = f32[48,2048]{1,0:T(8,128)S(1)} fusion(f32[2048,2048]{1,0:T(8,128)S(1)} %get-tuple-element.152, bf16[16,2048]{1,0:T(8,128)(2,1)S(1)} %get-tuple-element.113, bf16[16,2048]{1,0:T(8,128)(2,1)S(1)} %get-tuple-element.114, bf16[16,2048]{1,0:T(8,128)(2,1)S(1)} %get-tuple-element.134), kind=kOutput, calls=%fused_computation.8 | convolution fusion | flops 411631616 | bytes 17367040 | tf_op jit(solution)/shard_map/while/body/eval_jaxpr/while/body/eval_jaxpr/dot_general | solution.py:62
  54.0 5.7 %fusion.5 = f32[16,2048]{1,0:T(8,128)S(1)} fusion(bf16[16,2048]{1,0:T(8,128)(2,1)S(1)} %get-tuple-element.134, bf16[2048,2048]{1,0:T(8,128)(2,1)} %get-tuple-element.142, f32[32,2048]{1,0:T(8,128)S(1)} %fusion.7, f32[48,2048]{1,0:T(8,128)S(1)} %fusion.3, f32[81,2048]{1,0:T(8,128)S(1)} %all_gather.3, f32[]{:T(128)} %bitcast.80), kind=kOutput, calls=%fused_computation.14 | convolution fusion | flops 134447104 | bytes 9371652 | tf_op jit(solution)/shard_map/while/body/eval_jaxpr/while/body/eval_jaxpr/dot_general | solution.py:69
  60.0 1.5 %cholesky.59 = f32[16,16]{1,0:T(8,128)S(1)} custom-call(f32[16,16]{1,0:T(8,128)S(1)} %fusion.59), custom_call_target="Cholesky" | custom-call | tf_op jit(solution)/shard_map/jit(cholesky)/cholesky | solution.py:29
  61.6 0.6 compare_reduce_fusion.2
  62.2 0.6 fusion.42
  62.9 1.2 %custom-call.9 = f32[1,16,16]{1,2,0:T(8,128)S(1)} custom-call(f32[1,16,16]{2,1,0:T(8,128)S(1)} %fusion.42), custom_call_target="InvertDiagBlocksLowerTriangular" | custom-call | tf_op jit(solution)/shard_map/jit(_cho_solve)/triangular_solve | solution.py:29
  66.1 9.1 %fusion.6 = f32[32,2048]{1,0:T(8,128)S(1)} fusion(f32[2048,2048]{1,0:T(8,128)} %copy-done.1, bf16[16,2048]{1,0:T(8,128)(2,1)S(1)} %get-tuple-element.136, bf16[16,2048]{1,0:T(8,128)(2,1)S(1)} %get-tuple-element.137), kind=kOutput, calls=%fused_computation.15 | convolution fusion | flops 285474816 | bytes 17170432 | tf_op jit(solution)/shard_map/while/body/eval_jaxpr/while/body/eval_jaxpr/dot_general | solution.py:66
  75.2 2.6 %fusion.2 = f32[48,2048]{1,0:T(8,128)S(1)} fusion(f32[2048,2048]{1,0:T(8,128)S(1)} %copy-done.2, bf16[16,2048]{1,0:T(8,128)(2,1)S(1)} %get-tuple-element.135, bf16[16,2048]{1,0:T(8,128)(2,1)S(1)} %get-tuple-element.136, bf16[16,2048]{1,0:T(8,128)(2,1)S(1)} %get-tuple-element.137), kind=kOutput, calls=%fused_computation.7 | convolution fusion | flops 411631616 | bytes 17367040 | tf_op jit(solution)/shard_map/while/body/eval_jaxpr/while/body/eval_jaxpr/dot_general | solution.py:62
  77.9 5.7 %fusion.4 = f32[16,2048]{1,0:T(8,128)S(1)} fusion(bf16[16,2048]{1,0:T(8,128)(2,1)S(1)} %get-tuple-element.137, bf16[2048,2048]{1,0:T(8,128)(2,1)} %get-tuple-element.142, f32[32,2048]{1,0:T(8,128)S(1)} %fusion.6, f32[48,2048]{1,0:T(8,128)S(1)} %fusion.2, f32[16,2048]{1,0:T(8,128)S(1)} %get-tuple-element.153, f32[]{:T(128)} %bitcast.81), kind=kOutput, calls=%fused_computation.12 | convolution fusion | flops 134447104 | bytes 9371652 | tf_op jit(solution)/shard_map/while/body/eval_jaxpr/while/body/eval_jaxpr/dot_general | solution.py:69
  83.9 1.5 %cholesky.81 = f32[16,16]{1,0:T(8,128)S(1)} custom-call(f32[16,16]{1,0:T(8,128)S(1)} %fusion.49), custom_call_target="Cholesky" | custom-call | tf_op jit(solution)/shard_map/jit(cholesky)/cholesky | solution.py:29
  86.0 0.6 fusion.44
  86.7 1.2 %custom-call.11 = f32[1,16,16]{1,2,0:T(8,128)S(1)} custom-call(f32[1,16,16]{2,1,0:T(8,128)S(1)} %fusion.44), custom_call_target="InvertDiagBlocksLowerTriangular" | custom-call | tf_op jit(solution)/shard_map/jit(_cho_solve)/triangular_solve | solution.py:29
  (39 shorter events, 6.1 us)
Async XLA Ops:
  0.6 4.2 %copy-start = (bf16[512,512]{1,0:T(8,128)(2,1)S(1)}, bf16[512,512]{1,0:T(8,128)(2,1)}, u32[]{:S(2)}) copy-start(bf16[512,512]{1,0:T(8,128)(2,1)} %param.18) | copy-start | bytes 1572868
  48.3 5.7 %copy-start.1 = (f32[2048,2048]{1,0:T(8,128)}, f32[2048,2048]{1,0:T(8,128)S(1)}, u32[]{:S(2)}) copy-start(f32[2048,2048]{1,0:T(8,128)S(1)} %get-tuple-element.152) | copy-start | bytes 50331652
  64.1 11.1 %copy-start.2 = (f32[2048,2048]{1,0:T(8,128)S(1)}, f32[2048,2048]{1,0:T(8,128)}, u32[]{:S(2)}) copy-start(f32[2048,2048]{1,0:T(8,128)} %copy-done.1) | copy-start | bytes 50331652

commit v4 on v3

--- a/solution.py
+++ b/solution.py
@@ -104,7 +104,9 @@
                     rows_match[:, level : level + 1], cols_fidelity[level][None, :], tile_fidelity
                 )
             kernel = jnp.exp(-inverse_scale[0] * distance) * tile_fidelity
-            contribution = split_product(cols_direction, kernel)
+            contribution = lax.dot_general(
+                cols_direction, kernel, (((1,), (1,)), ((), ())), precision=lax.Precision.HIGHEST
+            )
             return (running + contribution, None)
 
         start_value = jnp.zeros((direction.shape[0], row_block), jnp.float32)

time: 89.9 us -> 93 us (1.034)
  local copies, waits for them, and re-layouts: 0.84 us -> 5.42 us
  matrix products: 46.8 us -> 45.7 us
    unnamed x6 -> x4, local copies, waits for them, and re-layouts: 0.49 us -> 5.07 us
    dot_general x3, matrix products: 13.9 us -> 9.47 us  [left_product(): lax.dot_general(weights, values, (((0,), (0,)), ((), ())), preferred_elem...]
    dot_general x6 -> x2, matrix products: 28.3 us -> 31.5 us  [one_col_block(): lax.dot_general(cols_direction, kernel, (((1,), (1,)), ((), ())), precisi...]
where the time goes in v4:
time: 93 us; the launch traced here: 92.7 us
  matrix products  45.7 us (49%)
  blocking collectives  25.3 us (27%)
  other arithmetic  14.3 us (15%)
  local copies, waits for them, and re-layouts  5.42 us (6%)
  between operations  2.09 us (2%)
    dot_general x2, matrix products, one_col_block(): lax.dot_general(cols_direction, kernel, (((1,), (1,)), ((), ())), precisi...  31.5 us
    all_gather x1, blocking collectives, on_device(): gathered = lax.all_gather(packed, ('row', 'col'), axis=1, tiled=True)  25.3 us
    dot_general x3, matrix products, left_product(): lax.dot_general(weights, values, (((0,), (0,)), ((), ())), preferred_elem...  9.47 us
    another operation x9, other arithmetic, solve_spd(): jnp.linalg.cholesky(matrix)  6.57 us
    another operation x6, other arithmetic, solve_spd(): jax.scipy.linalg.cho_solve((jnp.linalg.cholesky(matrix), True), right_side)  5.63 us
    unnamed x4, local copies, waits for them, and re-layouts  5.07 us

profile of v4, /device:TPU:0, one launch (start us, length us, event | category | flops | bytes accessed | tf_op | source)
XLA Modules:
  0.0 92.7 jit_solution(4419619351624045070)
XLA Ops:
  0.6 1.3 %multiply_convert_fusion.1 = bf16[512,128]{1,0:T(8,128)(2,1)S(1)} fusion(bf16[164,512]{1,0:T(8,128)(2,1)} %param.16, bf16[164,128]{1,0:T(8,128)(2,1)} %param.14, f32[512]{0:T(512)} %param.17), kind=kOutput, calls=%fused_computation.15 | convolution fusion | flops 21889024 | bytes 343040 | tf_op jit(solution)/shard_map/dot_general | solution.py:17
  2.0 1.3 %fusion.2 = f32[64,128]{1,0:T(8,128)S(1)} fusion(bf16[512,64]{0,1:T(8,128)(2,1)} %param.20, bf16[512,128]{1,0:T(8,128)(2,1)S(1)} %multiply_convert_fusion.1, bf16[512,512]{1,0:T(8,128)(2,1)S(1)} %copy-done, f32[512]{0:T(512)} %param.19), kind=kOutput, calls=%fused_computation.10 | convolution fusion | flops 75907072 | bytes 755712 | tf_op jit(solution)/shard_map/dot_general | solution.py:17
  3.3 0.7 bitcast_convert_fusion
  4.0 0.7 pad_maximum_fusion
  4.7 25.3 %all_gather.3 = f32[81,2048]{1,0:T(8,128)S(1)} all-gather(f32[81,128]{1,0:T(8,128)S(1)} %pad_maximum_fusion), channel_id=1, replica_groups=mesh['task'=2,'row'=4,'col'=4] {'row','col'}, dimensions={1}, use_global_device_ids=true | all-gather | bytes 705024 | tf_op jit(solution)/shard_map/all_gather | solution.py:151
  29.9 0.9 convolution_add_fusion.5
  31.9 6.8 %select_multiply_fusion = f32[2048,2048]{1,0:T(8,128)S(1)} fusion(f32[2048]{0:T(1024)S(1)} %bitcast.84, f32[2048]{0:T(1024)S(1)} %bitcast.85, f32[2048]{0:T(1024)S(1)} %bitcast.86, f32[2048]{0:T(1024)S(1)} %bitcast.83, f32[2048]{0:T(1024)S(1)} %multiply_reduce_fusion, f32[]{:T(128)} %bitcast.3, pred[2048]{0:T(1024)(128)(4,1)S(1)} %get-tuple-element.111, ...), kind=kOutput, calls=%fused_computation | convolution fusion | flops 570425344 | bytes 17094660 | tf_op jit(solution)/shard_map/while/body/eval_jaxpr/while/body/eval_jaxpr/dot_general | solution.py:17
  39.3 5.1 %copy-done.1 = f32[2048,2048]{1,0:T(8,128)} copy-done((f32[2048,2048]{1,0:T(8,128)}, f32[2048,2048]{1,0:T(8,128)S(1)}, u32[]{:S(2)}) %copy-start.1) | copy-done | bytes 16777240
  44.4 14.2 %convolution_add_fusion.2 = f32[16,2048]{1,0:T(8,128)S(1)} fusion(f32[2048,2048]{1,0:T(8,128)S(1)} %select_multiply_fusion, f32[81,2048]{1,0:T(8,128)S(1)} %all_gather.3, f32[]{:T(128)} %bitcast.79), kind=kOutput, calls=%fused_computation.4 | convolution fusion | flops 805371904 | bytes 17170436 | tf_op jit(solution)/shard_map/while/body/eval_jaxpr/while/body/eval_jaxpr/dot_general | solution.py:107
  58.9 1.5 %cholesky.59 = f32[16,16]{1,0:T(8,128)S(1)} custom-call(f32[16,16]{1,0:T(8,128)S(1)} %fusion.32), custom_call_target="Cholesky" | custom-call | tf_op jit(solution)/shard_map/jit(cholesky)/cholesky | solution.py:29
  60.5 0.6 compare_reduce_fusion.2
  61.1 0.6 fusion.15
  61.8 1.2 %custom-call.9 = f32[1,16,16]{1,2,0:T(8,128)S(1)} custom-call(f32[1,16,16]{2,1,0:T(8,128)S(1)} %fusion.15), custom_call_target="InvertDiagBlocksLowerTriangular" | custom-call | tf_op jit(solution)/shard_map/jit(_cho_solve)/triangular_solve | solution.py:29
  64.6 1.5 %cholesky.70 = f32[16,16]{1,0:T(8,128)S(1)} custom-call(f32[16,16]{1,0:T(8,128)S(1)} %fusion.27), custom_call_target="Cholesky" | custom-call | tf_op jit(solution)/shard_map/jit(cholesky)/cholesky | solution.py:29
  66.2 0.6 compare_reduce_fusion.1
  66.8 0.6 fusion.16
  67.5 1.2 %custom-call.10 = f32[1,16,16]{1,2,0:T(8,128)S(1)} custom-call(f32[1,16,16]{2,1,0:T(8,128)S(1)} %fusion.16), custom_call_target="InvertDiagBlocksLowerTriangular" | custom-call | tf_op jit(solution)/shard_map/jit(_cho_solve)/triangular_solve | solution.py:29
  69.0 0.3 convolution_add_fusion
  69.4 17.3 %convolution_add_fusion.1 = f32[16,2048]{1,0:T(8,128)S(1)} fusion(f32[16,2048]{1,0:T(8,128)S(1)} %convolution_add_fusion, f32[2048,2048]{1,0:T(8,128)} %copy-done.1, f32[]{:T(128)} %bitcast.80), kind=kOutput, calls=%fused_computation.3 | convolution fusion | flops 805371904 | bytes 17039364 | tf_op jit(solution)/shard_map/while/body/eval_jaxpr/while/body/eval_jaxpr/dot_general | solution.py:107
  87.0 1.5 %cholesky.81 = f32[16,16]{1,0:T(8,128)S(1)} custom-call(f32[16,16]{1,0:T(8,128)S(1)} %fusion.22), custom_call_target="Cholesky" | custom-call | tf_op jit(solution)/shard_map/jit(cholesky)/cholesky | solution.py:29
  88.6 0.6 compare_reduce_fusion
  89.2 0.6 fusion.17
  89.9 1.2 %custom-call.11 = f32[1,16,16]{1,2,0:T(8,128)S(1)} custom-call(f32[1,16,16]{2,1,0:T(8,128)S(1)} %fusion.17), custom_call_target="InvertDiagBlocksLowerTriangular" | custom-call | tf_op jit(solution)/shard_map/jit(_cho_solve)/triangular_solve | solution.py:29
  92.1 0.6 dynamic-slice_subtract_fusion
  (32 shorter events, 4.0 us)
Async XLA Ops:
  0.6 1.3 %copy-start = (bf16[512,512]{1,0:T(8,128)(2,1)S(1)}, bf16[512,512]{1,0:T(8,128)(2,1)}, u32[]{:S(2)}) copy-start(bf16[512,512]{1,0:T(8,128)(2,1)} %param.18) | copy-start | bytes 1572868
  38.7 5.7 %copy-start.1 = (f32[2048,2048]{1,0:T(8,128)}, f32[2048,2048]{1,0:T(8,128)S(1)}, u32[]{:S(2)}) copy-start(f32[2048,2048]{1,0:T(8,128)S(1)} %select_multiply_fusion) | copy-start | bytes 50331652

commit v5 on v2

--- a/solution.py
+++ b/solution.py
@@ -104,21 +104,23 @@
     hidden_two = jax.nn.silu(left_product(w_second, hidden_one) + b_second[:, None]).astype(
         jnp.bfloat16
     )
-    embedding = left_product(w_third, hidden_two).astype(jnp.bfloat16)
-    rung_value = rung_index.astype(jnp.float32).astype(jnp.bfloat16)
+    embedding = lax.reduce_precision(
+        left_product(w_third, hidden_two), exponent_bits=8, mantissa_bits=7
+    )
+    rung_value = rung_index.astype(jnp.float32)
     own_count = targets.shape[1]
     own_first = (lax.axis_index("row") * lax.axis_size("col") + lax.axis_index("col")) * own_count
 
     emb_rows = embedding.shape[0]
     packed = jnp.concatenate(
-        [embedding.astype(jnp.float32), targets, rung_value.astype(jnp.float32)[None, :]], axis=0
+        [embedding, targets, rung_value[None, :]], axis=0
     )
     gathered = lax.all_gather(packed, ("row", "col"), axis=1, tiled=True)
     all_embedding = gathered[:emb_rows].astype(jnp.bfloat16)
     all_targets = gathered[emb_rows : emb_rows + targets.shape[0]]
     all_rung = gathered[emb_rows + targets.shape[0]]
 
-    squares = jnp.sum(jnp.square(all_embedding.astype(jnp.float32)), axis=0)
+    squares = jnp.sum(jnp.square(gathered[:emb_rows]), axis=0)
     col_fidelity = rung_fidelity(fidelity, all_rung)
 
     solution = jnp.zeros_like(all_targets)

time: 79 us -> 79 us (level)
  no operation moved by 1% of the time
where the time goes in v5:
time: 79 us; the launch traced here: 78.7 us
  matrix products  31.6 us (40%)
  blocking collectives  25.3 us (32%)
  other arithmetic  14.3 us (18%)
  local copies, waits for them, and re-layouts  5.42 us (7%)
  between operations  2.1 us (3%)
    all_gather x1, blocking collectives, on_device(): gathered = lax.all_gather(packed, ('row', 'col'), axis=1, tiled=True)  25.3 us
    dot_general x2, matrix products, one_col_block(): lax.dot_general(cols_direction, kernel, (((1,), (1,)), ((), ())), precisi...  17.5 us
    dot_general x3, matrix products, left_product(): lax.dot_general(weights, values, (((0,), (0,)), ((), ())), preferred_elem...  9.47 us
    another operation x9, other arithmetic, solve_spd(): jnp.linalg.cholesky(matrix)  6.57 us
    another operation x6, other arithmetic, solve_spd(): jax.scipy.linalg.cho_solve((jnp.linalg.cholesky(matrix), True), right_side)  5.63 us
    unnamed x4, local copies, waits for them, and re-layouts  5.07 us

profile of v5, /device:TPU:0, one launch (start us, length us, event | category | flops | bytes accessed | tf_op | source)
XLA Modules:
  0.0 78.7 jit_solution(8711055109204484541)
XLA Ops:
  0.6 1.3 %multiply_convert_fusion.1 = bf16[512,128]{1,0:T(8,128)(2,1)S(1)} fusion(bf16[164,512]{1,0:T(8,128)(2,1)} %param.16, bf16[164,128]{1,0:T(8,128)(2,1)} %param.14, f32[512]{0:T(512)} %param.17), kind=kOutput, calls=%fused_computation.14 | convolution fusion | flops 21889024 | bytes 343040 | tf_op jit(solution)/shard_map/dot_general | solution.py:17
  2.0 1.3 %fusion.1 = f32[64,128]{1,0:T(8,128)S(1)} fusion(bf16[512,64]{0,1:T(8,128)(2,1)} %param.20, bf16[512,128]{1,0:T(8,128)(2,1)S(1)} %multiply_convert_fusion.1, bf16[512,512]{1,0:T(8,128)(2,1)S(1)} %copy-done, f32[512]{0:T(512)} %param.19), kind=kOutput, calls=%fused_computation.9 | convolution fusion | flops 75898880 | bytes 755712 | tf_op jit(solution)/shard_map/dot_general | solution.py:17
  3.3 0.7 convert_bitcast_fusion
  4.0 0.7 pad_maximum_fusion
  4.7 25.3 %all_gather.3 = f32[81,2048]{1,0:T(8,128)S(1)} all-gather(f32[81,128]{1,0:T(8,128)S(1)} %pad_maximum_fusion), channel_id=1, replica_groups=mesh['task'=2,'row'=4,'col'=4] {'row','col'}, dimensions={1}, use_global_device_ids=true | all-gather | bytes 705024 | tf_op jit(solution)/shard_map/all_gather | solution.py:118
  29.9 0.9 %convolution_add_fusion.5 = f32[4,4]{1,0:T(4,128)S(1)} fusion(f32[4,4]{1,0:T(4,128)} %param.22), kind=kOutput, calls=%fused_computation.10 | convolution fusion | flops 848 | bytes 128 | tf_op jit(solution)/shard_map/dot_general | solution.py:11
  31.9 6.8 %select_multiply_fusion = f32[2048,2048]{1,0:T(8,128)S(1)} fusion(f32[2048]{0:T(1024)S(1)} %bitcast.83, f32[2048]{0:T(1024)S(1)} %bitcast.84, f32[2048]{0:T(1024)S(1)} %bitcast.85, f32[2048]{0:T(1024)S(1)} %bitcast.82, f32[2048]{0:T(1024)S(1)} %multiply_reduce_fusion, f32[]{:T(128)} %bitcast.3, pred[2048]{0:T(1024)(128)(4,1)S(1)} %get-tuple-element.111, ...), kind=kOutput, calls=%fused_computation | convolution fusion | flops 570425344 | bytes 17094660 | tf_op jit(solution)/shard_map/while/body/eval_jaxpr/while/body/eval_jaxpr/dot_general | solution.py:17
  39.3 5.1 %copy-done.1 = f32[2048,2048]{1,0:T(8,128)} copy-done((f32[2048,2048]{1,0:T(8,128)}, f32[2048,2048]{1,0:T(8,128)S(1)}, u32[]{:S(2)}) %copy-start.1) | copy-done | bytes 16777240
  44.4 7.3 %convolution_add_fusion.2 = f32[16,2048]{1,0:T(8,128)S(1)} fusion(f32[2048,2048]{1,0:T(8,128)S(1)} %select_multiply_fusion, f32[81,2048]{1,0:T(8,128)S(1)} %all_gather.3, f32[]{:T(128)} %bitcast.78), kind=kOutput, calls=%fused_computation.4 | convolution fusion | flops 402718720 | bytes 17170436 | tf_op jit(solution)/shard_map/while/body/eval_jaxpr/while/body/eval_jaxpr/dot_general | solution.py:72
  52.1 1.5 %cholesky.59 = f32[16,16]{1,0:T(8,128)S(1)} custom-call(f32[16,16]{1,0:T(8,128)S(1)} %fusion.31), custom_call_target="Cholesky" | custom-call | tf_op jit(solution)/shard_map/jit(cholesky)/cholesky | solution.py:29
  53.6 0.6 compare_reduce_fusion.2
  54.3 0.6 fusion.14
  54.9 1.2 %custom-call.9 = f32[1,16,16]{1,2,0:T(8,128)S(1)} custom-call(f32[1,16,16]{2,1,0:T(8,128)S(1)} %fusion.14), custom_call_target="InvertDiagBlocksLowerTriangular" | custom-call | tf_op jit(solution)/shard_map/jit(_cho_solve)/triangular_solve | solution.py:29
  56.8 0.3 fusion.4
  57.8 1.5 %cholesky.70 = f32[16,16]{1,0:T(8,128)S(1)} custom-call(f32[16,16]{1,0:T(8,128)S(1)} %fusion.26), custom_call_target="Cholesky" | custom-call | tf_op jit(solution)/shard_map/jit(cholesky)/cholesky | solution.py:29
  59.3 0.6 compare_reduce_fusion.1
  60.0 0.6 fusion.15
  60.6 1.2 %custom-call.10 = f32[1,16,16]{1,2,0:T(8,128)S(1)} custom-call(f32[1,16,16]{2,1,0:T(8,128)S(1)} %fusion.15), custom_call_target="InvertDiagBlocksLowerTriangular" | custom-call | tf_op jit(solution)/shard_map/jit(_cho_solve)/triangular_solve | solution.py:29
  62.5 10.1 %convolution_add_fusion.1 = f32[16,2048]{1,0:T(8,128)S(1)} fusion(f32[16,2048]{1,0:T(8,128)S(1)} %convolution_add_fusion, f32[2048,2048]{1,0:T(8,128)} %copy-done.1, f32[]{:T(128)} %bitcast.79), kind=kOutput, calls=%fused_computation.3 | convolution fusion | flops 402718720 | bytes 17039364 | tf_op jit(solution)/shard_map/while/body/eval_jaxpr/while/body/eval_jaxpr/dot_general | solution.py:72
  73.0 1.5 %cholesky.81 = f32[16,16]{1,0:T(8,128)S(1)} custom-call(f32[16,16]{1,0:T(8,128)S(1)} %fusion.21), custom_call_target="Cholesky" | custom-call | tf_op jit(solution)/shard_map/jit(cholesky)/cholesky | solution.py:29
  74.5 0.6 compare_reduce_fusion
  75.2 0.6 fusion.16
  75.8 1.2 %custom-call.11 = f32[1,16,16]{1,2,0:T(8,128)S(1)} custom-call(f32[1,16,16]{2,1,0:T(8,128)S(1)} %fusion.16), custom_call_target="InvertDiagBlocksLowerTriangular" | custom-call | tf_op jit(solution)/shard_map/jit(_cho_solve)/triangular_solve | solution.py:29
  78.0 0.6 dynamic-slice_subtract_fusion
  (32 shorter events, 4.0 us)
Async XLA Ops:
  0.6 1.3 %copy-start = (bf16[512,512]{1,0:T(8,128)(2,1)S(1)}, bf16[512,512]{1,0:T(8,128)(2,1)}, u32[]{:S(2)}) copy-start(bf16[512,512]{1,0:T(8,128)(2,1)} %param.18) | copy-start | bytes 1572868
  38.7 5.7 %copy-start.1 = (f32[2048,2048]{1,0:T(8,128)}, f32[2048,2048]{1,0:T(8,128)S(1)}, u32[]{:S(2)}) copy-start(f32[2048,2048]{1,0:T(8,128)S(1)} %select_multiply_fusion) | copy-start | bytes 50331652

commit v6 on v5

--- a/solution.py
+++ b/solution.py
@@ -2,6 +2,8 @@
 import jax.numpy as jnp
 from jax import lax
 from jax.sharding import PartitionSpec as P
+from jax.experimental import pallas as pl
+from jax.experimental.pallas import tpu as pltpu
 
 ITERS = 2
 
@@ -42,46 +44,77 @@
     return jnp.dot(fidelity, onehot, precision=lax.Precision.HIGHEST)
 
 
+def image_block(rows_ref, cols_ref, cols_sq_ref, cols_fid_ref, dir_ref, scale_ref, out_ref):
+    emb_rows = cols_ref.shape[0]
+    rows_emb = rows_ref[:, :emb_rows].astype(jnp.bfloat16)
+    rows_sq = rows_ref[:, emb_rows : emb_rows + 1]
+    rows_rung = rows_ref[:, emb_rows + 1 : emb_rows + 2]
+    inner = jnp.dot(rows_emb, cols_ref[...], preferred_element_type=jnp.float32)
+    distance = rows_sq + cols_sq_ref[...] - 2.0 * inner
+    cols_fid = cols_fid_ref[...]
+    tile_fid = cols_fid[0:1, :]
+    for level in range(1, cols_fid.shape[0]):
+        tile_fid = jnp.where(rows_rung == float(level), cols_fid[level : level + 1, :], tile_fid)
+    kernel = jnp.exp(scale_ref[...] * distance) * tile_fid
+    kernel_hi = kernel.astype(jnp.bfloat16)
+    kernel_lo = (kernel - kernel_hi.astype(jnp.float32)).astype(jnp.bfloat16)
+    dims = (((1,), (1,)), ((), ()))
+    both = dir_ref[...]
+    count = out_ref.shape[0]
+    by_hi = lax.dot_general(both, kernel_hi, dims, preferred_element_type=jnp.float32)
+    by_lo = lax.dot_general(both[:count], kernel_lo, dims, preferred_element_type=jnp.float32)
+    contribution = (by_hi[:count] + by_hi[count:]) + by_lo
+
+    @pl.when(pl.program_id(1) == 0)
+    def _():
+        out_ref[...] = contribution
+
+    @pl.when(pl.program_id(1) != 0)
+    def _():
+        out_ref[...] = out_ref[...] + contribution
+
+
 def kernel_image(embedding, squares, rung_value, col_fidelity, inverse_scale, direction):
-    count = embedding.shape[1]
-    row_block = block_size(count, 2048)
+    emb_rows, count = embedding.shape
+    rhs = direction.shape[0]
+    row_block = block_size(count, 256)
     col_block = block_size(count, 2048)
-    levels = jnp.arange(col_fidelity.shape[0], dtype=jnp.float32)
-
-    def one_row_block(block_number):
-        first_row = block_number * row_block
-        rows_embedding = lax.dynamic_slice_in_dim(embedding, first_row, row_block, 1)
-        rows_squares = lax.dynamic_slice_in_dim(squares, first_row, row_block, 0)
-        rows_rung = lax.dynamic_slice_in_dim(rung_value, first_row, row_block, 0)
-        rows_match = rows_rung.astype(jnp.float32)[:, None] == levels[None, :]
-
-        def one_col_block(running, column_number):
-            first_col = column_number * col_block
-            cols_embedding = lax.dynamic_slice_in_dim(embedding, first_col, col_block, 1)
-            cols_squares = lax.dynamic_slice_in_dim(squares, first_col, col_block, 0)
-            cols_fidelity = lax.dynamic_slice_in_dim(col_fidelity, first_col, col_block, 1)
-            cols_direction = lax.dynamic_slice_in_dim(direction, first_col, col_block, 1)
-            inner = left_product(rows_embedding, cols_embedding)
-            distance = rows_squares[:, None] + cols_squares[None, :] - 2.0 * inner
-            tile_fidelity = cols_fidelity[0][None, :]
-            for level in range(1, col_fidelity.shape[0]):
-                tile_fidelity = jnp.where(
-                    rows_match[:, level : level + 1], cols_fidelity[level][None, :], tile_fidelity
-                )
-            kernel = jnp.exp(-inverse_scale[0] * distance) * tile_fidelity
-            contribution = lax.dot_general(
-                cols_direction, kernel, (((1,), (1,)), ((), ())), precision=lax.Precision.HIGH
-            )
-            return (running + contribution, None)
-
-        start_value = jnp.zeros((direction.shape[0], row_block), jnp.float32)
-        result, unused = lax.scan(
-            one_col_block, start_value, jnp.arange(count // col_block, dtype=jnp.int32)
-        )
-        return result
-
-    stacked = lax.map(one_row_block, jnp.arange(count // row_block, dtype=jnp.int32))
-    return jnp.transpose(stacked, (1, 0, 2)).reshape(direction.shape[0], count)
+    direction_hi = lax.reduce_precision(direction, exponent_bits=8, mantissa_bits=7)
+    direction_lo = (direction - direction_hi).astype(jnp.bfloat16)
+    stacked = jnp.concatenate([direction_hi.astype(jnp.bfloat16), direction_lo], axis=0)
+    scale = jnp.reshape(-inverse_scale[0], (1, 1))
+    grid = (count // row_block, count // col_block)
+    row_width = 128 * ((emb_rows + 2 + 127) // 128)
+    rows_packed = jnp.concatenate(
+        [
+            embedding,
+            squares[None, :],
+            rung_value[None, :],
+            jnp.zeros((row_width - emb_rows - 2, count), jnp.float32),
+        ],
+        axis=0,
+    ).T
+    return pl.pallas_call(
+        image_block,
+        grid=grid,
+        in_specs=[
+            pl.BlockSpec((row_block, row_width), lambda i, j: (i, 0)),
+            pl.BlockSpec((emb_rows, col_block), lambda i, j: (0, j)),
+            pl.BlockSpec((1, col_block), lambda i, j: (0, j)),
+            pl.BlockSpec((col_fidelity.shape[0], col_block), lambda i, j: (0, j)),
+            pl.BlockSpec((2 * rhs, col_block), lambda i, j: (0, j)),
+            pl.BlockSpec((1, 1), lambda i, j: (0, 0)),
+        ],
+        out_specs=pl.BlockSpec((rhs, row_block), lambda i, j: (0, i)),
+        out_shape=jax.ShapeDtypeStruct((rhs, count), jnp.float32),
+    )(
+        rows_packed,
+        embedding.astype(jnp.bfloat16),
+        squares[None, :],
+        col_fidelity,
+        stacked,
+        scale,
+    )
 
 
 def on_device(
@@ -129,7 +162,9 @@
     gram = outer_gram(residual, residual)
     for iteration in range(ITERS):
         image = (
-            kernel_image(all_embedding, squares, all_rung, col_fidelity, inverse_scale, direction)
+            kernel_image(
+                gathered[:emb_rows], squares, all_rung, col_fidelity, inverse_scale, direction
+            )
             + noise_var[0] * direction
         )
         curvature = outer_gram(direction, image)

time: 79 us -> 84 us (1.063)
  Pallas kernels: 0 us -> 29.4 us
  matrix products: 31.6 us -> 8.17 us
  local copies, waits for them, and re-layouts: 5.42 us -> 4.25 us
    pallas_call x0 -> x2, Pallas kernels: none -> 29.4 us  [kernel_image(): pl.pallas_call(image_block, grid=grid, in_specs=[pl.BlockSpec((row_block,...]
    dot_general x2 -> x0, matrix products: 17.5 us -> none  [one_col_block(): lax.dot_general(cols_direction, kernel, (((1,), (1,)), ((), ())), precisi...]
    dot_general x3 -> x2, matrix products: 9.47 us -> 1.81 us  [left_product(): lax.dot_general(weights, values, (((0,), (0,)), ((), ())), preferred_elem...]
    unnamed x4 -> x18, local copies, waits for them, and re-layouts: 5.07 us -> 1.87 us
    dot_general x4, matrix products: 0.93 us -> 2.75 us  [outer_gram(): lax.dot_general(left_side, right_side, (((1,), (1,)), ((), ())), precisio...]
    transpose x0 -> x1, local copies, waits for them, and re-layouts: none -> 1.33 us  [kernel_image(): rows_packed = jnp.concatenate([embedding, squares[None, :], rung_value[No...]
    concatenate x0 -> x2, other arithmetic: none -> 1.32 us  [kernel_image(): jnp.concatenate([direction_hi.astype(jnp.bfloat16), direction_lo], axis=0)]
where the time goes in v6:
time: 84 us; the launch traced here: 83.6 us
  Pallas kernels  29.4 us (35%)
  blocking collectives  25.3 us (30%)
  other arithmetic  14.4 us (17%)
  matrix products  8.17 us (10%)
  local copies, waits for them, and re-layouts  4.25 us (5%)
  between operations  2.17 us (3%)
    pallas_call x2, Pallas kernels, kernel_image(): pl.pallas_call(image_block, grid=grid, in_specs=[pl.BlockSpec((row_block,...  29.4 us
    all_gather x1, blocking collectives, on_device(): gathered = lax.all_gather(packed, ('row', 'col'), axis=1, tiled=True)  25.3 us
    another operation x9, other arithmetic, solve_spd(): jnp.linalg.cholesky(matrix)  6.63 us
    another operation x6, other arithmetic, solve_spd(): jax.scipy.linalg.cho_solve((jnp.linalg.cholesky(matrix), True), right_side)  5.6 us
    dot_general x4, matrix products, outer_gram(): lax.dot_general(left_side, right_side, (((1,), (1,)), ((), ())), precisio...  2.75 us
    unnamed x18, local copies, waits for them, and re-layouts  1.87 us
    dot_general x2, matrix products, left_product(): lax.dot_general(weights, values, (((0,), (0,)), ((), ())), preferred_elem...  1.81 us

profile of v6, /device:TPU:0, one launch (start us, length us, event | category | flops | bytes accessed | tf_op | source)
XLA Modules:
  0.0 83.6 jit_solution(2775744996420024277)
XLA Ops:
  0.7 1.3 %multiply_convert_fusion.1 = bf16[512,128]{1,0:T(8,128)(2,1)S(1)} fusion(bf16[164,512]{1,0:T(8,128)(2,1)} %param.16, bf16[164,128]{1,0:T(8,128)(2,1)} %param.14, f32[512]{0:T(512)} %param.17), kind=kOutput, calls=%fused_computation.11 | convolution fusion | flops 21889024 | bytes 343040 | tf_op jit(solution)/shard_map/dot_general | solution.py:19
  2.7 25.3 %all_gather.3 = f32[81,2048]{1,0:T(8,128)S(1)} all-gather(f32[81,128]{1,0:T(8,128)S(1)} %pad_maximum_fusion.2), channel_id=1, replica_groups=mesh['task'=2,'row'=4,'col'=4] {'row','col'}, dimensions={1}, use_global_device_ids=true | all-gather | bytes 705024 | tf_op jit(solution)/shard_map/all_gather | solution.py:151
  28.8 1.3 %copy.14.rows_ref = f32[2048,128]{1,0:T(8,128)} copy(f32[2048,128]{0,1:T(8,128)S(1)} %maximum_bitcast_fusion) | data formatting | bytes 2097152 | tf_op jit(solution)/shard_map/transpose | solution.py:96
  30.2 0.7 pad_maximum_fusion.dir_ref
  31.0 0.8 fusion.20.cols_fid_ref
  31.7 0.7 slice.47.cols_ref
  33.1 14.7 %shard_map.122 = f32[16,2048]{1,0:T(8,128)} custom-call(f32[2048,128]{1,0:T(8,128)} %copy.14.rows_ref, bf16[64,2048]{1,0:T(8,128)(2,1)} %slice.47.cols_ref, f32[1,2048]{1,0:T(1,128)} %bitcast.75, f32[4,2048]{1,0:T(4,128)} %fusion.20.cols_fid_ref, bf16[32,2048]{1,0:T(8,128)(2,1)} %pad_maximum_fusion.dir_ref, f32[1,1]{1,0:T(1,128)} %bitcast.6.scale_ref), custom_call_target="tpu_custom_call" | custom-call | tf_op jit(solution)/shard_map/pallas_call | solution.py:97
  48.5 1.1 %fusion.4 = f32[16,16]{1,0:T(8,128)S(1)} fusion(f32[16,2048]{1,0:T(8,128)} %shard_map.122, f32[81,2048]{1,0:T(8,128)S(1)} %all_gather.3, f32[]{:T(128)} %bitcast.70), kind=kOutput, calls=%fused_computation.22 | convolution fusion | flops 6356992 | bytes 394244 | tf_op jit(solution)/shard_map/dot_general | solution.py:25
  49.7 1.5 %cholesky.59 = f32[16,16]{1,0:T(8,128)S(1)} custom-call(f32[16,16]{1,0:T(8,128)S(1)} %fusion.39), custom_call_target="Cholesky" | custom-call | tf_op jit(solution)/shard_map/jit(cholesky)/cholesky | solution.py:31
  51.2 0.7 compare_reduce_fusion.2
  51.9 0.6 fusion.22
  52.6 1.2 %custom-call.9 = f32[1,16,16]{1,2,0:T(8,128)S(1)} custom-call(f32[1,16,16]{2,1,0:T(8,128)S(1)} %fusion.22), custom_call_target="InvertDiagBlocksLowerTriangular" | custom-call | tf_op jit(solution)/shard_map/jit(_cho_solve)/triangular_solve | solution.py:31
  56.0 1.5 %cholesky.70 = f32[16,16]{1,0:T(8,128)S(1)} custom-call(f32[16,16]{1,0:T(8,128)S(1)} %fusion.34), custom_call_target="Cholesky" | custom-call | tf_op jit(solution)/shard_map/jit(cholesky)/cholesky | solution.py:31
  57.5 0.7 compare_reduce_fusion.1
  58.2 0.6 fusion.23
  58.8 1.2 %custom-call.10 = f32[1,16,16]{1,2,0:T(8,128)S(1)} custom-call(f32[1,16,16]{2,1,0:T(8,128)S(1)} %fusion.23), custom_call_target="InvertDiagBlocksLowerTriangular" | custom-call | tf_op jit(solution)/shard_map/jit(_cho_solve)/triangular_solve | solution.py:31
  60.8 0.7 pad_maximum_fusion.1.dir_ref
  61.4 14.7 %shard_map.123 = f32[16,2048]{1,0:T(8,128)} custom-call(f32[2048,128]{1,0:T(8,128)} %copy.14.rows_ref, bf16[64,2048]{1,0:T(8,128)(2,1)} %slice.47.cols_ref, f32[1,2048]{1,0:T(1,128)} %bitcast.76, f32[4,2048]{1,0:T(4,128)} %fusion.20.cols_fid_ref, bf16[32,2048]{1,0:T(8,128)(2,1)} %pad_maximum_fusion.1.dir_ref, f32[1,1]{1,0:T(1,128)} %bitcast.6.scale_ref), custom_call_target="tpu_custom_call" | custom-call | tf_op jit(solution)/shard_map/pallas_call | solution.py:97
  76.1 1.1 %fusion.8 = f32[16,16]{1,0:T(8,128)S(1)} fusion(f32[16,2048]{1,0:T(8,128)S(1)} %get-tuple-element.10, f32[16,2048]{1,0:T(8,128)} %shard_map.123, f32[]{:T(128)} %bitcast.73), kind=kOutput, calls=%fused_computation.26 | convolution fusion | flops 6356992 | bytes 263172 | tf_op jit(solution)/shard_map/dot_general | solution.py:25
  77.3 1.5 %cholesky.81 = f32[16,16]{1,0:T(8,128)S(1)} custom-call(f32[16,16]{1,0:T(8,128)S(1)} %fusion.29), custom_call_target="Cholesky" | custom-call | tf_op jit(solution)/shard_map/jit(cholesky)/cholesky | solution.py:31
  78.9 0.6 compare_reduce_fusion
  79.5 0.6 fusion.24
  80.2 1.2 %custom-call.11 = f32[1,16,16]{1,2,0:T(8,128)S(1)} custom-call(f32[1,16,16]{2,1,0:T(8,128)S(1)} %fusion.24), custom_call_target="InvertDiagBlocksLowerTriangular" | custom-call | tf_op jit(solution)/shard_map/jit(_cho_solve)/triangular_solve | solution.py:31
  83.0 0.6 dynamic-slice_subtract_fusion
  (50 shorter events, 6.3 us)
Async XLA Ops:
  0.6 1.4 %copy-start = (bf16[512,512]{1,0:T(8,128)(2,1)S(1)}, bf16[512,512]{1,0:T(8,128)(2,1)}, u32[]{:S(2)}) copy-start(bf16[512,512]{1,0:T(8,128)(2,1)} %param.18) | copy-start | bytes 1572868
  0.6 1.3 %copy-start.6 = (f32[512]{0:T(512)S(1)}, f32[512]{0:T(512)}, u32[]{:S(2)}) copy-start(f32[512]{0:T(512)} %param.19) | copy-start | bytes 6148
  0.7 1.3 %copy-start.5 = (bf16[512,64]{0,1:T(8,128)(2,1)S(1)}, bf16[512,64]{0,1:T(8,128)(2,1)}, u32[]{:S(2)}) copy-start(bf16[512,64]{0,1:T(8,128)(2,1)} %param.20) | copy-start | bytes 196612
  2.0 0.7 copy-start.8
  2.0 0.7 copy-start.4
  28.1 0.6 copy-start.3
  30.1 0.7 copy-start.7
  54.4 0.9 %copy-start.2 = (f32[16,2048]{1,0:T(8,128)S(1)}, f32[16,2048]{1,0:T(8,128)}, u32[]{:S(2)}) copy-start(f32[16,2048]{1,0:T(8,128)} %shard_map.122) | copy-start | bytes 393220
  81.7 0.9 %copy-start.1 = (f32[16,2048]{1,0:T(8,128)S(1)}, f32[16,2048]{1,0:T(8,128)}, u32[]{:S(2)}) copy-start(f32[16,2048]{1,0:T(8,128)} %shard_map.123) | copy-start | bytes 393220

commit v7 on v6

--- a/solution.py
+++ b/solution.py
@@ -44,25 +44,24 @@
     return jnp.dot(fidelity, onehot, precision=lax.Precision.HIGHEST)
 
 
-def image_block(rows_ref, cols_ref, cols_sq_ref, cols_fid_ref, dir_ref, scale_ref, out_ref):
-    emb_rows = cols_ref.shape[0]
-    rows_emb = rows_ref[:, :emb_rows].astype(jnp.bfloat16)
-    rows_sq = rows_ref[:, emb_rows : emb_rows + 1]
-    rows_rung = rows_ref[:, emb_rows + 1 : emb_rows + 2]
-    inner = jnp.dot(rows_emb, cols_ref[...], preferred_element_type=jnp.float32)
-    distance = rows_sq + cols_sq_ref[...] - 2.0 * inner
-    cols_fid = cols_fid_ref[...]
-    tile_fid = cols_fid[0:1, :]
-    for level in range(1, cols_fid.shape[0]):
-        tile_fid = jnp.where(rows_rung == float(level), cols_fid[level : level + 1, :], tile_fid)
+def image_block(sum_ref, out_emb_ref, out_sq_ref, out_fid_ref, dir_ref, scale_ref, out_ref):
+    emb_rows = out_emb_ref.shape[0]
+    sum_emb = sum_ref[:, :emb_rows].astype(jnp.bfloat16)
+    sum_sq = sum_ref[:, emb_rows : emb_rows + 1]
+    sum_rung = sum_ref[:, emb_rows + 1 : emb_rows + 2]
+    inner = jnp.dot(sum_emb, out_emb_ref[...], preferred_element_type=jnp.float32)
+    distance = out_sq_ref[...] + sum_sq - 2.0 * inner
+    out_fid = out_fid_ref[...]
+    tile_fid = out_fid[0:1, :]
+    for level in range(1, out_fid.shape[0]):
+        tile_fid = jnp.where(sum_rung == float(level), out_fid[level : level + 1, :], tile_fid)
     kernel = jnp.exp(scale_ref[...] * distance) * tile_fid
     kernel_hi = kernel.astype(jnp.bfloat16)
     kernel_lo = (kernel - kernel_hi.astype(jnp.float32)).astype(jnp.bfloat16)
-    dims = (((1,), (1,)), ((), ()))
     both = dir_ref[...]
     count = out_ref.shape[0]
-    by_hi = lax.dot_general(both, kernel_hi, dims, preferred_element_type=jnp.float32)
-    by_lo = lax.dot_general(both[:count], kernel_lo, dims, preferred_element_type=jnp.float32)
+    by_hi = jnp.dot(both, kernel_hi, preferred_element_type=jnp.float32)
+    by_lo = jnp.dot(both[:count], kernel_lo, preferred_element_type=jnp.float32)
     contribution = (by_hi[:count] + by_hi[count:]) + by_lo
 
     @pl.when(pl.program_id(1) == 0)
@@ -77,20 +76,20 @@
 def kernel_image(embedding, squares, rung_value, col_fidelity, inverse_scale, direction):
     emb_rows, count = embedding.shape
     rhs = direction.shape[0]
-    row_block = block_size(count, 256)
-    col_block = block_size(count, 2048)
+    out_block = block_size(count, 256)
+    sum_block = block_size(count, 2048)
     direction_hi = lax.reduce_precision(direction, exponent_bits=8, mantissa_bits=7)
     direction_lo = (direction - direction_hi).astype(jnp.bfloat16)
     stacked = jnp.concatenate([direction_hi.astype(jnp.bfloat16), direction_lo], axis=0)
     scale = jnp.reshape(-inverse_scale[0], (1, 1))
-    grid = (count // row_block, count // col_block)
-    row_width = 128 * ((emb_rows + 2 + 127) // 128)
-    rows_packed = jnp.concatenate(
+    grid = (count // out_block, count // sum_block)
+    sum_width = 128 * ((emb_rows + 2 + 127) // 128)
+    sum_packed = jnp.concatenate(
         [
             embedding,
             squares[None, :],
             rung_value[None, :],
-            jnp.zeros((row_width - emb_rows - 2, count), jnp.float32),
+            jnp.zeros((sum_width - emb_rows - 2, count), jnp.float32),
         ],
         axis=0,
     ).T
@@ -98,17 +97,17 @@
         image_block,
         grid=grid,
         in_specs=[
-            pl.BlockSpec((row_block, row_width), lambda i, j: (i, 0)),
-            pl.BlockSpec((emb_rows, col_block), lambda i, j: (0, j)),
-            pl.BlockSpec((1, col_block), lambda i, j: (0, j)),
-            pl.BlockSpec((col_fidelity.shape[0], col_block), lambda i, j: (0, j)),
-            pl.BlockSpec((2 * rhs, col_block), lambda i, j: (0, j)),
+            pl.BlockSpec((sum_block, sum_width), lambda i, j: (j, 0)),
+            pl.BlockSpec((emb_rows, out_block), lambda i, j: (0, i)),
+            pl.BlockSpec((1, out_block), lambda i, j: (0, i)),
+            pl.BlockSpec((col_fidelity.shape[0], out_block), lambda i, j: (0, i)),
+            pl.BlockSpec((2 * rhs, sum_block), lambda i, j: (0, j)),
             pl.BlockSpec((1, 1), lambda i, j: (0, 0)),
         ],
-        out_specs=pl.BlockSpec((rhs, row_block), lambda i, j: (0, i)),
+        out_specs=pl.BlockSpec((rhs, out_block), lambda i, j: (0, i)),
         out_shape=jax.ShapeDtypeStruct((rhs, count), jnp.float32),
     )(
-        rows_packed,
+        sum_packed,
         embedding.astype(jnp.bfloat16),
         squares[None, :],
         col_fidelity,

time: 84 us -> 89.7 us (1.068)
  Pallas kernels: 29.4 us -> 35.1 us
    pallas_call x2, Pallas kernels: 29.4 us -> 35.1 us  [kernel_image(): pl.pallas_call(image_block, grid=grid, in_specs=[pl.BlockSpec((sum_block,...]
where the time goes in v7:
time: 89.7 us; the launch traced here: 89.3 us
  Pallas kernels  35.1 us (39%)
  blocking collectives  25.3 us (28%)
  other arithmetic  14.4 us (16%)
  matrix products  8.16 us (9%)
  local copies, waits for them, and re-layouts  4.25 us (5%)
  between operations  2.17 us (2%)
    pallas_call x2, Pallas kernels, kernel_image(): pl.pallas_call(image_block, grid=grid, in_specs=[pl.BlockSpec((sum_block,...  35.1 us
    all_gather x1, blocking collectives, on_device(): gathered = lax.all_gather(packed, ('row', 'col'), axis=1, tiled=True)  25.3 us
    another operation x9, other arithmetic, solve_spd(): jnp.linalg.cholesky(matrix)  6.63 us
    another operation x6, other arithmetic, solve_spd(): jax.scipy.linalg.cho_solve((jnp.linalg.cholesky(matrix), True), right_side)  5.6 us
    dot_general x4, matrix products, outer_gram(): lax.dot_general(left_side, right_side, (((1,), (1,)), ((), ())), precisio...  2.75 us
    unnamed x18, local copies, waits for them, and re-layouts  1.87 us
    dot_general x2, matrix products, left_product(): lax.dot_general(weights, values, (((0,), (0,)), ((), ())), preferred_elem...  1.81 us

profile of v7, /device:TPU:0, one launch (start us, length us, event | category | flops | bytes accessed | tf_op | source)
XLA Modules:
  0.0 89.3 jit_solution(18135814655700060295)
XLA Ops:
  0.7 1.3 %multiply_convert_fusion.1 = bf16[512,128]{1,0:T(8,128)(2,1)S(1)} fusion(bf16[164,512]{1,0:T(8,128)(2,1)} %param.16, bf16[164,128]{1,0:T(8,128)(2,1)} %param.14, f32[512]{0:T(512)} %param.17), kind=kOutput, calls=%fused_computation.11 | convolution fusion | flops 21889024 | bytes 343040 | tf_op jit(solution)/shard_map/dot_general | solution.py:19
  2.7 25.3 %all_gather.3 = f32[81,2048]{1,0:T(8,128)S(1)} all-gather(f32[81,128]{1,0:T(8,128)S(1)} %pad_maximum_fusion.2), channel_id=1, replica_groups=mesh['task'=2,'row'=4,'col'=4] {'row','col'}, dimensions={1}, use_global_device_ids=true | all-gather | bytes 705024 | tf_op jit(solution)/shard_map/all_gather | solution.py:150
  28.8 1.3 %copy.14.sum_ref = f32[2048,128]{1,0:T(8,128)} copy(f32[2048,128]{0,1:T(8,128)S(1)} %maximum_bitcast_fusion) | data formatting | bytes 2097152 | tf_op jit(solution)/shard_map/transpose | solution.py:95
  30.2 0.7 pad_maximum_fusion.dir_ref
  31.0 0.8 fusion.20.out_fid_ref
  31.7 0.7 slice.47.out_emb_ref
  33.1 17.5 %shard_map.122 = f32[16,2048]{1,0:T(8,128)} custom-call(f32[2048,128]{1,0:T(8,128)} %copy.14.sum_ref, bf16[64,2048]{1,0:T(8,128)(2,1)} %slice.47.out_emb_ref, f32[1,2048]{1,0:T(1,128)} %bitcast.75, f32[4,2048]{1,0:T(4,128)} %fusion.20.out_fid_ref, bf16[32,2048]{1,0:T(8,128)(2,1)} %pad_maximum_fusion.dir_ref, f32[1,1]{1,0:T(1,128)} %bitcast.6.scale_ref), custom_call_target="tpu_custom_call" | custom-call | tf_op jit(solution)/shard_map/pallas_call | solution.py:96
  51.3 1.1 %fusion.4 = f32[16,16]{1,0:T(8,128)S(1)} fusion(f32[16,2048]{1,0:T(8,128)} %shard_map.122, f32[81,2048]{1,0:T(8,128)S(1)} %all_gather.3, f32[]{:T(128)} %bitcast.70), kind=kOutput, calls=%fused_computation.22 | convolution fusion | flops 6356992 | bytes 394244 | tf_op jit(solution)/shard_map/dot_general | solution.py:25
  52.5 1.5 %cholesky.59 = f32[16,16]{1,0:T(8,128)S(1)} custom-call(f32[16,16]{1,0:T(8,128)S(1)} %fusion.39), custom_call_target="Cholesky" | custom-call | tf_op jit(solution)/shard_map/jit(cholesky)/cholesky | solution.py:31
  54.1 0.7 compare_reduce_fusion.2
  54.8 0.6 fusion.22
  55.4 1.2 %custom-call.9 = f32[1,16,16]{1,2,0:T(8,128)S(1)} custom-call(f32[1,16,16]{2,1,0:T(8,128)S(1)} %fusion.22), custom_call_target="InvertDiagBlocksLowerTriangular" | custom-call | tf_op jit(solution)/shard_map/jit(_cho_solve)/triangular_solve | solution.py:31
  58.8 1.5 %cholesky.70 = f32[16,16]{1,0:T(8,128)S(1)} custom-call(f32[16,16]{1,0:T(8,128)S(1)} %fusion.34), custom_call_target="Cholesky" | custom-call | tf_op jit(solution)/shard_map/jit(cholesky)/cholesky | solution.py:31
  60.4 0.7 compare_reduce_fusion.1
  61.0 0.6 fusion.23
  61.7 1.2 %custom-call.10 = f32[1,16,16]{1,2,0:T(8,128)S(1)} custom-call(f32[1,16,16]{2,1,0:T(8,128)S(1)} %fusion.23), custom_call_target="InvertDiagBlocksLowerTriangular" | custom-call | tf_op jit(solution)/shard_map/jit(_cho_solve)/triangular_solve | solution.py:31
  63.6 0.7 pad_maximum_fusion.1.dir_ref
  64.3 17.5 %shard_map.123 = f32[16,2048]{1,0:T(8,128)} custom-call(f32[2048,128]{1,0:T(8,128)} %copy.14.sum_ref, bf16[64,2048]{1,0:T(8,128)(2,1)} %slice.47.out_emb_ref, f32[1,2048]{1,0:T(1,128)} %bitcast.76, f32[4,2048]{1,0:T(4,128)} %fusion.20.out_fid_ref, bf16[32,2048]{1,0:T(8,128)(2,1)} %pad_maximum_fusion.1.dir_ref, f32[1,1]{1,0:T(1,128)} %bitcast.6.scale_ref), custom_call_target="tpu_custom_call" | custom-call | tf_op jit(solution)/shard_map/pallas_call | solution.py:96
  81.8 1.1 %fusion.8 = f32[16,16]{1,0:T(8,128)S(1)} fusion(f32[16,2048]{1,0:T(8,128)S(1)} %get-tuple-element.10, f32[16,2048]{1,0:T(8,128)} %shard_map.123, f32[]{:T(128)} %bitcast.73), kind=kOutput, calls=%fused_computation.26 | convolution fusion | flops 6356992 | bytes 263172 | tf_op jit(solution)/shard_map/dot_general | solution.py:25
  83.0 1.5 %cholesky.81 = f32[16,16]{1,0:T(8,128)S(1)} custom-call(f32[16,16]{1,0:T(8,128)S(1)} %fusion.29), custom_call_target="Cholesky" | custom-call | tf_op jit(solution)/shard_map/jit(cholesky)/cholesky | solution.py:31
  84.6 0.6 compare_reduce_fusion
  85.2 0.6 fusion.24
  85.9 1.2 %custom-call.11 = f32[1,16,16]{1,2,0:T(8,128)S(1)} custom-call(f32[1,16,16]{2,1,0:T(8,128)S(1)} %fusion.24), custom_call_target="InvertDiagBlocksLowerTriangular" | custom-call | tf_op jit(solution)/shard_map/jit(_cho_solve)/triangular_solve | solution.py:31
  88.7 0.6 dynamic-slice_subtract_fusion
  (50 shorter events, 6.3 us)
Async XLA Ops:
  0.6 1.4 %copy-start = (bf16[512,512]{1,0:T(8,128)(2,1)S(1)}, bf16[512,512]{1,0:T(8,128)(2,1)}, u32[]{:S(2)}) copy-start(bf16[512,512]{1,0:T(8,128)(2,1)} %param.18) | copy-start | bytes 1572868
  0.6 1.3 %copy-start.6 = (f32[512]{0:T(512)S(1)}, f32[512]{0:T(512)}, u32[]{:S(2)}) copy-start(f32[512]{0:T(512)} %param.19) | copy-start | bytes 6148
  0.7 1.3 %copy-start.5 = (bf16[512,64]{0,1:T(8,128)(2,1)S(1)}, bf16[512,64]{0,1:T(8,128)(2,1)}, u32[]{:S(2)}) copy-start(bf16[512,64]{0,1:T(8,128)(2,1)} %param.20) | copy-start | bytes 196612
  2.0 0.7 copy-start.8
  2.0 0.7 copy-start.4
  28.1 0.6 copy-start.3
  30.1 0.7 copy-start.7
  57.3 0.9 %copy-start.2 = (f32[16,2048]{1,0:T(8,128)S(1)}, f32[16,2048]{1,0:T(8,128)}, u32[]{:S(2)}) copy-start(f32[16,2048]{1,0:T(8,128)} %shard_map.122) | copy-start | bytes 393220
  87.4 0.9 %copy-start.1 = (f32[16,2048]{1,0:T(8,128)S(1)}, f32[16,2048]{1,0:T(8,128)}, u32[]{:S(2)}) copy-start(f32[16,2048]{1,0:T(8,128)} %shard_map.123) | copy-start | bytes 393220

commit v8 on v5

--- a/solution.py
+++ b/solution.py
@@ -42,6 +42,24 @@
     return jnp.dot(fidelity, onehot, precision=lax.Precision.HIGHEST)
 
 
+def split_two(values):
+    high = lax.reduce_precision(values, exponent_bits=8, mantissa_bits=7)
+    return high.astype(jnp.bfloat16), (values - high).astype(jnp.bfloat16)
+
+
+def split_product(direction, kernel):
+    count = direction.shape[0]
+    d_high, d_low = split_two(direction)
+    k_high, k_low = split_two(kernel)
+    dims = (((1,), (1,)), ((), ()))
+    by_high = lax.dot_general(
+        jnp.concatenate([d_high, d_low], axis=0), k_high, dims,
+        preferred_element_type=jnp.float32,
+    )
+    by_low = lax.dot_general(d_high, k_low, dims, preferred_element_type=jnp.float32)
+    return (by_high[:count] + by_high[count:]) + by_low
+
+
 def kernel_image(embedding, squares, rung_value, col_fidelity, inverse_scale, direction):
     count = embedding.shape[1]
     row_block = block_size(count, 2048)
@@ -69,9 +87,7 @@
                     rows_match[:, level : level + 1], cols_fidelity[level][None, :], tile_fidelity
                 )
             kernel = jnp.exp(-inverse_scale[0] * distance) * tile_fidelity
-            contribution = lax.dot_general(
-                cols_direction, kernel, (((1,), (1,)), ((), ())), precision=lax.Precision.HIGH
-            )
+            contribution = split_product(cols_direction, kernel)
             return (running + contribution, None)
 
         start_value = jnp.zeros((direction.shape[0], row_block), jnp.float32)

time: 79 us -> 73.7 us (0.933)
  local copies, waits for them, and re-layouts: 5.42 us -> 1.02 us
  matrix products: 31.6 us -> 30.5 us
    unnamed x4 -> x6, local copies, waits for them, and re-layouts: 5.07 us -> 0.67 us
    dot_general x2 -> x4, matrix products: 17.5 us -> 16.4 us  [the longest x2 11.7 us: split_product(): lax.dot_general(jnp.concatenate([d_high, d_low], axis=0), k_high, dims, p...]
where the time goes in v8:
time: 73.7 us; the launch traced here: 73.3 us
  matrix products  30.5 us (41%)
  blocking collectives  25.3 us (34%)
  other arithmetic  14.4 us (20%)
  between operations  2.16 us (3%)
  local copies, waits for them, and re-layouts  1.02 us (1%)
    all_gather x1, blocking collectives, on_device(): gathered = lax.all_gather(packed, ('row', 'col'), axis=1, tiled=True)  25.3 us
    dot_general x2, matrix products, split_product(): lax.dot_general(jnp.concatenate([d_high, d_low], axis=0), k_high, dims, p...  11.7 us
    dot_general x3, matrix products, left_product(): lax.dot_general(weights, values, (((0,), (0,)), ((), ())), preferred_elem...  9.38 us
    another operation x9, other arithmetic, solve_spd(): jnp.linalg.cholesky(matrix)  6.65 us
    another operation x6, other arithmetic, solve_spd(): jax.scipy.linalg.cho_solve((jnp.linalg.cholesky(matrix), True), right_side)  5.67 us
    dot_general x2, matrix products, split_product(): lax.dot_general(d_high, k_low, dims, preferred_element_type=jnp.float32)  4.75 us

profile of v8, /device:TPU:0, one launch (start us, length us, event | category | flops | bytes accessed | tf_op | source)
XLA Modules:
  0.0 73.3 jit_solution(13817716047501878236)
XLA Ops:
  2.0 0.7 convert_bitcast_fusion
  2.7 0.9 %convolution_add_fusion.5 = f32[4,4]{1,0:T(4,128)S(1)} fusion(f32[4,4]{1,0:T(4,128)} %param.22), kind=kOutput, calls=%fused_computation.17 | convolution fusion | flops 848 | bytes 128 | tf_op jit(solution)/shard_map/dot_general | solution.py:11
  3.5 1.3 %multiply_convert_fusion.1 = bf16[512,128]{1,0:T(8,128)(2,1)S(1)} fusion(bf16[164,512]{1,0:T(8,128)(2,1)} %param.16, bf16[164,128]{1,0:T(8,128)(2,1)} %param.14, f32[512]{0:T(512)} %param.17), kind=kOutput, calls=%fused_computation.21 | convolution fusion | flops 21889024 | bytes 343040 | tf_op jit(solution)/shard_map/dot_general | solution.py:17
  4.8 1.4 %fusion.8 = f32[64,128]{1,0:T(8,128)S(1)} fusion(bf16[512,64]{0,1:T(8,128)(2,1)} %param.20, bf16[512,128]{1,0:T(8,128)(2,1)S(1)} %multiply_convert_fusion.1, bf16[512,512]{1,0:T(8,128)(2,1)S(1)} %copy-done, f32[512]{0:T(512)} %param.19), kind=kOutput, calls=%fused_computation.16 | convolution fusion | flops 75898880 | bytes 755712 | tf_op jit(solution)/shard_map/dot_general | solution.py:17
  6.2 0.7 pad_maximum_fusion
  6.9 25.3 %all_gather.3 = f32[81,2048]{1,0:T(8,128)S(1)} all-gather(f32[81,128]{1,0:T(8,128)S(1)} %pad_maximum_fusion), channel_id=1, replica_groups=mesh['task'=2,'row'=4,'col'=4] {'row','col'}, dimensions={1}, use_global_device_ids=true | all-gather | bytes 705024 | tf_op jit(solution)/shard_map/all_gather | solution.py:134
  32.4 1.5 %cholesky.70 = f32[16,16]{1,0:T(8,128)S(1)} custom-call(f32[16,16]{1,0:T(8,128)S(1)} %fusion.40), custom_call_target="Cholesky" | custom-call | tf_op jit(solution)/shard_map/jit(cholesky)/cholesky | solution.py:29
  34.0 0.7 compare_reduce_fusion.1
  34.7 0.7 fusion.29
  35.4 1.2 %custom-call.10 = f32[1,16,16]{1,2,0:T(8,128)S(1)} custom-call(f32[1,16,16]{2,1,0:T(8,128)S(1)} %fusion.29), custom_call_target="InvertDiagBlocksLowerTriangular" | custom-call | tf_op jit(solution)/shard_map/jit(_cho_solve)/triangular_solve | solution.py:29
  37.1 6.8 %select_multiply_fusion = f32[2048,2048]{1,0:T(8,128)S(1)} fusion(f32[2048]{0:T(1024)S(1)} %bitcast.82, f32[2048]{0:T(1024)S(1)} %bitcast.83, f32[2048]{0:T(1024)S(1)} %bitcast.84, f32[2048]{0:T(1024)S(1)} %bitcast.81, f32[2048]{0:T(1024)S(1)} %multiply_reduce_fusion, f32[]{:T(128)} %bitcast.3, pred[2048]{0:T(1024)(128)(4,1)S(1)} %get-tuple-element.111, ...), kind=kOutput, calls=%fused_computation.3 | convolution fusion | flops 570425344 | bytes 17094660 | tf_op jit(solution)/shard_map/while/body/eval_jaxpr/while/body/eval_jaxpr/dot_general | solution.py:17
  43.8 2.6 %fusion.2 = f32[32,2048]{1,0:T(8,128)S(1)} fusion(f32[2048,2048]{1,0:T(8,128)S(1)} %select_multiply_fusion, bf16[16,2048]{1,0:T(8,128)(2,1)S(1)} %get-tuple-element.113, bf16[16,2048]{1,0:T(8,128)(2,1)S(1)} %get-tuple-element.114), kind=kOutput, calls=%fused_computation.5 | convolution fusion | flops 277086208 | bytes 17170432 | tf_op jit(solution)/shard_map/while/body/eval_jaxpr/while/body/eval_jaxpr/dot_general | solution.py:55
  46.4 2.5 %fusion.4 = f32[16,2048]{1,0:T(8,128)S(1)} fusion(bf16[16,2048]{1,0:T(8,128)(2,1)S(1)} %get-tuple-element.114, f32[2048,2048]{1,0:T(8,128)S(1)} %select_multiply_fusion, f32[32,2048]{1,0:T(8,128)S(1)} %fusion.2, f32[81,2048]{1,0:T(8,128)S(1)} %all_gather.3, f32[]{:T(128)} %bitcast.77), kind=kOutput, calls=%fused_computation.11 | convolution fusion | flops 146931712 | bytes 17367044 | tf_op jit(solution)/shard_map/while/body/eval_jaxpr/while/body/eval_jaxpr/dot_general | solution.py:59
  48.9 0.6 copy-done.1
  49.9 1.5 %cholesky.59 = f32[16,16]{1,0:T(8,128)S(1)} custom-call(f32[16,16]{1,0:T(8,128)S(1)} %fusion.45), custom_call_target="Cholesky" | custom-call | tf_op jit(solution)/shard_map/jit(cholesky)/cholesky | solution.py:29
  51.4 0.6 compare_reduce_fusion.2
  52.1 0.6 fusion.28
  52.7 1.2 %custom-call.9 = f32[1,16,16]{1,2,0:T(8,128)S(1)} custom-call(f32[1,16,16]{2,1,0:T(8,128)S(1)} %fusion.28), custom_call_target="InvertDiagBlocksLowerTriangular" | custom-call | tf_op jit(solution)/shard_map/jit(_cho_solve)/triangular_solve | solution.py:29
  55.9 9.1 %fusion.1 = f32[32,2048]{1,0:T(8,128)S(1)} fusion(f32[2048,2048]{1,0:T(8,128)} %copy-done.1, bf16[16,2048]{1,0:T(8,128)(2,1)S(1)} %get-tuple-element.134, bf16[16,2048]{1,0:T(8,128)(2,1)S(1)} %get-tuple-element.135), kind=kOutput, calls=%fused_computation.4 | convolution fusion | flops 277086208 | bytes 17170432 | tf_op jit(solution)/shard_map/while/body/eval_jaxpr/while/body/eval_jaxpr/dot_general | solution.py:55
  65.0 2.3 %fusion.3 = f32[16,2048]{1,0:T(8,128)S(1)} fusion(bf16[16,2048]{1,0:T(8,128)(2,1)S(1)} %get-tuple-element.135, f32[2048,2048]{1,0:T(8,128)S(1)} %copy-done.2, f32[32,2048]{1,0:T(8,128)S(1)} %fusion.1, f32[16,2048]{1,0:T(8,128)S(1)} %get-tuple-element.140, f32[]{:T(128)} %bitcast.78), kind=kOutput, calls=%fused_computation.9 | convolution fusion | flops 146931712 | bytes 17367044 | tf_op jit(solution)/shard_map/while/body/eval_jaxpr/while/body/eval_jaxpr/dot_general | solution.py:59
  67.6 1.5 %cholesky.81 = f32[16,16]{1,0:T(8,128)S(1)} custom-call(f32[16,16]{1,0:T(8,128)S(1)} %fusion.35), custom_call_target="Cholesky" | custom-call | tf_op jit(solution)/shard_map/jit(cholesky)/cholesky | solution.py:29
  69.2 0.6 compare_reduce_fusion
  69.8 0.6 fusion.30
  70.5 1.2 %custom-call.11 = f32[1,16,16]{1,2,0:T(8,128)S(1)} custom-call(f32[1,16,16]{2,1,0:T(8,128)S(1)} %fusion.30), custom_call_target="InvertDiagBlocksLowerTriangular" | custom-call | tf_op jit(solution)/shard_map/jit(_cho_solve)/triangular_solve | solution.py:29
  (37 shorter events, 5.0 us)
Async XLA Ops:
  0.6 4.2 %copy-start = (bf16[512,512]{1,0:T(8,128)(2,1)S(1)}, bf16[512,512]{1,0:T(8,128)(2,1)}, u32[]{:S(2)}) copy-start(bf16[512,512]{1,0:T(8,128)(2,1)} %param.18) | copy-start | bytes 1572868
  43.8 5.7 %copy-start.1 = (f32[2048,2048]{1,0:T(8,128)}, f32[2048,2048]{1,0:T(8,128)S(1)}, u32[]{:S(2)}) copy-start(f32[2048,2048]{1,0:T(8,128)S(1)} %select_multiply_fusion) | copy-start | bytes 50331652
  53.9 11.1 %copy-start.2 = (f32[2048,2048]{1,0:T(8,128)S(1)}, f32[2048,2048]{1,0:T(8,128)}, u32[]{:S(2)}) copy-start(f32[2048,2048]{1,0:T(8,128)} %copy-done.1) | copy-start | bytes 50331652

commit v9 on v8

--- a/solution.py
+++ b/solution.py
@@ -2,6 +2,7 @@
 import jax.numpy as jnp
 from jax import lax
 from jax.sharding import PartitionSpec as P
+from jax.experimental import pallas as pl
 
 ITERS = 2
 
@@ -25,8 +26,50 @@
     )
 
 
+def cholesky_solve_block(matrix_ref, right_ref, out_ref):
+    size = matrix_ref.shape[0]
+    work = matrix_ref[...]
+    rows = lax.broadcasted_iota(jnp.int32, (size, size), 0)
+    cols = lax.broadcasted_iota(jnp.int32, (size, size), 1)
+    row_index = rows[:, 0:1]
+    col_index = cols[0:1, :]
+    right_rows = lax.broadcasted_iota(jnp.int32, right_ref.shape, 0)
+    lower = jnp.zeros((size, size), jnp.float32)
+    upper = jnp.zeros((size, size), jnp.float32)
+    for j in range(size):
+        column = jnp.sum(jnp.where(cols == j, work, 0.0), axis=1, keepdims=True)
+        row = jnp.sum(jnp.where(rows == j, work, 0.0), axis=0, keepdims=True)
+        pivot = jnp.sum(jnp.where(col_index == j, row, 0.0), axis=1, keepdims=True)
+        root = jnp.sqrt(pivot)
+        column = jnp.where(row_index >= j, column / root, 0.0)
+        row = jnp.where(col_index >= j, row / root, 0.0)
+        lower = lower + jnp.where(cols == j, column, 0.0)
+        upper = upper + jnp.where(rows == j, row, 0.0)
+        work = work - column * row
+    solved = right_ref[...]
+    for j in range(size):
+        column = jnp.sum(jnp.where(cols == j, lower, 0.0), axis=1, keepdims=True)
+        diagonal = jnp.sum(jnp.where(row_index == j, column, 0.0), axis=0, keepdims=True)
+        picked = jnp.sum(jnp.where(right_rows == j, solved, 0.0), axis=0, keepdims=True)
+        value = picked / diagonal
+        below = jnp.where(row_index > j, column, 0.0)
+        solved = jnp.where(right_rows == j, value, solved - below * value)
+    for j in reversed(range(size)):
+        column = jnp.sum(jnp.where(cols == j, upper, 0.0), axis=1, keepdims=True)
+        diagonal = jnp.sum(jnp.where(row_index == j, column, 0.0), axis=0, keepdims=True)
+        picked = jnp.sum(jnp.where(right_rows == j, solved, 0.0), axis=0, keepdims=True)
+        value = picked / diagonal
+        above = jnp.where(row_index < j, column, 0.0)
+        solved = jnp.where(right_rows == j, value, solved - above * value)
+    out_ref[...] = solved
+
+
 def solve_spd(matrix, right_side):
-    return jax.scipy.linalg.cho_solve((jnp.linalg.cholesky(matrix), True), right_side)
+    symmetric = (matrix + matrix.T) / 2.0
+    return pl.pallas_call(
+        cholesky_solve_block,
+        out_shape=jax.ShapeDtypeStruct(right_side.shape, jnp.float32),
+    )(symmetric, right_side)
 
 
 def block_size(total_count, largest):

time: 73.7 us -> 77.2 us (1.047)
  other arithmetic: 14.4 us -> 4.02 us
  Pallas kernels: 0 us -> 10.2 us
  matrix products: 30.5 us -> 33.4 us
    another operation x15 -> x0, other arithmetic: 12.3 us -> none  [the longest x9 6.65 us: solve_spd(): jnp.linalg.cholesky(matrix)]
    pallas_call x0 -> x3, Pallas kernels: none -> 10.2 us  [solve_spd(): pl.pallas_call(cholesky_solve_block, out_shape=jax.ShapeDtypeStruct(right...]
    div x3, other arithmetic: 0.02 us -> 1.95 us  [solve_spd(): symmetric = (matrix + matrix.T) / 2.0]
    dot_general x2, matrix products: 0.64 us -> 2.17 us  [on_device(): jnp.dot(step_matrix.T, direction, precision=lax.Precision.HIGHEST)]
    dot_general x2, matrix products: 0.66 us -> 2.02 us  [on_device(): jnp.dot(step_matrix.T, image, precision=lax.Precision.HIGHEST)]
    another operation x6 -> x0, matrix products: 1.08 us -> none  [solve_spd(): jax.scipy.linalg.cho_solve((jnp.linalg.cholesky(matrix), True), right_side)]
    dot_general x1, matrix products: 0.33 us -> 1.28 us  [on_device(): jnp.dot(update_matrix.T, direction, precision=lax.Precision.HIGHEST)]
where the time goes in v9:
time: 77.2 us; the launch traced here: 76.3 us
  matrix products  33.4 us (43%)
  blocking collectives  25.3 us (33%)
  Pallas kernels  10.2 us (13%)
  other arithmetic  4.02 us (5%)
  between operations  2.14 us (3%)
  local copies, waits for them, and re-layouts  1.25 us (2%)
    all_gather x1, blocking collectives, on_device(): gathered = lax.all_gather(packed, ('row', 'col'), axis=1, tiled=True)  25.3 us
    dot_general x2, matrix products, split_product(): lax.dot_general(jnp.concatenate([d_high, d_low], axis=0), k_high, dims, p...  11.3 us
    pallas_call x3, Pallas kernels, solve_spd(): pl.pallas_call(cholesky_solve_block, out_shape=jax.ShapeDtypeStruct(right...  10.2 us
    dot_general x3, matrix products, left_product(): lax.dot_general(weights, values, (((0,), (0,)), ((), ())), preferred_elem...  9.43 us
    dot_general x2, matrix products, split_product(): lax.dot_general(d_high, k_low, dims, preferred_element_type=jnp.float32)  4.57 us
    dot_general x2, matrix products, on_device(): jnp.dot(step_matrix.T, direction, precision=lax.Precision.HIGHEST)  2.17 us
    dot_general x2, matrix products, on_device(): jnp.dot(step_matrix.T, image, precision=lax.Precision.HIGHEST)  2.02 us
    div x3, other arithmetic, solve_spd(): symmetric = (matrix + matrix.T) / 2.0  1.95 us

profile of v9, /device:TPU:0, one launch (start us, length us, event | category | flops | bytes accessed | tf_op | source)
XLA Modules:
  0.0 76.3 jit_solution(7620974131996138602)
XLA Ops:
  2.0 0.7 convert_bitcast_fusion
  2.7 0.9 %convolution_add_fusion.5 = f32[4,4]{1,0:T(4,128)S(1)} fusion(f32[4,4]{1,0:T(4,128)} %param.19), kind=kOutput, calls=%fused_computation.17 | convolution fusion | flops 848 | bytes 128 | tf_op jit(solution)/shard_map/dot_general | solution.py:12
  3.5 1.3 %multiply_convert_fusion.1 = bf16[512,128]{1,0:T(8,128)(2,1)S(1)} fusion(bf16[164,512]{1,0:T(8,128)(2,1)} %param.13, bf16[164,128]{1,0:T(8,128)(2,1)} %param.11, f32[512]{0:T(512)} %param.14), kind=kOutput, calls=%fused_computation.21 | convolution fusion | flops 21889024 | bytes 343040 | tf_op jit(solution)/shard_map/dot_general | solution.py:18
  4.8 1.4 %fusion.8 = f32[64,128]{1,0:T(8,128)S(1)} fusion(bf16[512,64]{0,1:T(8,128)(2,1)} %param.17, bf16[512,128]{1,0:T(8,128)(2,1)S(1)} %multiply_convert_fusion.1, bf16[512,512]{1,0:T(8,128)(2,1)S(1)} %copy-done, f32[512]{0:T(512)} %param.16), kind=kOutput, calls=%fused_computation.16 | convolution fusion | flops 75898880 | bytes 755712 | tf_op jit(solution)/shard_map/dot_general | solution.py:18
  6.2 0.7 pad_maximum_fusion
  6.9 25.3 %all_gather.3 = f32[81,2048]{1,0:T(8,128)S(1)} all-gather(f32[81,128]{1,0:T(8,128)S(1)} %pad_maximum_fusion), channel_id=1, replica_groups=mesh['task'=2,'row'=4,'col'=4] {'row','col'}, dimensions={1}, use_global_device_ids=true | all-gather | bytes 705024 | tf_op jit(solution)/shard_map/all_gather | solution.py:177
  33.5 6.8 %select_multiply_fusion = f32[2048,2048]{1,0:T(8,128)S(1)} fusion(f32[2048]{0:T(1024)S(1)} %bitcast.55, f32[2048]{0:T(1024)S(1)} %bitcast.56, f32[2048]{0:T(1024)S(1)} %bitcast.57, f32[2048]{0:T(1024)S(1)} %bitcast.54, f32[2048]{0:T(1024)S(1)} %multiply_reduce_fusion, f32[]{:T(128)} %bitcast.3, pred[2048]{0:T(1024)(128)(4,1)S(1)} %get-tuple-element.109, ...), kind=kOutput, calls=%fused_computation.3 | convolution fusion | flops 570425344 | bytes 17094660 | tf_op jit(solution)/shard_map/while/body/eval_jaxpr/while/body/eval_jaxpr/dot_general | solution.py:18
  40.4 2.6 %fusion.2 = f32[32,2048]{1,0:T(8,128)S(1)} fusion(f32[2048,2048]{1,0:T(8,128)S(1)} %select_multiply_fusion, bf16[16,2048]{1,0:T(8,128)(2,1)S(1)} %get-tuple-element.111, bf16[16,2048]{1,0:T(8,128)(2,1)S(1)} %get-tuple-element.112), kind=kOutput, calls=%fused_computation.5 | convolution fusion | flops 277086208 | bytes 17170432 | tf_op jit(solution)/shard_map/while/body/eval_jaxpr/while/body/eval_jaxpr/dot_general | solution.py:98
  42.9 2.3 %fusion.4 = f32[16,2048]{1,0:T(8,128)S(1)} fusion(bf16[16,2048]{1,0:T(8,128)(2,1)S(1)} %get-tuple-element.112, f32[2048,2048]{1,0:T(8,128)S(1)} %select_multiply_fusion, f32[32,2048]{1,0:T(8,128)S(1)} %fusion.2, f32[81,2048]{1,0:T(8,128)S(1)} %all_gather.3, f32[]{:T(128)} %bitcast.50), kind=kOutput, calls=%fused_computation.11 | convolution fusion | flops 146931712 | bytes 17367044 | tf_op jit(solution)/shard_map/while/body/eval_jaxpr/while/body/eval_jaxpr/dot_general | solution.py:102
  45.2 0.8 %copy-done.1 = f32[2048,2048]{1,0:T(8,128)} copy-done((f32[2048,2048]{1,0:T(8,128)}, f32[2048,2048]{1,0:T(8,128)S(1)}, u32[]{:S(2)}) %copy-start.1) | copy-done | bytes 16777240
  46.4 0.7 fusion.30.matrix_ref
  47.0 3.5 %shard_map.122 = f32[16,16]{1,0:T(8,128)} custom-call(f32[16,16]{1,0:T(8,128)} %fusion.30.matrix_ref, f32[16,16]{1,0:T(8,128)} %copy-done.3), custom_call_target="tpu_custom_call" | custom-call | tf_op jit(solution)/shard_map/pallas_call | solution.py:69
  50.5 1.0 %convolution_subtract_fusion = f32[16,2048]{1,0:T(8,128)S(1)} fusion(f32[16,16]{1,0:T(8,128)} %shard_map.122, f32[16,2048]{1,0:T(8,128)S(1)} %fusion.4, f32[81,2048]{1,0:T(8,128)S(1)} %all_gather.3), kind=kOutput, calls=%fused_computation.7 | convolution fusion | flops 6324224 | bytes 394240 | tf_op jit(solution)/shard_map/dot_general | solution.py:197
  51.5 0.9 %fusion.38.right_ref = f32[16,16]{1,0:T(8,128)} fusion(f32[16,2048]{1,0:T(8,128)S(1)} %convolution_subtract_fusion), kind=kOutput, calls=%fused_computation.71 | convolution fusion | flops 6291456 | bytes 132096 | tf_op jit(solution)/shard_map/dot_general | solution.py:24
  52.5 3.3 %shard_map.123 = f32[16,16]{1,0:T(8,128)} custom-call(f32[16,16]{1,0:T(8,128)} %fusion.29.matrix_ref, f32[16,16]{1,0:T(8,128)} %fusion.38.right_ref), custom_call_target="tpu_custom_call" | custom-call | tf_op jit(solution)/shard_map/pallas_call | solution.py:69
  55.8 1.2 %fusion.20 = f32[16,2048]{1,0:T(8,128)S(1)} fusion(f32[16,16]{1,0:T(8,128)} %shard_map.122, f32[81,2048]{1,0:T(8,128)S(1)} %all_gather.3), kind=kOutput, calls=%fused_computation.39 | convolution fusion | flops 6291456 | bytes 263168 | tf_op jit(solution)/shard_map/dot_general | solution.py:196
  56.9 1.3 %fusion.10 = (bf16[16,2048]{1,0:T(8,128)(2,1)S(1)}, bf16[16,2048]{1,0:T(8,128)(2,1)S(1)}, f32[16,2048]{1,0:T(8,128)S(1)}) fusion(f32[16,2048]{1,0:T(8,128)S(1)} %convolution_subtract_fusion, f32[16,16]{1,0:T(8,128)} %shard_map.123, f32[81,2048]{1,0:T(8,128)S(1)} %all_gather.3), kind=kOutput, calls=%fused_computation.27 | convolution fusion | flops 6455296 | bytes 525312 | tf_op jit(solution)/shard_map/dot_general | solution.py:201
  58.2 8.8 %fusion.1 = f32[32,2048]{1,0:T(8,128)S(1)} fusion(f32[2048,2048]{1,0:T(8,128)} %copy-done.1, bf16[16,2048]{1,0:T(8,128)(2,1)S(1)} %get-tuple-element.113, bf16[16,2048]{1,0:T(8,128)(2,1)S(1)} %get-tuple-element.114), kind=kOutput, calls=%fused_computation.4 | convolution fusion | flops 277086208 | bytes 17170432 | tf_op jit(solution)/shard_map/while/body/eval_jaxpr/while/body/eval_jaxpr/dot_general | solution.py:98
  67.0 2.3 %fusion.3 = f32[16,2048]{1,0:T(8,128)S(1)} fusion(bf16[16,2048]{1,0:T(8,128)(2,1)S(1)} %get-tuple-element.114, f32[2048,2048]{1,0:T(8,128)S(1)} %copy-done.2, f32[32,2048]{1,0:T(8,128)S(1)} %fusion.1, f32[16,2048]{1,0:T(8,128)S(1)} %get-tuple-element.138, f32[]{:T(128)} %bitcast.51), kind=kOutput, calls=%fused_computation.9 | convolution fusion | flops 146931712 | bytes 17367044 | tf_op jit(solution)/shard_map/while/body/eval_jaxpr/while/body/eval_jaxpr/dot_general | solution.py:102
  69.6 0.7 fusion.28.matrix_ref
  70.3 3.3 %shard_map.124 = f32[16,16]{1,0:T(8,128)} custom-call(f32[16,16]{1,0:T(8,128)} %fusion.28.matrix_ref, f32[16,16]{1,0:T(8,128)} %fusion.38.right_ref), custom_call_target="tpu_custom_call" | custom-call | tf_op jit(solution)/shard_map/pallas_call | solution.py:69
  73.6 1.0 %fusion.41 = f32[16,2048]{1,0:T(8,128)S(1)} fusion(f32[16,16]{1,0:T(8,128)} %shard_map.124, f32[16,2048]{1,0:T(8,128)S(1)} %fusion.3), kind=kOutput, calls=%fused_computation.74 | convolution fusion | flops 6291456 | bytes 263168 | tf_op jit(solution)/shard_map/dot_general | solution.py:197
  74.6 1.0 %fusion.40 = f32[16,2048]{1,0:T(8,128)S(1)} fusion(f32[16,16]{1,0:T(8,128)} %shard_map.124, f32[16,2048]{1,0:T(8,128)S(1)} %get-tuple-element.138), kind=kOutput, calls=%fused_computation.73 | convolution fusion | flops 6291456 | bytes 263168 | tf_op jit(solution)/shard_map/dot_general | solution.py:196
  75.6 0.6 dynamic-slice_subtract_fusion
  (21 shorter events, 2.0 us)
Async XLA Ops:
  0.6 4.2 %copy-start = (bf16[512,512]{1,0:T(8,128)(2,1)S(1)}, bf16[512,512]{1,0:T(8,128)(2,1)}, u32[]{:S(2)}) copy-start(bf16[512,512]{1,0:T(8,128)(2,1)} %param.15) | copy-start | bytes 1572868
  32.4 8.0 %copy-start.3 = (f32[16,16]{1,0:T(8,128)}, f32[16,16]{1,0:T(8,128)S(1)}, u32[]{:S(2)}) copy-start(f32[16,16]{1,0:T(8,128)S(1)} %fusion.22.right_ref) | copy-start | bytes 3076
  40.3 5.7 %copy-start.1 = (f32[2048,2048]{1,0:T(8,128)}, f32[2048,2048]{1,0:T(8,128)S(1)}, u32[]{:S(2)}) copy-start(f32[2048,2048]{1,0:T(8,128)S(1)} %select_multiply_fusion) | copy-start | bytes 50331652
  55.8 11.2 %copy-start.2 = (f32[2048,2048]{1,0:T(8,128)S(1)}, f32[2048,2048]{1,0:T(8,128)}, u32[]{:S(2)}) copy-start(f32[2048,2048]{1,0:T(8,128)} %copy-done.1) | copy-start | bytes 50331652

commit v10 on v8

--- a/solution.py
+++ b/solution.py
@@ -48,9 +48,13 @@
 
 
 def split_product(direction, kernel):
+    return pieces_product(direction, split_two(kernel))
+
+
+def pieces_product(direction, pieces):
     count = direction.shape[0]
     d_high, d_low = split_two(direction)
-    k_high, k_low = split_two(kernel)
+    k_high, k_low = pieces
     dims = (((1,), (1,)), ((), ()))
     by_high = lax.dot_general(
         jnp.concatenate([d_high, d_low], axis=0), k_high, dims,
@@ -60,7 +64,20 @@
     return (by_high[:count] + by_high[count:]) + by_low
 
 
-def kernel_image(embedding, squares, rung_value, col_fidelity, inverse_scale, direction):
+def whole_kernel_pieces(embedding, squares, rung_value, col_fidelity, inverse_scale):
+    count = embedding.shape[1]
+    if block_size(count, 2048) != count:
+        return None
+    direction = jnp.zeros((1, count), jnp.float32)
+    (kernel,) = kernel_image(
+        embedding, squares, rung_value, col_fidelity, inverse_scale, direction, whole=True
+    )
+    return lax.optimization_barrier(split_two(kernel))
+
+
+def kernel_image(
+    embedding, squares, rung_value, col_fidelity, inverse_scale, direction, whole=False
+):
     count = embedding.shape[1]
     row_block = block_size(count, 2048)
     col_block = block_size(count, 2048)
@@ -87,15 +104,22 @@
                     rows_match[:, level : level + 1], cols_fidelity[level][None, :], tile_fidelity
                 )
             kernel = jnp.exp(-inverse_scale[0] * distance) * tile_fidelity
+            if whole:
+                return (running + (kernel,), None)
             contribution = split_product(cols_direction, kernel)
             return (running + contribution, None)
 
+        if whole:
+            result, unused = one_col_block((), 0)
+            return result
         start_value = jnp.zeros((direction.shape[0], row_block), jnp.float32)
         result, unused = lax.scan(
             one_col_block, start_value, jnp.arange(count // col_block, dtype=jnp.int32)
         )
         return result
 
+    if whole:
+        return one_row_block(0)
     stacked = lax.map(one_row_block, jnp.arange(count // row_block, dtype=jnp.int32))
     return jnp.transpose(stacked, (1, 0, 2)).reshape(direction.shape[0], count)
 
@@ -139,15 +163,19 @@
     squares = jnp.sum(jnp.square(gathered[:emb_rows]), axis=0)
     col_fidelity = rung_fidelity(fidelity, all_rung)
 
+    pieces = whole_kernel_pieces(all_embedding, squares, all_rung, col_fidelity, inverse_scale)
     solution = jnp.zeros_like(all_targets)
     residual = all_targets
     direction = all_targets
     gram = outer_gram(residual, residual)
     for iteration in range(ITERS):
-        image = (
-            kernel_image(all_embedding, squares, all_rung, col_fidelity, inverse_scale, direction)
-            + noise_var[0] * direction
-        )
+        if pieces is None:
+            product = kernel_image(
+                all_embedding, squares, all_rung, col_fidelity, inverse_scale, direction
+            )
+        else:
+            product = pieces_product(direction, pieces)
+        image = product + noise_var[0] * direction
         curvature = outer_gram(direction, image)
         step_matrix = solve_spd(curvature, gram)
         solution = solution + jnp.dot(step_matrix.T, direction, precision=lax.Precision.HIGHEST)

time: 73.7 us -> 73.9 us (level)
    dot_general x3, matrix products: 9.38 us -> 12.3 us  [left_product(): lax.dot_general(weights, values, (((0,), (0,)), ((), ())), preferred_elem...]
    dot_general x4, matrix products: 16.4 us -> 13.5 us  [the longest x2 8.97 us: pieces_product(): lax.dot_general(jnp.concatenate([d_high, d_low], axis=0), k_high, dims, p...]
where the time goes in v10:
time: 73.9 us; the launch traced here: 73.6 us
  matrix products  30.5 us (41%)
  blocking collectives  25.3 us (34%)
  other arithmetic  14.4 us (19%)
  between operations  2.17 us (3%)
  local copies, waits for them, and re-layouts  1.21 us (2%)
    all_gather x1, blocking collectives, on_device(): gathered = lax.all_gather(packed, ('row', 'col'), axis=1, tiled=True)  25.3 us
    dot_general x3, matrix products, left_product(): lax.dot_general(weights, values, (((0,), (0,)), ((), ())), preferred_elem...  12.3 us
    dot_general x2, matrix products, pieces_product(): lax.dot_general(jnp.concatenate([d_high, d_low], axis=0), k_high, dims, p...  8.97 us
    another operation x9, other arithmetic, solve_spd(): jnp.linalg.cholesky(matrix)  6.66 us
    another operation x6, other arithmetic, solve_spd(): jax.scipy.linalg.cho_solve((jnp.linalg.cholesky(matrix), True), right_side)  5.67 us
    dot_general x2, matrix products, pieces_product(): lax.dot_general(d_high, k_low, dims, preferred_element_type=jnp.float32)  4.55 us

profile of v10, /device:TPU:0, one launch (start us, length us, event | category | flops | bytes accessed | tf_op | source)
XLA Modules:
  0.0 73.6 jit_solution(12565202867421532595)
XLA Ops:
  2.0 0.7 convert_bitcast_fusion
  2.7 0.9 %convolution_add_fusion.5 = f32[4,4]{1,0:T(4,128)S(1)} fusion(f32[4,4]{1,0:T(4,128)} %param.22), kind=kOutput, calls=%fused_computation.15 | convolution fusion | flops 848 | bytes 128 | tf_op jit(solution)/shard_map/dot_general | solution.py:11
  3.5 1.3 %multiply_convert_fusion.1 = bf16[512,128]{1,0:T(8,128)(2,1)S(1)} fusion(bf16[164,512]{1,0:T(8,128)(2,1)} %param.16, bf16[164,128]{1,0:T(8,128)(2,1)} %param.14, f32[512]{0:T(512)} %param.17), kind=kOutput, calls=%fused_computation.19 | convolution fusion | flops 21889024 | bytes 343040 | tf_op jit(solution)/shard_map/dot_general | solution.py:17
  4.8 1.4 %fusion.4 = f32[64,128]{1,0:T(8,128)S(1)} fusion(bf16[512,64]{0,1:T(8,128)(2,1)} %param.20, bf16[512,128]{1,0:T(8,128)(2,1)S(1)} %multiply_convert_fusion.1, bf16[512,512]{1,0:T(8,128)(2,1)S(1)} %copy-done, f32[512]{0:T(512)} %param.19), kind=kOutput, calls=%fused_computation.14 | convolution fusion | flops 75898880 | bytes 755712 | tf_op jit(solution)/shard_map/dot_general | solution.py:17
  6.2 0.7 pad_maximum_fusion
  6.9 25.3 %all_gather.3 = f32[81,2048]{1,0:T(8,128)S(1)} all-gather(f32[81,128]{1,0:T(8,128)S(1)} %pad_maximum_fusion), channel_id=1, replica_groups=mesh['task'=2,'row'=4,'col'=4] {'row','col'}, dimensions={1}, use_global_device_ids=true | all-gather | bytes 705024 | tf_op jit(solution)/shard_map/all_gather | solution.py:158
  32.4 1.5 %cholesky.70 = f32[16,16]{1,0:T(8,128)S(1)} custom-call(f32[16,16]{1,0:T(8,128)S(1)} %fusion.38), custom_call_target="Cholesky" | custom-call | tf_op jit(solution)/shard_map/jit(cholesky)/cholesky | solution.py:29
  34.0 0.7 compare_reduce_fusion.1
  34.7 0.7 fusion.27
  35.4 1.2 %custom-call.10 = f32[1,16,16]{1,2,0:T(8,128)S(1)} custom-call(f32[1,16,16]{2,1,0:T(8,128)S(1)} %fusion.27), custom_call_target="InvertDiagBlocksLowerTriangular" | custom-call | tf_op jit(solution)/shard_map/jit(_cho_solve)/triangular_solve | solution.py:29
  37.1 9.7 %fusion = (bf16[2048,2048]{1,0:T(8,128)(2,1)S(1)}, bf16[2048,2048]{1,0:T(8,128)(2,1)S(1)}) fusion(f32[2048]{0:T(1024)S(1)} %bitcast.86, f32[2048]{0:T(1024)S(1)} %bitcast.87, pred[2048]{0:T(1024)(128)(4,1)S(1)} %get-tuple-element.9, f32[2048]{0:T(1024)S(1)} %bitcast.88, pred[2048]{0:T(1024)(128)(4,1)S(1)} %get-tuple-element.10, f32[2048]{0:T(1024)S(1)} %bitcast.85, ...), kind=kOutput, calls=%fused_computation.2 | convolution fusion | flops 587202560 | bytes 17094660 | tf_op jit(solution)/shard_map/dot_general | solution.py:17
  46.8 2.6 %fusion.7 = f32[32,2048]{1,0:T(8,128)S(1)} fusion(bf16[2048,2048]{1,0:T(8,128)(2,1)S(1)} %get-tuple-element.6, bf16[16,2048]{1,0:T(8,128)(2,1)S(1)} %get-tuple-element.13, bf16[16,2048]{1,0:T(8,128)(2,1)S(1)} %get-tuple-element.14), kind=kOutput, calls=%fused_computation.28 | convolution fusion | flops 268697600 | bytes 8781824 | tf_op jit(solution)/shard_map/dot_general | solution.py:59
  49.4 2.3 %fusion.2 = f32[16,2048]{1,0:T(8,128)S(1)} fusion(bf16[16,2048]{1,0:T(8,128)(2,1)S(1)} %get-tuple-element.14, bf16[2048,2048]{1,0:T(8,128)(2,1)S(1)} %get-tuple-element.7, f32[32,2048]{1,0:T(8,128)S(1)} %fusion.7, f32[81,2048]{1,0:T(8,128)S(1)} %all_gather.3, f32[]{:T(128)} %bitcast.81), kind=kOutput, calls=%fused_computation.9 | convolution fusion | flops 134348800 | bytes 8978436 | tf_op jit(solution)/shard_map/dot_general | solution.py:63
  51.7 0.8 %copy-done.3 = bf16[2048,2048]{1,0:T(8,128)(2,1)} copy-done((bf16[2048,2048]{1,0:T(8,128)(2,1)}, bf16[2048,2048]{1,0:T(8,128)(2,1)S(1)}, u32[]{:S(2)}) %copy-start.3) | copy-done | bytes 8388632
  52.8 1.5 %cholesky.59 = f32[16,16]{1,0:T(8,128)S(1)} custom-call(f32[16,16]{1,0:T(8,128)S(1)} %fusion.43), custom_call_target="Cholesky" | custom-call | tf_op jit(solution)/shard_map/jit(cholesky)/cholesky | solution.py:29
  54.4 0.6 compare_reduce_fusion.2
  55.0 0.6 fusion.26
  55.7 1.2 %custom-call.9 = f32[1,16,16]{1,2,0:T(8,128)S(1)} custom-call(f32[1,16,16]{2,1,0:T(8,128)S(1)} %fusion.26), custom_call_target="InvertDiagBlocksLowerTriangular" | custom-call | tf_op jit(solution)/shard_map/jit(_cho_solve)/triangular_solve | solution.py:29
  58.9 6.4 %fusion.11 = f32[32,2048]{1,0:T(8,128)S(1)} fusion(bf16[2048,2048]{1,0:T(8,128)(2,1)} %copy-done.3, bf16[16,2048]{1,0:T(8,128)(2,1)S(1)} %get-tuple-element.15, bf16[16,2048]{1,0:T(8,128)(2,1)S(1)} %get-tuple-element.16), kind=kOutput, calls=%fused_computation.32 | convolution fusion | flops 268697600 | bytes 8781824 | tf_op jit(solution)/shard_map/dot_general | solution.py:59
  65.3 2.3 %fusion.1 = f32[16,2048]{1,0:T(8,128)S(1)} fusion(bf16[16,2048]{1,0:T(8,128)(2,1)S(1)} %get-tuple-element.16, bf16[2048,2048]{1,0:T(8,128)(2,1)S(1)} %copy-done.2, f32[32,2048]{1,0:T(8,128)S(1)} %fusion.11, f32[16,2048]{1,0:T(8,128)S(1)} %get-tuple-element.21, f32[]{:T(128)} %bitcast.82), kind=kOutput, calls=%fused_computation.7 | convolution fusion | flops 134348800 | bytes 8978436 | tf_op jit(solution)/shard_map/dot_general | solution.py:63
  67.9 1.5 %cholesky.81 = f32[16,16]{1,0:T(8,128)S(1)} custom-call(f32[16,16]{1,0:T(8,128)S(1)} %fusion.33), custom_call_target="Cholesky" | custom-call | tf_op jit(solution)/shard_map/jit(cholesky)/cholesky | solution.py:29
  69.4 0.6 compare_reduce_fusion
  70.1 0.6 fusion.28
  70.7 1.2 %custom-call.11 = f32[1,16,16]{1,2,0:T(8,128)S(1)} custom-call(f32[1,16,16]{2,1,0:T(8,128)S(1)} %fusion.28), custom_call_target="InvertDiagBlocksLowerTriangular" | custom-call | tf_op jit(solution)/shard_map/jit(_cho_solve)/triangular_solve | solution.py:29
  (39 shorter events, 5.0 us)
Async XLA Ops:
  0.6 4.2 %copy-start = (bf16[512,512]{1,0:T(8,128)(2,1)S(1)}, bf16[512,512]{1,0:T(8,128)(2,1)}, u32[]{:S(2)}) copy-start(bf16[512,512]{1,0:T(8,128)(2,1)} %param.18) | copy-start | bytes 1572868
  46.8 4.9 %copy-start.1 = (bf16[2048,2048]{1,0:T(8,128)(2,1)}, bf16[2048,2048]{1,0:T(8,128)(2,1)S(1)}, u32[]{:S(2)}) copy-start(bf16[2048,2048]{1,0:T(8,128)(2,1)S(1)} %get-tuple-element.7) | copy-start | bytes 25165828
  46.8 5.7 %copy-start.3 = (bf16[2048,2048]{1,0:T(8,128)(2,1)}, bf16[2048,2048]{1,0:T(8,128)(2,1)S(1)}, u32[]{:S(2)}) copy-start(bf16[2048,2048]{1,0:T(8,128)(2,1)S(1)} %get-tuple-element.6) | copy-start | bytes 25165828
  56.9 8.4 %copy-start.2 = (bf16[2048,2048]{1,0:T(8,128)(2,1)S(1)}, bf16[2048,2048]{1,0:T(8,128)(2,1)}, u32[]{:S(2)}) copy-start(bf16[2048,2048]{1,0:T(8,128)(2,1)} %copy-done.1) | copy-start | bytes 25165828

commit v11 on v8

--- a/solution.py
+++ b/solution.py
@@ -2,6 +2,7 @@
 import jax.numpy as jnp
 from jax import lax
 from jax.sharding import PartitionSpec as P
+from jax.experimental import pallas as pl
 
 ITERS = 2
 
@@ -100,6 +101,29 @@
     return jnp.transpose(stacked, (1, 0, 2)).reshape(direction.shape[0], count)
 
 
+def embed_block(
+    features_ref, w_first_ref, b_first_ref, w_second_ref, b_second_ref, w_third_ref,
+    targets_ref, rung_ref, out_ref,
+):
+    dims = (((0,), (0,)), ((), ()))
+    first = lax.dot_general(
+        w_first_ref[...], features_ref[...], dims, preferred_element_type=jnp.float32
+    )
+    hidden_one = jax.nn.silu(first + b_first_ref[...]).astype(jnp.bfloat16)
+    second = lax.dot_general(
+        w_second_ref[...], hidden_one, dims, preferred_element_type=jnp.float32
+    )
+    hidden_two = jax.nn.silu(second + b_second_ref[...]).astype(jnp.bfloat16)
+    embedding = lax.dot_general(
+        w_third_ref[...], hidden_two, dims, preferred_element_type=jnp.float32
+    )
+    emb_rows = embedding.shape[0]
+    rhs = targets_ref.shape[0]
+    out_ref[:emb_rows, :] = embedding.astype(jnp.bfloat16).astype(jnp.float32)
+    out_ref[emb_rows : emb_rows + rhs, :] = targets_ref[...]
+    out_ref[emb_rows + rhs :, :] = rung_ref[...]
+
+
 def on_device(
     features,
     rung_index,
@@ -114,22 +138,23 @@
     noise_var,
 ):
     fidelity = fidelity_matrix(fidelity_factor)
-    hidden_one = jax.nn.silu(left_product(w_first, features) + b_first[:, None]).astype(
-        jnp.bfloat16
-    )
-    hidden_two = jax.nn.silu(left_product(w_second, hidden_one) + b_second[:, None]).astype(
-        jnp.bfloat16
-    )
-    embedding = lax.reduce_precision(
-        left_product(w_third, hidden_two), exponent_bits=8, mantissa_bits=7
-    )
-    rung_value = rung_index.astype(jnp.float32)
+    emb_rows = w_third.shape[1]
     own_count = targets.shape[1]
     own_first = (lax.axis_index("row") * lax.axis_size("col") + lax.axis_index("col")) * own_count
-
-    emb_rows = embedding.shape[0]
-    packed = jnp.concatenate(
-        [embedding, targets, rung_value[None, :]], axis=0
+    packed = pl.pallas_call(
+        embed_block,
+        out_shape=jax.ShapeDtypeStruct(
+            (emb_rows + targets.shape[0] + 1, own_count), jnp.float32
+        ),
+    )(
+        features,
+        w_first,
+        b_first[:, None],
+        w_second,
+        b_second[:, None],
+        w_third,
+        targets,
+        rung_index.astype(jnp.float32)[None, :],
     )
     gathered = lax.all_gather(packed, ("row", "col"), axis=1, tiled=True)
     all_embedding = gathered[:emb_rows].astype(jnp.bfloat16)

time: 73.7 us -> 78.4 us (1.064)
  local copies, waits for them, and re-layouts: 1.02 us -> 6.34 us
  matrix products: 30.5 us -> 27.2 us
  Pallas kernels: 0 us -> 2.69 us
    broadcast_in_dim x0 -> x2, local copies, waits for them, and re-layouts: none -> 3.06 us  [the longest x1 1.53 us: on_device(): b_second[:, None]]
    pallas_call x0 -> x1, Pallas kernels: none -> 2.69 us  [on_device(): pl.pallas_call(embed_block, out_shape=jax.ShapeDtypeStruct((emb_rows + ta...]
    dot_general x3 -> x1, matrix products: 9.38 us -> 6.76 us  [left_product(): lax.dot_general(weights, values, (((0,), (0,)), ((), ())), preferred_elem...]
    unnamed x6 -> x5, local copies, waits for them, and re-layouts: 0.67 us -> 2.93 us
where the time goes in v11:
time: 78.4 us; the launch traced here: 78.1 us
  matrix products  27.2 us (35%)
  blocking collectives  25.5 us (33%)
  other arithmetic  14.2 us (18%)
  local copies, waits for them, and re-layouts  6.34 us (8%)
  Pallas kernels  2.69 us (3%)
  between operations  2.14 us (3%)
    all_gather x1, blocking collectives, on_device(): gathered = lax.all_gather(packed, ('row', 'col'), axis=1, tiled=True)  25.5 us
    dot_general x2, matrix products, split_product(): lax.dot_general(jnp.concatenate([d_high, d_low], axis=0), k_high, dims, p...  11.2 us
    dot_general x1, matrix products, left_product(): lax.dot_general(weights, values, (((0,), (0,)), ((), ())), preferred_elem...  6.76 us
    another operation x9, other arithmetic, solve_spd(): jnp.linalg.cholesky(matrix)  6.57 us
    another operation x6, other arithmetic, solve_spd(): jax.scipy.linalg.cho_solve((jnp.linalg.cholesky(matrix), True), right_side)  5.74 us
    dot_general x2, matrix products, split_product(): lax.dot_general(d_high, k_low, dims, preferred_element_type=jnp.float32)  4.55 us
    unnamed x5, local copies, waits for them, and re-layouts  2.93 us
    pallas_call x1, Pallas kernels, on_device(): pl.pallas_call(embed_block, out_shape=jax.ShapeDtypeStruct((emb_rows + ta...  2.69 us

profile of v11, /device:TPU:0, one launch (start us, length us, event | category | flops | bytes accessed | tf_op | source)
XLA Modules:
  0.0 78.1 jit_solution(27209201489667982)
XLA Ops:
  0.6 1.5 %copy.17.b_first_ref = f32[512,1]{1,0:T(8,128)} copy(f32[512,1]{0,1:T(1,128)} %bitcast.74) | data formatting | bytes 4096 | tf_op jit(solution)/shard_map/broadcast_in_dim | solution.py:152
  2.2 1.5 %copy.18.b_second_ref = f32[512,1]{1,0:T(8,128)} copy(f32[512,1]{0,1:T(1,128)} %bitcast.75) | data formatting | bytes 4096 | tf_op jit(solution)/shard_map/broadcast_in_dim | solution.py:154
  3.7 1.6 %copy.19.w_third_ref = bf16[512,64]{1,0:T(8,128)(2,1)} copy(bf16[512,64]{0,1:T(8,128)(2,1)} %param.20) | data formatting | bytes 131072 | tf_op args[6]
  5.3 1.2 %convert_bitcast_fusion.rung_ref = f32[1,128]{1,0:T(1,128)} fusion(s32[128]{0:T(128)} %param.15), kind=kLoop, calls=%fused_computation.81 | loop fusion | flops 128 | bytes 1024 | tf_op jit(solution)/shard_map/broadcast_in_dim | solution.py:157
  6.4 2.7 %shard_map.122 = f32[81,128]{1,0:T(8,128)} custom-call(bf16[164,128]{1,0:T(8,128)(2,1)} %features_ref.1, bf16[164,512]{1,0:T(8,128)(2,1)} %w_first_ref.1, f32[512,1]{1,0:T(8,128)} %copy.17.b_first_ref, bf16[512,512]{1,0:T(8,128)(2,1)} %w_second_ref.1, f32[512,1]{1,0:T(8,128)} %copy.18.b_second_ref, bf16[512,64]{1,0:T(8,128)(2,1)} %copy.19.w_third_ref, ...), custom_call_target="tpu_custom_call" | custom-call | tf_op jit(solution)/shard_map/pallas_call | solution.py:144
  9.1 25.5 %all_gather.3 = f32[81,2048]{1,0:T(8,128)S(1)} all-gather(f32[81,128]{1,0:T(8,128)} %shard_map.122), channel_id=1, replica_groups=mesh['task'=2,'row'=4,'col'=4] {'row','col'}, dimensions={1}, use_global_device_ids=true | all-gather | bytes 705024 | tf_op jit(solution)/shard_map/all_gather | solution.py:159
  34.6 0.9 %convolution_add_fusion.3 = f32[4,4]{1,0:T(4,128)S(1)} fusion(f32[4,4]{1,0:T(4,128)} %param.22), kind=kOutput, calls=%fused_computation.12 | convolution fusion | flops 848 | bytes 128 | tf_op jit(solution)/shard_map/dot_general | solution.py:12
  36.6 6.8 %select_multiply_fusion = f32[2048,2048]{1,0:T(8,128)S(1)} fusion(f32[2048]{0:T(1024)S(1)} %bitcast.71, f32[2048]{0:T(1024)S(1)} %bitcast.72, f32[2048]{0:T(1024)S(1)} %bitcast.73, f32[2048]{0:T(1024)S(1)} %bitcast.70, f32[2048]{0:T(1024)S(1)} %multiply_reduce_fusion, f32[]{:T(128)} %bitcast.3, pred[2048]{0:T(1024)(128)(4,1)S(1)} %get-tuple-element.111, ...), kind=kOutput, calls=%fused_computation.3 | convolution fusion | flops 570425344 | bytes 17094660 | tf_op jit(solution)/shard_map/while/body/eval_jaxpr/while/body/eval_jaxpr/dot_general | solution.py:18
  43.4 2.6 %fusion.2 = f32[32,2048]{1,0:T(8,128)S(1)} fusion(f32[2048,2048]{1,0:T(8,128)S(1)} %select_multiply_fusion, bf16[16,2048]{1,0:T(8,128)(2,1)S(1)} %get-tuple-element.113, bf16[16,2048]{1,0:T(8,128)(2,1)S(1)} %get-tuple-element.114), kind=kOutput, calls=%fused_computation.5 | convolution fusion | flops 277086208 | bytes 17170432 | tf_op jit(solution)/shard_map/while/body/eval_jaxpr/while/body/eval_jaxpr/dot_general | solution.py:56
  46.7 2.3 %fusion.4 = f32[16,2048]{1,0:T(8,128)S(1)} fusion(bf16[16,2048]{1,0:T(8,128)(2,1)S(1)} %get-tuple-element.114, f32[2048,2048]{1,0:T(8,128)S(1)} %select_multiply_fusion, f32[32,2048]{1,0:T(8,128)S(1)} %fusion.2, f32[81,2048]{1,0:T(8,128)S(1)} %all_gather.3, f32[]{:T(128)} %bitcast.66), kind=kOutput, calls=%fused_computation.11 | convolution fusion | flops 146931712 | bytes 17367044 | tf_op jit(solution)/shard_map/while/body/eval_jaxpr/while/body/eval_jaxpr/dot_general | solution.py:60
  49.4 1.5 %cholesky.59 = f32[16,16]{1,0:T(8,128)S(1)} custom-call(f32[16,16]{1,0:T(8,128)S(1)} %fusion.41), custom_call_target="Cholesky" | custom-call | tf_op jit(solution)/shard_map/jit(cholesky)/cholesky | solution.py:30
  50.9 0.6 compare_reduce_fusion.2
  51.6 0.6 fusion.24
  52.2 1.3 %custom-call.9 = f32[1,16,16]{1,2,0:T(8,128)S(1)} custom-call(f32[1,16,16]{2,1,0:T(8,128)S(1)} %fusion.24), custom_call_target="InvertDiagBlocksLowerTriangular" | custom-call | tf_op jit(solution)/shard_map/jit(_cho_solve)/triangular_solve | solution.py:30
  55.2 1.5 %cholesky.70 = f32[16,16]{1,0:T(8,128)S(1)} custom-call(f32[16,16]{1,0:T(8,128)S(1)} %fusion.36), custom_call_target="Cholesky" | custom-call | tf_op jit(solution)/shard_map/jit(cholesky)/cholesky | solution.py:30
  57.3 0.6 fusion.25
  58.0 1.2 %custom-call.10 = f32[1,16,16]{1,2,0:T(8,128)S(1)} custom-call(f32[1,16,16]{2,1,0:T(8,128)S(1)} %fusion.25), custom_call_target="InvertDiagBlocksLowerTriangular" | custom-call | tf_op jit(solution)/shard_map/jit(_cho_solve)/triangular_solve | solution.py:30
  59.9 8.6 %fusion.1 = f32[32,2048]{1,0:T(8,128)S(1)} fusion(f32[2048,2048]{1,0:T(8,128)} %copy-done, bf16[16,2048]{1,0:T(8,128)(2,1)S(1)} %get-tuple-element.134, bf16[16,2048]{1,0:T(8,128)(2,1)S(1)} %get-tuple-element.135), kind=kOutput, calls=%fused_computation.4 | convolution fusion | flops 277086208 | bytes 17170432 | tf_op jit(solution)/shard_map/while/body/eval_jaxpr/while/body/eval_jaxpr/dot_general | solution.py:56
  68.6 1.2 %copy-done.1 = f32[2048,2048]{1,0:T(8,128)S(1)} copy-done((f32[2048,2048]{1,0:T(8,128)S(1)}, f32[2048,2048]{1,0:T(8,128)}, u32[]{:S(2)}) %copy-start.1) | copy-done | bytes 16777240
  69.8 2.3 %fusion.3 = f32[16,2048]{1,0:T(8,128)S(1)} fusion(bf16[16,2048]{1,0:T(8,128)(2,1)S(1)} %get-tuple-element.135, f32[2048,2048]{1,0:T(8,128)S(1)} %copy-done.1, f32[32,2048]{1,0:T(8,128)S(1)} %fusion.1, f32[16,2048]{1,0:T(8,128)S(1)} %get-tuple-element.140, f32[]{:T(128)} %bitcast.67), kind=kOutput, calls=%fused_computation.9 | convolution fusion | flops 146931712 | bytes 17367044 | tf_op jit(solution)/shard_map/while/body/eval_jaxpr/while/body/eval_jaxpr/dot_general | solution.py:60
  72.4 1.5 %cholesky.81 = f32[16,16]{1,0:T(8,128)S(1)} custom-call(f32[16,16]{1,0:T(8,128)S(1)} %fusion.31), custom_call_target="Cholesky" | custom-call | tf_op jit(solution)/shard_map/jit(cholesky)/cholesky | solution.py:30
  73.9 0.6 compare_reduce_fusion
  74.6 0.6 fusion.26
  75.2 1.2 %custom-call.11 = f32[1,16,16]{1,2,0:T(8,128)S(1)} custom-call(f32[1,16,16]{2,1,0:T(8,128)S(1)} %fusion.26), custom_call_target="InvertDiagBlocksLowerTriangular" | custom-call | tf_op jit(solution)/shard_map/jit(_cho_solve)/triangular_solve | solution.py:30
  (36 shorter events, 5.7 us)
Async XLA Ops:
  43.3 5.7 %copy-start = (f32[2048,2048]{1,0:T(8,128)}, f32[2048,2048]{1,0:T(8,128)S(1)}, u32[]{:S(2)}) copy-start(f32[2048,2048]{1,0:T(8,128)S(1)} %select_multiply_fusion) | copy-start | bytes 50331652
  59.2 10.6 %copy-start.1 = (f32[2048,2048]{1,0:T(8,128)S(1)}, f32[2048,2048]{1,0:T(8,128)}, u32[]{:S(2)}) copy-start(f32[2048,2048]{1,0:T(8,128)} %copy-done) | copy-start | bytes 50331652

commit v12 on v8

--- a/solution.py
+++ b/solution.py
@@ -71,7 +71,7 @@
         rows_embedding = lax.dynamic_slice_in_dim(embedding, first_row, row_block, 1)
         rows_squares = lax.dynamic_slice_in_dim(squares, first_row, row_block, 0)
         rows_rung = lax.dynamic_slice_in_dim(rung_value, first_row, row_block, 0)
-        rows_match = rows_rung.astype(jnp.float32)[:, None] == levels[None, :]
+        rows_fidelity = lax.dynamic_slice_in_dim(col_fidelity, first_row, row_block, 1)
 
         def one_col_block(running, column_number):
             first_col = column_number * col_block
@@ -79,15 +79,24 @@
             cols_squares = lax.dynamic_slice_in_dim(squares, first_col, col_block, 0)
             cols_fidelity = lax.dynamic_slice_in_dim(col_fidelity, first_col, col_block, 1)
             cols_direction = lax.dynamic_slice_in_dim(direction, first_col, col_block, 1)
+            cols_rung = lax.dynamic_slice_in_dim(rung_value, first_col, col_block, 0)
             inner = left_product(rows_embedding, cols_embedding)
             distance = rows_squares[:, None] + cols_squares[None, :] - 2.0 * inner
-            tile_fidelity = cols_fidelity[0][None, :]
+            radial = jnp.exp(-inverse_scale[0] * distance)
+            by_rung = jnp.concatenate(
+                [
+                    jnp.where(cols_rung[None, :] == levels[level], cols_direction, 0.0)
+                    for level in range(col_fidelity.shape[0])
+                ],
+                axis=0,
+            )
+            rung_products = split_product(by_rung, radial)
+            rhs = direction.shape[0]
+            contribution = rows_fidelity[0][None, :] * rung_products[:rhs]
             for level in range(1, col_fidelity.shape[0]):
-                tile_fidelity = jnp.where(
-                    rows_match[:, level : level + 1], cols_fidelity[level][None, :], tile_fidelity
-                )
-            kernel = jnp.exp(-inverse_scale[0] * distance) * tile_fidelity
-            contribution = split_product(cols_direction, kernel)
+                contribution = contribution + rows_fidelity[level][None, :] * rung_products[
+                    level * rhs : (level + 1) * rhs
+                ]
             return (running + contribution, None)
 
         start_value = jnp.zeros((direction.shape[0], row_block), jnp.float32)

time: 73.7 us -> 73.2 us (level)
  matrix products: 30.5 us -> 27 us
  other arithmetic: 14.4 us -> 17.3 us
    eq x1, other arithmetic: 0.03 us -> 2.64 us  [one_col_block(): cols_rung[None, :] == levels[level]]
    dot_general x2, matrix products: 11.7 us -> 9.5 us  [split_product(): lax.dot_general(jnp.concatenate([d_high, d_low], axis=0), k_high, dims, p...]
    dot_general x3, matrix products: 9.38 us -> 8.3 us  [left_product(): lax.dot_general(weights, values, (((0,), (0,)), ((), ())), preferred_elem...]
    dot_general x1, matrix products: 0.88 us -> 0.13 us  [fidelity_matrix(): jnp.dot(lower, lower.T, precision=lax.Precision.HIGHEST)]
where the time goes in v12:
time: 73.2 us; the launch traced here: 72.9 us
  matrix products  27 us (37%)
  blocking collectives  25.3 us (35%)
  other arithmetic  17.3 us (24%)
  between operations  2.19 us (3%)
  local copies, waits for them, and re-layouts  1.16 us (2%)
    all_gather x1, blocking collectives, on_device(): gathered = lax.all_gather(packed, ('row', 'col'), axis=1, tiled=True)  25.3 us
    dot_general x2, matrix products, split_product(): lax.dot_general(jnp.concatenate([d_high, d_low], axis=0), k_high, dims, p...  9.5 us
    dot_general x3, matrix products, left_product(): lax.dot_general(weights, values, (((0,), (0,)), ((), ())), preferred_elem...  8.3 us
    another operation x9, other arithmetic, solve_spd(): jnp.linalg.cholesky(matrix)  6.57 us
    another operation x6, other arithmetic, solve_spd(): jax.scipy.linalg.cho_solve((jnp.linalg.cholesky(matrix), True), right_side)  5.63 us
    dot_general x2, matrix products, split_product(): lax.dot_general(d_high, k_low, dims, preferred_element_type=jnp.float32)  5.32 us
    eq x1, other arithmetic, one_col_block(): cols_rung[None, :] == levels[level]  2.64 us

profile of v12, /device:TPU:0, one launch (start us, length us, event | category | flops | bytes accessed | tf_op | source)
XLA Modules:
  0.0 72.9 jit_solution(681606448874315957)
XLA Ops:
  0.6 0.7 convert_bitcast_fusion
  1.4 1.2 %multiply_convert_fusion.1 = bf16[512,128]{1,0:T(8,128)(2,1)S(1)} fusion(bf16[164,512]{1,0:T(8,128)(2,1)} %param.16, bf16[164,128]{1,0:T(8,128)(2,1)} %param.14, f32[512]{0:T(512)} %param.17), kind=kOutput, calls=%fused_computation.36 | convolution fusion | flops 21889024 | bytes 343040 | tf_op jit(solution)/shard_map/dot_general | solution.py:17
  2.6 1.4 %fusion.2 = f32[64,128]{1,0:T(8,128)S(1)} fusion(bf16[512,64]{0,1:T(8,128)(2,1)} %param.20, bf16[512,128]{1,0:T(8,128)(2,1)S(1)} %multiply_convert_fusion.1, bf16[512,512]{1,0:T(8,128)(2,1)S(1)} %copy-done, f32[512]{0:T(512)} %param.19), kind=kOutput, calls=%fused_computation.12 | convolution fusion | flops 75898880 | bytes 755712 | tf_op jit(solution)/shard_map/dot_general | solution.py:17
  4.0 0.7 pad_maximum_fusion.2
  4.7 25.3 %all_gather.3 = f32[81,2048]{1,0:T(8,128)S(1)} all-gather(f32[81,128]{1,0:T(8,128)S(1)} %pad_maximum_fusion.2), channel_id=1, replica_groups=mesh['task'=2,'row'=4,'col'=4] {'row','col'}, dimensions={1}, use_global_device_ids=true | all-gather | bytes 705024 | tf_op jit(solution)/shard_map/all_gather | solution.py:143
  30.2 0.7 fusion.58
  30.9 2.6 %compare_reduce_fusion.3 = (pred[2048]{0:T(1024)(128)(4,1)S(1)}, pred[2048]{0:T(1024)(128)(4,1)S(1)}, pred[2048]{0:T(1024)(128)(4,1)S(1)}, pred[2048]{0:T(1024)(128)(4,1)S(1)}) fusion(f32[]{:T(128)} %bitcast.5, f32[81,2048]{1,0:T(8,128)S(1)} %all_gather.3, f32[]{:T(128)} %bitcast.6, f32[]{:T(128)} %bitcast.7, f32[]{:T(128)} %bitcast.8), kind=kLoop, calls=%fused_computation.76 | loop fusion | flops 8192 | bytes 16400 | tf_op jit(solution)/shard_map/while/body/eval_jaxpr/while/body/eval_jaxpr/eq | solution.py:88
  34.4 5.7 %reduce-precision_convert_fusion = (bf16[2048,2048]{1,0:T(8,128)(2,1)S(1)}, bf16[2048,2048]{1,0:T(8,128)(2,1)S(1)}) fusion(f32[2048]{0:T(1024)S(1)} %multiply_reduce_fusion, f32[]{:T(128)} %bitcast.9, f32[81,2048]{1,0:T(8,128)S(1)} %all_gather.3), kind=kOutput, calls=%fused_computation.1 | convolution fusion | flops 570425344 | bytes 17055748 | tf_op jit(solution)/shard_map/while/body/eval_jaxpr/while/body/eval_jaxpr/dot_general | solution.py:17
  40.1 2.9 %fusion.5 = f32[128,2048]{1,0:T(8,128)S(1)} fusion(bf16[2048,2048]{1,0:T(8,128)(2,1)S(1)} %get-tuple-element.121, bf16[64,2048]{1,0:T(8,128)(2,1)S(1)} %get-tuple-element.149, bf16[64,2048]{1,0:T(8,128)(2,1)S(1)} %get-tuple-element.150), kind=kOutput, calls=%fused_computation.23 | convolution fusion | flops 1074790400 | bytes 9961472 | tf_op jit(solution)/shard_map/while/body/eval_jaxpr/while/body/eval_jaxpr/dot_general | solution.py:55
  43.0 2.7 %convolution_add_fusion.1 = f32[64,2048]{1,0:T(8,128)S(1)} fusion(bf16[64,2048]{1,0:T(8,128)(2,1)S(1)} %get-tuple-element.150, bf16[2048,2048]{1,0:T(8,128)(2,1)S(1)} %get-tuple-element.142, f32[128,2048]{1,0:T(8,128)S(1)} %fusion.5), kind=kOutput, calls=%fused_computation.5 | convolution fusion | flops 537133056 | bytes 10223616 | tf_op jit(solution)/shard_map/while/body/eval_jaxpr/while/body/eval_jaxpr/dot_general | solution.py:59
  47.2 1.5 %cholesky.59 = f32[16,16]{1,0:T(8,128)S(1)} custom-call(f32[16,16]{1,0:T(8,128)S(1)} %fusion.50), custom_call_target="Cholesky" | custom-call | tf_op jit(solution)/shard_map/jit(cholesky)/cholesky | solution.py:29
  48.8 0.6 compare_reduce_fusion.6
  49.4 0.6 fusion.33
  50.1 1.2 %custom-call.9 = f32[1,16,16]{1,2,0:T(8,128)S(1)} custom-call(f32[1,16,16]{2,1,0:T(8,128)S(1)} %fusion.33), custom_call_target="InvertDiagBlocksLowerTriangular" | custom-call | tf_op jit(solution)/shard_map/jit(_cho_solve)/triangular_solve | solution.py:29
  52.3 1.5 %cholesky.70 = f32[16,16]{1,0:T(8,128)S(1)} custom-call(f32[16,16]{1,0:T(8,128)S(1)} %fusion.45), custom_call_target="Cholesky" | custom-call | tf_op jit(solution)/shard_map/jit(cholesky)/cholesky | solution.py:29
  53.8 0.6 compare_reduce_fusion.5
  54.5 0.6 fusion.34
  55.1 1.2 %custom-call.10 = f32[1,16,16]{1,2,0:T(8,128)S(1)} custom-call(f32[1,16,16]{2,1,0:T(8,128)S(1)} %fusion.34), custom_call_target="InvertDiagBlocksLowerTriangular" | custom-call | tf_op jit(solution)/shard_map/jit(_cho_solve)/triangular_solve | solution.py:29
  57.2 6.6 %fusion.9 = f32[128,2048]{1,0:T(8,128)S(1)} fusion(bf16[2048,2048]{1,0:T(8,128)(2,1)} %copy-done.3, bf16[64,2048]{1,0:T(8,128)(2,1)S(1)} %get-tuple-element.147, bf16[64,2048]{1,0:T(8,128)(2,1)S(1)} %get-tuple-element.148), kind=kOutput, calls=%fused_computation.28 | convolution fusion | flops 1074790400 | bytes 9961472 | tf_op jit(solution)/shard_map/while/body/eval_jaxpr/while/body/eval_jaxpr/dot_general | solution.py:55
  63.8 2.7 %convolution_add_fusion = f32[64,2048]{1,0:T(8,128)S(1)} fusion(bf16[64,2048]{1,0:T(8,128)(2,1)S(1)} %get-tuple-element.148, bf16[2048,2048]{1,0:T(8,128)(2,1)S(1)} %copy-done.2, f32[128,2048]{1,0:T(8,128)S(1)} %fusion.9), kind=kOutput, calls=%fused_computation.4 | convolution fusion | flops 537133056 | bytes 10223616 | tf_op jit(solution)/shard_map/while/body/eval_jaxpr/while/body/eval_jaxpr/dot_general | solution.py:59
  66.8 1.5 %cholesky.81 = f32[16,16]{1,0:T(8,128)S(1)} custom-call(f32[16,16]{1,0:T(8,128)S(1)} %fusion.40), custom_call_target="Cholesky" | custom-call | tf_op jit(solution)/shard_map/jit(cholesky)/cholesky | solution.py:29
  68.4 0.6 compare_reduce_fusion.4
  69.0 0.6 fusion.35
  69.7 1.2 %custom-call.11 = f32[1,16,16]{1,2,0:T(8,128)S(1)} custom-call(f32[1,16,16]{2,1,0:T(8,128)S(1)} %fusion.35), custom_call_target="InvertDiagBlocksLowerTriangular" | custom-call | tf_op jit(solution)/shard_map/jit(_cho_solve)/triangular_solve | solution.py:29
  (46 shorter events, 5.5 us)
Async XLA Ops:
  0.6 2.0 %copy-start = (bf16[512,512]{1,0:T(8,128)(2,1)S(1)}, bf16[512,512]{1,0:T(8,128)(2,1)}, u32[]{:S(2)}) copy-start(bf16[512,512]{1,0:T(8,128)(2,1)} %param.18) | copy-start | bytes 1572868
  40.1 5.6 %copy-start.1 = (bf16[2048,2048]{1,0:T(8,128)(2,1)}, bf16[2048,2048]{1,0:T(8,128)(2,1)S(1)}, u32[]{:S(2)}) copy-start(bf16[2048,2048]{1,0:T(8,128)(2,1)S(1)} %get-tuple-element.142) | copy-start | bytes 25165828
  40.1 5.7 %copy-start.3 = (bf16[2048,2048]{1,0:T(8,128)(2,1)}, bf16[2048,2048]{1,0:T(8,128)(2,1)S(1)}, u32[]{:S(2)}) copy-start(bf16[2048,2048]{1,0:T(8,128)(2,1)S(1)} %get-tuple-element.121) | copy-start | bytes 25165828
  40.1 6.3 %copy-start.4 = (f32[4,4]{1,0:T(4,128)S(1)}, f32[4,4]{1,0:T(4,128)}, u32[]{:S(2)}) copy-start(f32[4,4]{1,0:T(4,128)} %param.22) | copy-start | bytes 196
  56.4 7.4 %copy-start.2 = (bf16[2048,2048]{1,0:T(8,128)(2,1)S(1)}, bf16[2048,2048]{1,0:T(8,128)(2,1)}, u32[]{:S(2)}) copy-start(bf16[2048,2048]{1,0:T(8,128)(2,1)} %copy-done.1) | copy-start | bytes 25165828

commit v13 on v12

--- a/solution.py
+++ b/solution.py
@@ -39,7 +39,7 @@
 def rung_fidelity(fidelity, rung_value):
     levels = jnp.arange(fidelity.shape[0], dtype=jnp.float32)
     onehot = (rung_value.astype(jnp.float32)[None, :] == levels[:, None]).astype(jnp.float32)
-    return jnp.dot(fidelity, onehot, precision=lax.Precision.HIGHEST)
+    return jnp.dot(fidelity, onehot, precision=lax.Precision.HIGHEST), onehot
 
 
 def split_two(values):
@@ -60,7 +60,7 @@
     return (by_high[:count] + by_high[count:]) + by_low
 
 
-def kernel_image(embedding, squares, rung_value, col_fidelity, inverse_scale, direction):
+def kernel_image(embedding, squares, rung_onehot, col_fidelity, inverse_scale, direction):
     count = embedding.shape[1]
     row_block = block_size(count, 2048)
     col_block = block_size(count, 2048)
@@ -70,7 +70,6 @@
         first_row = block_number * row_block
         rows_embedding = lax.dynamic_slice_in_dim(embedding, first_row, row_block, 1)
         rows_squares = lax.dynamic_slice_in_dim(squares, first_row, row_block, 0)
-        rows_rung = lax.dynamic_slice_in_dim(rung_value, first_row, row_block, 0)
         rows_fidelity = lax.dynamic_slice_in_dim(col_fidelity, first_row, row_block, 1)
 
         def one_col_block(running, column_number):
@@ -79,13 +78,13 @@
             cols_squares = lax.dynamic_slice_in_dim(squares, first_col, col_block, 0)
             cols_fidelity = lax.dynamic_slice_in_dim(col_fidelity, first_col, col_block, 1)
             cols_direction = lax.dynamic_slice_in_dim(direction, first_col, col_block, 1)
-            cols_rung = lax.dynamic_slice_in_dim(rung_value, first_col, col_block, 0)
+            cols_onehot = lax.dynamic_slice_in_dim(rung_onehot, first_col, col_block, 1)
             inner = left_product(rows_embedding, cols_embedding)
             distance = rows_squares[:, None] + cols_squares[None, :] - 2.0 * inner
             radial = jnp.exp(-inverse_scale[0] * distance)
             by_rung = jnp.concatenate(
                 [
-                    jnp.where(cols_rung[None, :] == levels[level], cols_direction, 0.0)
+                    cols_direction * cols_onehot[level][None, :]
                     for level in range(col_fidelity.shape[0])
                 ],
                 axis=0,
@@ -146,7 +145,7 @@
     all_rung = gathered[emb_rows + targets.shape[0]]
 
     squares = jnp.sum(jnp.square(gathered[:emb_rows]), axis=0)
-    col_fidelity = rung_fidelity(fidelity, all_rung)
+    col_fidelity, rung_onehot = rung_fidelity(fidelity, all_rung)
 
     solution = jnp.zeros_like(all_targets)
     residual = all_targets
@@ -154,7 +153,7 @@
     gram = outer_gram(residual, residual)
     for iteration in range(ITERS):
         image = (
-            kernel_image(all_embedding, squares, all_rung, col_fidelity, inverse_scale, direction)
+            kernel_image(all_embedding, squares, rung_onehot, col_fidelity, inverse_scale, direction)
             + noise_var[0] * direction
         )
         curvature = outer_gram(direction, image)

time: 73.2 us -> 69.9 us (0.955)
  other arithmetic: 17.3 us -> 14.6 us
    eq x1 -> x0, other arithmetic: 2.64 us -> none  [one_col_block(): cols_rung[None, :] == levels[level]]
where the time goes in v13:
time: 69.9 us; the launch traced here: 69.6 us
  matrix products  27 us (39%)
  blocking collectives  25.3 us (36%)
  other arithmetic  14.6 us (21%)
  between operations  2.2 us (3%)
    all_gather x1, blocking collectives, on_device(): gathered = lax.all_gather(packed, ('row', 'col'), axis=1, tiled=True)  25.3 us
    dot_general x2, matrix products, split_product(): lax.dot_general(jnp.concatenate([d_high, d_low], axis=0), k_high, dims, p...  9.5 us
    dot_general x3, matrix products, left_product(): lax.dot_general(weights, values, (((0,), (0,)), ((), ())), preferred_elem...  8.27 us
    another operation x9, other arithmetic, solve_spd(): jnp.linalg.cholesky(matrix)  6.58 us
    another operation x6, other arithmetic, solve_spd(): jax.scipy.linalg.cho_solve((jnp.linalg.cholesky(matrix), True), right_side)  5.63 us
    dot_general x2, matrix products, split_product(): lax.dot_general(d_high, k_low, dims, preferred_element_type=jnp.float32)  5.32 us

profile of v13, /device:TPU:0, one launch (start us, length us, event | category | flops | bytes accessed | tf_op | source)
XLA Modules:
  0.0 69.6 jit_solution(14056495379713091680)
XLA Ops:
  0.6 0.7 %convert_bitcast_fusion = f32[1,128]{1,0:T(1,128)S(1)} fusion(s32[128]{0:T(128)} %param.15), kind=kLoop, calls=%fused_computation.113 | loop fusion | flops 128 | bytes 1024 | tf_op jit(solution)/shard_map/broadcast_in_dim | solution.py:140
  1.4 1.2 %multiply_convert_fusion.1 = bf16[512,128]{1,0:T(8,128)(2,1)S(1)} fusion(bf16[164,512]{1,0:T(8,128)(2,1)} %param.16, bf16[164,128]{1,0:T(8,128)(2,1)} %param.14, f32[512]{0:T(512)} %param.17), kind=kOutput, calls=%fused_computation.36 | convolution fusion | flops 21889024 | bytes 343040 | tf_op jit(solution)/shard_map/dot_general | solution.py:17
  2.6 1.4 %fusion.2 = f32[64,128]{1,0:T(8,128)S(1)} fusion(bf16[512,64]{0,1:T(8,128)(2,1)} %param.20, bf16[512,128]{1,0:T(8,128)(2,1)S(1)} %multiply_convert_fusion.1, bf16[512,512]{1,0:T(8,128)(2,1)S(1)} %copy-done, f32[512]{0:T(512)} %param.19), kind=kOutput, calls=%fused_computation.12 | convolution fusion | flops 75898880 | bytes 755712 | tf_op jit(solution)/shard_map/dot_general | solution.py:17
  4.0 0.7 %pad_maximum_fusion.2 = f32[81,128]{1,0:T(8,128)S(1)} fusion(f32[1,128]{1,0:T(1,128)S(1)} %convert_bitcast_fusion, f32[16,128]{1,0:T(8,128)} %param.21, f32[64,128]{1,0:T(8,128)S(1)} %fusion.2), kind=kLoop, calls=%fused_computation.70 | loop fusion | flops 20736 | bytes 82944 | tf_op jit(solution)/shard_map/concatenate | solution.py:139
  4.7 25.3 %all_gather.3 = f32[81,2048]{1,0:T(8,128)S(1)} all-gather(f32[81,128]{1,0:T(8,128)S(1)} %pad_maximum_fusion.2), channel_id=1, replica_groups=mesh['task'=2,'row'=4,'col'=4] {'row','col'}, dimensions={1}, use_global_device_ids=true | all-gather | bytes 705024 | tf_op jit(solution)/shard_map/all_gather | solution.py:142
  31.1 5.7 %reduce-precision_convert_fusion = (bf16[2048,2048]{1,0:T(8,128)(2,1)S(1)}, bf16[2048,2048]{1,0:T(8,128)(2,1)S(1)}) fusion(f32[2048]{0:T(1024)S(1)} %multiply_reduce_fusion, f32[]{:T(128)} %bitcast.9, f32[81,2048]{1,0:T(8,128)S(1)} %all_gather.3), kind=kOutput, calls=%fused_computation.1 | convolution fusion | flops 570425344 | bytes 17055748 | tf_op jit(solution)/shard_map/while/body/eval_jaxpr/while/body/eval_jaxpr/dot_general | solution.py:17
  36.8 2.9 %fusion.5 = f32[128,2048]{1,0:T(8,128)S(1)} fusion(bf16[2048,2048]{1,0:T(8,128)(2,1)S(1)} %get-tuple-element.106, bf16[64,2048]{1,0:T(8,128)(2,1)S(1)} %get-tuple-element.132, bf16[64,2048]{1,0:T(8,128)(2,1)S(1)} %get-tuple-element.133), kind=kOutput, calls=%fused_computation.23 | convolution fusion | flops 1074790400 | bytes 9961472 | tf_op jit(solution)/shard_map/while/body/eval_jaxpr/while/body/eval_jaxpr/dot_general | solution.py:55
  39.7 2.7 %convolution_add_fusion.1 = f32[64,2048]{1,0:T(8,128)S(1)} fusion(bf16[64,2048]{1,0:T(8,128)(2,1)S(1)} %get-tuple-element.133, bf16[2048,2048]{1,0:T(8,128)(2,1)S(1)} %get-tuple-element.107, f32[128,2048]{1,0:T(8,128)S(1)} %fusion.5), kind=kOutput, calls=%fused_computation.5 | convolution fusion | flops 537133056 | bytes 10223616 | tf_op jit(solution)/shard_map/while/body/eval_jaxpr/while/body/eval_jaxpr/dot_general | solution.py:59
  43.9 1.5 %cholesky.59 = f32[16,16]{1,0:T(8,128)S(1)} custom-call(f32[16,16]{1,0:T(8,128)S(1)} %fusion.51), custom_call_target="Cholesky" | custom-call | tf_op jit(solution)/shard_map/jit(cholesky)/cholesky | solution.py:29
  45.5 0.6 compare_reduce_fusion.2
  46.1 0.6 fusion.34
  46.8 1.2 %custom-call.9 = f32[1,16,16]{1,2,0:T(8,128)S(1)} custom-call(f32[1,16,16]{2,1,0:T(8,128)S(1)} %fusion.34), custom_call_target="InvertDiagBlocksLowerTriangular" | custom-call | tf_op jit(solution)/shard_map/jit(_cho_solve)/triangular_solve | solution.py:29
  49.0 1.5 %cholesky.70 = f32[16,16]{1,0:T(8,128)S(1)} custom-call(f32[16,16]{1,0:T(8,128)S(1)} %fusion.46), custom_call_target="Cholesky" | custom-call | tf_op jit(solution)/shard_map/jit(cholesky)/cholesky | solution.py:29
  50.5 0.6 compare_reduce_fusion.1
  51.2 0.6 fusion.35
  51.8 1.2 %custom-call.10 = f32[1,16,16]{1,2,0:T(8,128)S(1)} custom-call(f32[1,16,16]{2,1,0:T(8,128)S(1)} %fusion.35), custom_call_target="InvertDiagBlocksLowerTriangular" | custom-call | tf_op jit(solution)/shard_map/jit(_cho_solve)/triangular_solve | solution.py:29
  53.4 0.4 broadcast_multiply_fusion.6
  53.9 6.6 %fusion.9 = f32[128,2048]{1,0:T(8,128)S(1)} fusion(bf16[2048,2048]{1,0:T(8,128)(2,1)} %copy-done.3, bf16[64,2048]{1,0:T(8,128)(2,1)S(1)} %get-tuple-element.130, bf16[64,2048]{1,0:T(8,128)(2,1)S(1)} %get-tuple-element.131), kind=kOutput, calls=%fused_computation.28 | convolution fusion | flops 1074790400 | bytes 9961472 | tf_op jit(solution)/shard_map/while/body/eval_jaxpr/while/body/eval_jaxpr/dot_general | solution.py:55
  60.5 2.7 %convolution_add_fusion = f32[64,2048]{1,0:T(8,128)S(1)} fusion(bf16[64,2048]{1,0:T(8,128)(2,1)S(1)} %get-tuple-element.131, bf16[2048,2048]{1,0:T(8,128)(2,1)S(1)} %copy-done.2, f32[128,2048]{1,0:T(8,128)S(1)} %fusion.9), kind=kOutput, calls=%fused_computation.4 | convolution fusion | flops 537133056 | bytes 10223616 | tf_op jit(solution)/shard_map/while/body/eval_jaxpr/while/body/eval_jaxpr/dot_general | solution.py:59
  63.5 1.5 %cholesky.81 = f32[16,16]{1,0:T(8,128)S(1)} custom-call(f32[16,16]{1,0:T(8,128)S(1)} %fusion.41), custom_call_target="Cholesky" | custom-call | tf_op jit(solution)/shard_map/jit(cholesky)/cholesky | solution.py:29
  65.1 0.6 compare_reduce_fusion
  65.7 0.6 fusion.36
  66.4 1.2 %custom-call.11 = f32[1,16,16]{1,2,0:T(8,128)S(1)} custom-call(f32[1,16,16]{2,1,0:T(8,128)S(1)} %fusion.36), custom_call_target="InvertDiagBlocksLowerTriangular" | custom-call | tf_op jit(solution)/shard_map/jit(_cho_solve)/triangular_solve | solution.py:29
  68.9 0.6 dynamic-slice_subtract_fusion
  (45 shorter events, 4.5 us)
Async XLA Ops:
  0.6 2.0 %copy-start = (bf16[512,512]{1,0:T(8,128)(2,1)S(1)}, bf16[512,512]{1,0:T(8,128)(2,1)}, u32[]{:S(2)}) copy-start(bf16[512,512]{1,0:T(8,128)(2,1)} %param.18) | copy-start | bytes 1572868
  36.8 5.6 %copy-start.1 = (bf16[2048,2048]{1,0:T(8,128)(2,1)}, bf16[2048,2048]{1,0:T(8,128)(2,1)S(1)}, u32[]{:S(2)}) copy-start(bf16[2048,2048]{1,0:T(8,128)(2,1)S(1)} %get-tuple-element.107) | copy-start | bytes 25165828
  36.8 5.7 %copy-start.3 = (bf16[2048,2048]{1,0:T(8,128)(2,1)}, bf16[2048,2048]{1,0:T(8,128)(2,1)S(1)}, u32[]{:S(2)}) copy-start(bf16[2048,2048]{1,0:T(8,128)(2,1)S(1)} %get-tuple-element.106) | copy-start | bytes 25165828
  36.8 6.3 %copy-start.4 = (f32[4,4]{1,0:T(4,128)S(1)}, f32[4,4]{1,0:T(4,128)}, u32[]{:S(2)}) copy-start(f32[4,4]{1,0:T(4,128)} %param.22) | copy-start | bytes 196
  53.1 7.4 %copy-start.2 = (bf16[2048,2048]{1,0:T(8,128)(2,1)S(1)}, bf16[2048,2048]{1,0:T(8,128)(2,1)}, u32[]{:S(2)}) copy-start(bf16[2048,2048]{1,0:T(8,128)(2,1)} %copy-done.1) | copy-start | bytes 25165828

commit v14 on v13

--- a/solution.py
+++ b/solution.py
@@ -48,9 +48,13 @@
 
 
 def split_product(direction, kernel):
+    return pieces_product(direction, split_two(kernel))
+
+
+def pieces_product(direction, pieces):
     count = direction.shape[0]
     d_high, d_low = split_two(direction)
-    k_high, k_low = split_two(kernel)
+    k_high, k_low = pieces
     dims = (((1,), (1,)), ((), ()))
     by_high = lax.dot_general(
         jnp.concatenate([d_high, d_low], axis=0), k_high, dims,
@@ -60,7 +64,19 @@
     return (by_high[:count] + by_high[count:]) + by_low
 
 
-def kernel_image(embedding, squares, rung_onehot, col_fidelity, inverse_scale, direction):
+def whole_radial_pieces(embedding, squares, inverse_scale):
+    count = embedding.shape[1]
+    if block_size(count, 2048) != count:
+        return None
+    inner = left_product(embedding, embedding)
+    distance = squares[:, None] + squares[None, :] - 2.0 * inner
+    radial = jnp.exp(-inverse_scale[0] * distance)
+    return lax.optimization_barrier(split_two(radial))
+
+
+def kernel_image(
+    embedding, squares, rung_onehot, col_fidelity, inverse_scale, direction, pieces=None
+):
     count = embedding.shape[1]
     row_block = block_size(count, 2048)
     col_block = block_size(count, 2048)
@@ -79,9 +95,12 @@
             cols_fidelity = lax.dynamic_slice_in_dim(col_fidelity, first_col, col_block, 1)
             cols_direction = lax.dynamic_slice_in_dim(direction, first_col, col_block, 1)
             cols_onehot = lax.dynamic_slice_in_dim(rung_onehot, first_col, col_block, 1)
-            inner = left_product(rows_embedding, cols_embedding)
-            distance = rows_squares[:, None] + cols_squares[None, :] - 2.0 * inner
-            radial = jnp.exp(-inverse_scale[0] * distance)
+            if pieces is None:
+                inner = left_product(rows_embedding, cols_embedding)
+                distance = rows_squares[:, None] + cols_squares[None, :] - 2.0 * inner
+                radial_pieces = split_two(jnp.exp(-inverse_scale[0] * distance))
+            else:
+                radial_pieces = pieces
             by_rung = jnp.concatenate(
                 [
                     cols_direction * cols_onehot[level][None, :]
@@ -89,7 +108,7 @@
                 ],
                 axis=0,
             )
-            rung_products = split_product(by_rung, radial)
+            rung_products = pieces_product(by_rung, radial_pieces)
             rhs = direction.shape[0]
             contribution = rows_fidelity[0][None, :] * rung_products[:rhs]
             for level in range(1, col_fidelity.shape[0]):
@@ -147,13 +166,17 @@
     squares = jnp.sum(jnp.square(gathered[:emb_rows]), axis=0)
     col_fidelity, rung_onehot = rung_fidelity(fidelity, all_rung)
 
+    pieces = whole_radial_pieces(all_embedding, squares, inverse_scale)
     solution = jnp.zeros_like(all_targets)
     residual = all_targets
     direction = all_targets
     gram = outer_gram(residual, residual)
     for iteration in range(ITERS):
         image = (
-            kernel_image(all_embedding, squares, rung_onehot, col_fidelity, inverse_scale, direction)
+            kernel_image(
+                all_embedding, squares, rung_onehot, col_fidelity, inverse_scale, direction,
+                pieces,
+            )
             + noise_var[0] * direction
         )
         curvature = outer_gram(direction, image)

time: 69.9 us -> 69.9 us (level)
  no operation moved by 1% of the time
where the time goes in v14:
time: 69.9 us; the launch traced here: 69.6 us
  matrix products  27 us (39%)
  blocking collectives  25.3 us (36%)
  other arithmetic  14.6 us (21%)
  between operations  2.2 us (3%)
    all_gather x1, blocking collectives, on_device(): gathered = lax.all_gather(packed, ('row', 'col'), axis=1, tiled=True)  25.3 us
    dot_general x2, matrix products, pieces_product(): lax.dot_general(jnp.concatenate([d_high, d_low], axis=0), k_high, dims, p...  9.5 us
    dot_general x3, matrix products, left_product(): lax.dot_general(weights, values, (((0,), (0,)), ((), ())), preferred_elem...  8.27 us
    another operation x9, other arithmetic, solve_spd(): jnp.linalg.cholesky(matrix)  6.57 us
    another operation x6, other arithmetic, solve_spd(): jax.scipy.linalg.cho_solve((jnp.linalg.cholesky(matrix), True), right_side)  5.63 us
    dot_general x2, matrix products, pieces_product(): lax.dot_general(d_high, k_low, dims, preferred_element_type=jnp.float32)  5.32 us

profile of v14, /device:TPU:0, one launch (start us, length us, event | category | flops | bytes accessed | tf_op | source)
XLA Modules:
  0.0 69.6 jit_solution(1832466048637910518)
XLA Ops:
  0.6 0.7 %convert_bitcast_fusion = f32[1,128]{1,0:T(1,128)S(1)} fusion(s32[128]{0:T(128)} %param.15), kind=kLoop, calls=%fused_computation.113 | loop fusion | flops 128 | bytes 1024 | tf_op jit(solution)/shard_map/broadcast_in_dim | solution.py:159
  1.4 1.2 %multiply_convert_fusion.1 = bf16[512,128]{1,0:T(8,128)(2,1)S(1)} fusion(bf16[164,512]{1,0:T(8,128)(2,1)} %param.16, bf16[164,128]{1,0:T(8,128)(2,1)} %param.14, f32[512]{0:T(512)} %param.17), kind=kOutput, calls=%fused_computation.36 | convolution fusion | flops 21889024 | bytes 343040 | tf_op jit(solution)/shard_map/dot_general | solution.py:17
  2.6 1.4 %fusion.2 = f32[64,128]{1,0:T(8,128)S(1)} fusion(bf16[512,64]{0,1:T(8,128)(2,1)} %param.20, bf16[512,128]{1,0:T(8,128)(2,1)S(1)} %multiply_convert_fusion.1, bf16[512,512]{1,0:T(8,128)(2,1)S(1)} %copy-done, f32[512]{0:T(512)} %param.19), kind=kOutput, calls=%fused_computation.12 | convolution fusion | flops 75898880 | bytes 755712 | tf_op jit(solution)/shard_map/dot_general | solution.py:17
  4.0 0.7 %pad_maximum_fusion.2 = f32[81,128]{1,0:T(8,128)S(1)} fusion(f32[1,128]{1,0:T(1,128)S(1)} %convert_bitcast_fusion, f32[16,128]{1,0:T(8,128)} %param.21, f32[64,128]{1,0:T(8,128)S(1)} %fusion.2), kind=kLoop, calls=%fused_computation.70 | loop fusion | flops 20736 | bytes 82944 | tf_op jit(solution)/shard_map/concatenate | solution.py:158
  4.7 25.3 %all_gather.3 = f32[81,2048]{1,0:T(8,128)S(1)} all-gather(f32[81,128]{1,0:T(8,128)S(1)} %pad_maximum_fusion.2), channel_id=1, replica_groups=mesh['task'=2,'row'=4,'col'=4] {'row','col'}, dimensions={1}, use_global_device_ids=true | all-gather | bytes 705024 | tf_op jit(solution)/shard_map/all_gather | solution.py:161
  31.1 5.7 %fusion = (bf16[2048,2048]{1,0:T(8,128)(2,1)S(1)}, bf16[2048,2048]{1,0:T(8,128)(2,1)S(1)}) fusion(f32[2048]{0:T(1024)S(1)} %multiply_reduce_fusion, f32[]{:T(128)} %bitcast.9, f32[81,2048]{1,0:T(8,128)S(1)} %all_gather.3), kind=kOutput, calls=%fused_computation.2 | convolution fusion | flops 570425344 | bytes 17055748 | tf_op jit(solution)/shard_map/dot_general | solution.py:17
  36.8 2.9 %fusion.5 = f32[128,2048]{1,0:T(8,128)S(1)} fusion(bf16[2048,2048]{1,0:T(8,128)(2,1)S(1)} %get-tuple-element.83, bf16[64,2048]{1,0:T(8,128)(2,1)S(1)} %get-tuple-element.114, bf16[64,2048]{1,0:T(8,128)(2,1)S(1)} %get-tuple-element.115), kind=kOutput, calls=%fused_computation.23 | convolution fusion | flops 1074790400 | bytes 9961472 | tf_op jit(solution)/shard_map/while/body/eval_jaxpr/while/body/eval_jaxpr/dot_general | solution.py:59
  39.7 2.7 %convolution_add_fusion.1 = f32[64,2048]{1,0:T(8,128)S(1)} fusion(bf16[64,2048]{1,0:T(8,128)(2,1)S(1)} %get-tuple-element.115, bf16[2048,2048]{1,0:T(8,128)(2,1)S(1)} %get-tuple-element.98, f32[128,2048]{1,0:T(8,128)S(1)} %fusion.5), kind=kOutput, calls=%fused_computation.5 | convolution fusion | flops 537133056 | bytes 10223616 | tf_op jit(solution)/shard_map/while/body/eval_jaxpr/while/body/eval_jaxpr/dot_general | solution.py:63
  43.9 1.5 %cholesky.59 = f32[16,16]{1,0:T(8,128)S(1)} custom-call(f32[16,16]{1,0:T(8,128)S(1)} %fusion.51), custom_call_target="Cholesky" | custom-call | tf_op jit(solution)/shard_map/jit(cholesky)/cholesky | solution.py:29
  45.5 0.6 compare_reduce_fusion.2
  46.1 0.6 fusion.34
  46.8 1.2 %custom-call.9 = f32[1,16,16]{1,2,0:T(8,128)S(1)} custom-call(f32[1,16,16]{2,1,0:T(8,128)S(1)} %fusion.34), custom_call_target="InvertDiagBlocksLowerTriangular" | custom-call | tf_op jit(solution)/shard_map/jit(_cho_solve)/triangular_solve | solution.py:29
  49.0 1.5 %cholesky.70 = f32[16,16]{1,0:T(8,128)S(1)} custom-call(f32[16,16]{1,0:T(8,128)S(1)} %fusion.46), custom_call_target="Cholesky" | custom-call | tf_op jit(solution)/shard_map/jit(cholesky)/cholesky | solution.py:29
  50.5 0.6 compare_reduce_fusion.1
  51.2 0.6 fusion.35
  51.8 1.2 %custom-call.10 = f32[1,16,16]{1,2,0:T(8,128)S(1)} custom-call(f32[1,16,16]{2,1,0:T(8,128)S(1)} %fusion.35), custom_call_target="InvertDiagBlocksLowerTriangular" | custom-call | tf_op jit(solution)/shard_map/jit(_cho_solve)/triangular_solve | solution.py:29
  53.4 0.4 broadcast_multiply_fusion.6
  53.9 6.6 %fusion.9 = f32[128,2048]{1,0:T(8,128)S(1)} fusion(bf16[2048,2048]{1,0:T(8,128)(2,1)} %copy-done.3, bf16[64,2048]{1,0:T(8,128)(2,1)S(1)} %get-tuple-element.112, bf16[64,2048]{1,0:T(8,128)(2,1)S(1)} %get-tuple-element.113), kind=kOutput, calls=%fused_computation.28 | convolution fusion | flops 1074790400 | bytes 9961472 | tf_op jit(solution)/shard_map/while/body/eval_jaxpr/while/body/eval_jaxpr/dot_general | solution.py:59
  60.5 2.7 %convolution_add_fusion = f32[64,2048]{1,0:T(8,128)S(1)} fusion(bf16[64,2048]{1,0:T(8,128)(2,1)S(1)} %get-tuple-element.113, bf16[2048,2048]{1,0:T(8,128)(2,1)S(1)} %copy-done.2, f32[128,2048]{1,0:T(8,128)S(1)} %fusion.9), kind=kOutput, calls=%fused_computation.4 | convolution fusion | flops 537133056 | bytes 10223616 | tf_op jit(solution)/shard_map/while/body/eval_jaxpr/while/body/eval_jaxpr/dot_general | solution.py:63
  63.5 1.5 %cholesky.81 = f32[16,16]{1,0:T(8,128)S(1)} custom-call(f32[16,16]{1,0:T(8,128)S(1)} %fusion.41), custom_call_target="Cholesky" | custom-call | tf_op jit(solution)/shard_map/jit(cholesky)/cholesky | solution.py:29
  65.1 0.6 compare_reduce_fusion
  65.7 0.6 fusion.36
  66.4 1.2 %custom-call.11 = f32[1,16,16]{1,2,0:T(8,128)S(1)} custom-call(f32[1,16,16]{2,1,0:T(8,128)S(1)} %fusion.36), custom_call_target="InvertDiagBlocksLowerTriangular" | custom-call | tf_op jit(solution)/shard_map/jit(_cho_solve)/triangular_solve | solution.py:29
  68.9 0.6 dynamic-slice_subtract_fusion
  (45 shorter events, 4.5 us)
Async XLA Ops:
  0.6 2.0 %copy-start = (bf16[512,512]{1,0:T(8,128)(2,1)S(1)}, bf16[512,512]{1,0:T(8,128)(2,1)}, u32[]{:S(2)}) copy-start(bf16[512,512]{1,0:T(8,128)(2,1)} %param.18) | copy-start | bytes 1572868
  36.8 5.6 %copy-start.1 = (bf16[2048,2048]{1,0:T(8,128)(2,1)}, bf16[2048,2048]{1,0:T(8,128)(2,1)S(1)}, u32[]{:S(2)}) copy-start(bf16[2048,2048]{1,0:T(8,128)(2,1)S(1)} %get-tuple-element.98) | copy-start | bytes 25165828
  36.8 5.7 %copy-start.3 = (bf16[2048,2048]{1,0:T(8,128)(2,1)}, bf16[2048,2048]{1,0:T(8,128)(2,1)S(1)}, u32[]{:S(2)}) copy-start(bf16[2048,2048]{1,0:T(8,128)(2,1)S(1)} %get-tuple-element.83) | copy-start | bytes 25165828
  36.8 6.3 %copy-start.4 = (f32[4,4]{1,0:T(4,128)S(1)}, f32[4,4]{1,0:T(4,128)}, u32[]{:S(2)}) copy-start(f32[4,4]{1,0:T(4,128)} %param.22) | copy-start | bytes 196
  53.1 7.4 %copy-start.2 = (bf16[2048,2048]{1,0:T(8,128)(2,1)S(1)}, bf16[2048,2048]{1,0:T(8,128)(2,1)}, u32[]{:S(2)}) copy-start(bf16[2048,2048]{1,0:T(8,128)(2,1)} %copy-done.1) | copy-start | bytes 25165828

commit v15 on v14

--- a/solution.py
+++ b/solution.py
@@ -181,6 +181,11 @@
         )
         curvature = outer_gram(direction, image)
         step_matrix = solve_spd(curvature, gram)
+        if iteration + 1 == ITERS:
+            own = lambda values: lax.dynamic_slice_in_dim(values, own_first, own_count, 1)
+            solution, residual, direction, image = (
+                own(solution), own(residual), own(direction), own(image)
+            )
         solution = solution + jnp.dot(step_matrix.T, direction, precision=lax.Precision.HIGHEST)
         residual = residual - jnp.dot(step_matrix.T, image, precision=lax.Precision.HIGHEST)
         if iteration + 1 < ITERS:
@@ -190,9 +195,7 @@
                 update_matrix.T, direction, precision=lax.Precision.HIGHEST
             )
             gram = new_gram
-    own_solution = lax.dynamic_slice_in_dim(solution, own_first, own_count, 1)
-    own_residual = lax.dynamic_slice_in_dim(residual, own_first, own_count, 1)
-    return (own_solution, own_residual)
+    return (solution, residual)
 
 
 def solution(mesh):

time: 69.9 us -> 70.2 us (level)
  matrix products: 27 us -> 27.9 us
where the time goes in v15:
time: 70.2 us; the launch traced here: 69.9 us
  matrix products  27.9 us (40%)
  blocking collectives  25.3 us (36%)
  other arithmetic  14 us (20%)
  between operations  2.17 us (3%)
    all_gather x1, blocking collectives, on_device(): gathered = lax.all_gather(packed, ('row', 'col'), axis=1, tiled=True)  25.3 us
    dot_general x2, matrix products, pieces_product(): lax.dot_general(jnp.concatenate([d_high, d_low], axis=0), k_high, dims, p...  9.5 us
    dot_general x3, matrix products, left_product(): lax.dot_general(weights, values, (((0,), (0,)), ((), ())), preferred_elem...  8.27 us
    another operation x9, other arithmetic, solve_spd(): jnp.linalg.cholesky(matrix)  6.57 us
    another operation x6, other arithmetic, solve_spd(): jax.scipy.linalg.cho_solve((jnp.linalg.cholesky(matrix), True), right_side)  5.63 us
    dot_general x2, matrix products, pieces_product(): lax.dot_general(d_high, k_low, dims, preferred_element_type=jnp.float32)  5.32 us

profile of v15, /device:TPU:0, one launch (start us, length us, event | category | flops | bytes accessed | tf_op | source)
XLA Modules:
  0.0 69.9 jit_solution(8296823960190719565)
XLA Ops:
  0.6 0.7 %convert_bitcast_fusion = f32[1,128]{1,0:T(1,128)S(1)} fusion(s32[128]{0:T(128)} %param.15), kind=kLoop, calls=%fused_computation.117 | loop fusion | flops 128 | bytes 1024 | tf_op jit(solution)/shard_map/broadcast_in_dim | solution.py:159
  1.4 1.2 %multiply_convert_fusion.1 = bf16[512,128]{1,0:T(8,128)(2,1)S(1)} fusion(bf16[164,512]{1,0:T(8,128)(2,1)} %param.16, bf16[164,128]{1,0:T(8,128)(2,1)} %param.14, f32[512]{0:T(512)} %param.17), kind=kOutput, calls=%fused_computation.38 | convolution fusion | flops 21889024 | bytes 343040 | tf_op jit(solution)/shard_map/dot_general | solution.py:17
  2.6 1.4 %fusion.2 = f32[64,128]{1,0:T(8,128)S(1)} fusion(bf16[512,64]{0,1:T(8,128)(2,1)} %param.20, bf16[512,128]{1,0:T(8,128)(2,1)S(1)} %multiply_convert_fusion.1, bf16[512,512]{1,0:T(8,128)(2,1)S(1)} %copy-done, f32[512]{0:T(512)} %param.19), kind=kOutput, calls=%fused_computation.12 | convolution fusion | flops 75898880 | bytes 755712 | tf_op jit(solution)/shard_map/dot_general | solution.py:17
  4.0 0.7 %pad_maximum_fusion.2 = f32[81,128]{1,0:T(8,128)S(1)} fusion(f32[1,128]{1,0:T(1,128)S(1)} %convert_bitcast_fusion, f32[16,128]{1,0:T(8,128)} %param.21, f32[64,128]{1,0:T(8,128)S(1)} %fusion.2), kind=kLoop, calls=%fused_computation.72 | loop fusion | flops 20736 | bytes 82944 | tf_op jit(solution)/shard_map/concatenate | solution.py:158
  4.7 25.3 %all_gather.3 = f32[81,2048]{1,0:T(8,128)S(1)} all-gather(f32[81,128]{1,0:T(8,128)S(1)} %pad_maximum_fusion.2), channel_id=1, replica_groups=mesh['task'=2,'row'=4,'col'=4] {'row','col'}, dimensions={1}, use_global_device_ids=true | all-gather | bytes 705024 | tf_op jit(solution)/shard_map/all_gather | solution.py:161
  31.1 5.7 %fusion = (bf16[2048,2048]{1,0:T(8,128)(2,1)S(1)}, bf16[2048,2048]{1,0:T(8,128)(2,1)S(1)}) fusion(f32[2048]{0:T(1024)S(1)} %multiply_reduce_fusion, f32[]{:T(128)} %bitcast.9, f32[81,2048]{1,0:T(8,128)S(1)} %all_gather.3), kind=kOutput, calls=%fused_computation.2 | convolution fusion | flops 570425344 | bytes 17055748 | tf_op jit(solution)/shard_map/dot_general | solution.py:17
  36.8 2.9 %fusion.5 = f32[128,2048]{1,0:T(8,128)S(1)} fusion(bf16[2048,2048]{1,0:T(8,128)(2,1)S(1)} %get-tuple-element.83, bf16[64,2048]{1,0:T(8,128)(2,1)S(1)} %get-tuple-element.114, bf16[64,2048]{1,0:T(8,128)(2,1)S(1)} %get-tuple-element.115), kind=kOutput, calls=%fused_computation.25 | convolution fusion | flops 1074790400 | bytes 9961472 | tf_op jit(solution)/shard_map/while/body/eval_jaxpr/while/body/eval_jaxpr/dot_general | solution.py:59
  39.7 2.7 %convolution_add_fusion.1 = f32[64,2048]{1,0:T(8,128)S(1)} fusion(bf16[64,2048]{1,0:T(8,128)(2,1)S(1)} %get-tuple-element.115, bf16[2048,2048]{1,0:T(8,128)(2,1)S(1)} %get-tuple-element.98, f32[128,2048]{1,0:T(8,128)S(1)} %fusion.5), kind=kOutput, calls=%fused_computation.5 | convolution fusion | flops 537133056 | bytes 10223616 | tf_op jit(solution)/shard_map/while/body/eval_jaxpr/while/body/eval_jaxpr/dot_general | solution.py:63
  43.9 1.5 %cholesky.59 = f32[16,16]{1,0:T(8,128)S(1)} custom-call(f32[16,16]{1,0:T(8,128)S(1)} %fusion.51), custom_call_target="Cholesky" | custom-call | tf_op jit(solution)/shard_map/jit(cholesky)/cholesky | solution.py:29
  45.5 0.6 compare_reduce_fusion.2
  46.1 0.6 fusion.34
  46.8 1.2 %custom-call.9 = f32[1,16,16]{1,2,0:T(8,128)S(1)} custom-call(f32[1,16,16]{2,1,0:T(8,128)S(1)} %fusion.34), custom_call_target="InvertDiagBlocksLowerTriangular" | custom-call | tf_op jit(solution)/shard_map/jit(_cho_solve)/triangular_solve | solution.py:29
  49.0 1.5 %cholesky.70 = f32[16,16]{1,0:T(8,128)S(1)} custom-call(f32[16,16]{1,0:T(8,128)S(1)} %fusion.46), custom_call_target="Cholesky" | custom-call | tf_op jit(solution)/shard_map/jit(cholesky)/cholesky | solution.py:29
  50.5 0.6 compare_reduce_fusion.1
  51.2 0.6 fusion.35
  51.8 1.2 %custom-call.10 = f32[1,16,16]{1,2,0:T(8,128)S(1)} custom-call(f32[1,16,16]{2,1,0:T(8,128)S(1)} %fusion.35), custom_call_target="InvertDiagBlocksLowerTriangular" | custom-call | tf_op jit(solution)/shard_map/jit(_cho_solve)/triangular_solve | solution.py:29
  53.9 6.6 %fusion.9 = f32[128,2048]{1,0:T(8,128)S(1)} fusion(bf16[2048,2048]{1,0:T(8,128)(2,1)} %copy-done.3, bf16[64,2048]{1,0:T(8,128)(2,1)S(1)} %get-tuple-element.112, bf16[64,2048]{1,0:T(8,128)(2,1)S(1)} %get-tuple-element.113), kind=kOutput, calls=%fused_computation.30 | convolution fusion | flops 1074790400 | bytes 9961472 | tf_op jit(solution)/shard_map/while/body/eval_jaxpr/while/body/eval_jaxpr/dot_general | solution.py:59
  60.5 2.7 %convolution_add_fusion = f32[64,2048]{1,0:T(8,128)S(1)} fusion(bf16[64,2048]{1,0:T(8,128)(2,1)S(1)} %get-tuple-element.113, bf16[2048,2048]{1,0:T(8,128)(2,1)S(1)} %copy-done.2, f32[128,2048]{1,0:T(8,128)S(1)} %fusion.9), kind=kOutput, calls=%fused_computation.4 | convolution fusion | flops 537133056 | bytes 10223616 | tf_op jit(solution)/shard_map/while/body/eval_jaxpr/while/body/eval_jaxpr/dot_general | solution.py:63
  63.5 1.5 %cholesky.81 = f32[16,16]{1,0:T(8,128)S(1)} custom-call(f32[16,16]{1,0:T(8,128)S(1)} %fusion.41), custom_call_target="Cholesky" | custom-call | tf_op jit(solution)/shard_map/jit(cholesky)/cholesky | solution.py:29
  65.1 0.6 compare_reduce_fusion
  65.7 0.6 fusion.36
  66.4 1.2 %custom-call.11 = f32[1,16,16]{1,2,0:T(8,128)S(1)} custom-call(f32[1,16,16]{2,1,0:T(8,128)S(1)} %fusion.36), custom_call_target="InvertDiagBlocksLowerTriangular" | custom-call | tf_op jit(solution)/shard_map/jit(_cho_solve)/triangular_solve | solution.py:29
  68.3 0.8 %convolution_add_fusion.5 = f32[16,128]{1,0:T(8,128)} fusion(f32[16,16]{1,0:T(8,128)S(1)} %fusion.37, f32[16,2048]{1,0:T(8,128)S(1)} %get-tuple-element.128, s32[]{:T(128)S(6)} %select_n.26, f32[16,2048]{1,0:T(8,128)S(1)} %fusion.25), kind=kOutput, calls=%fused_computation.14 | convolution fusion | flops 395264 | bytes 33792 | tf_op jit(solution)/shard_map/dot_general | solution.py:189
  69.1 0.8 %convolution_subtract_fusion.1 = f32[16,128]{1,0:T(8,128)} fusion(f32[16,16]{1,0:T(8,128)S(1)} %fusion.37, f32[16,2048]{1,0:T(8,128)S(1)} %fusion.15, s32[]{:T(128)S(6)} %select_n.26, f32[16,2048]{1,0:T(8,128)S(1)} %convolution_subtract_fusion), kind=kOutput, calls=%fused_computation.13 | convolution fusion | flops 395264 | bytes 33792 | tf_op jit(solution)/shard_map/dot_general | solution.py:190
  (44 shorter events, 4.2 us)
Async XLA Ops:
  0.6 2.0 %copy-start = (bf16[512,512]{1,0:T(8,128)(2,1)S(1)}, bf16[512,512]{1,0:T(8,128)(2,1)}, u32[]{:S(2)}) copy-start(bf16[512,512]{1,0:T(8,128)(2,1)} %param.18) | copy-start | bytes 1572868
  36.8 5.6 %copy-start.1 = (bf16[2048,2048]{1,0:T(8,128)(2,1)}, bf16[2048,2048]{1,0:T(8,128)(2,1)S(1)}, u32[]{:S(2)}) copy-start(bf16[2048,2048]{1,0:T(8,128)(2,1)S(1)} %get-tuple-element.98) | copy-start | bytes 25165828
  36.8 5.7 %copy-start.3 = (bf16[2048,2048]{1,0:T(8,128)(2,1)}, bf16[2048,2048]{1,0:T(8,128)(2,1)S(1)}, u32[]{:S(2)}) copy-start(bf16[2048,2048]{1,0:T(8,128)(2,1)S(1)} %get-tuple-element.83) | copy-start | bytes 25165828
  36.8 6.3 %copy-start.4 = (f32[4,4]{1,0:T(4,128)S(1)}, f32[4,4]{1,0:T(4,128)}, u32[]{:S(2)}) copy-start(f32[4,4]{1,0:T(4,128)} %param.22) | copy-start | bytes 196
  53.1 7.4 %copy-start.2 = (bf16[2048,2048]{1,0:T(8,128)(2,1)S(1)}, bf16[2048,2048]{1,0:T(8,128)(2,1)}, u32[]{:S(2)}) copy-start(bf16[2048,2048]{1,0:T(8,128)(2,1)} %copy-done.1) | copy-start | bytes 25165828
